TPU v7x, 768 devices: a whole 4x8x12 slice. The times are simulated.
768 devices in a mesh: atom: 96 (over y, z), energy: 8 (over x, core).
Axes of the slice: x: 4, y: 8, z: 12, core: 2. Of those that a mesh axis runs over, the one named last changes fastest.
Arguments:
- green: bfloat16 [192, 2, 12, 12, 1024], P('atom', None, None, None, 'energy'), may hold values from -6 to 6
- coupling: bfloat16 [192, 34, 2, 12, 12], P('atom'), may hold values from -0.5 to 0.5
- neighbours: int32 [192, 34], P('atom'), may hold values from 0 to 191, as said below
- offsets: int32 [70], replicated, may hold values from 1 to 48, as said below
- w_emit: float32 [70], replicated, may hold values from 0.02 to 0.2
- w_absorb: float32 [70], replicated, may hold values from 0.02 to 0.2
Outputs:
- self_energy: float32 [192, 2, 12, 12, 1024], P('atom', None, None, None, 'energy')
Inputs may be any that keep to these rules, and one draw needn't show every extreme that they name: neighbours[a, k] lies among the atoms a // 2 - 1, a // 2, a // 2 + 1 times 2 plus 0 to 1, that is, among the atoms of the same index of atom or of an index one away. `offsets`: some frequency equals 48.
All inputs are finite; a program needn't handle non-finite values.
Results may differ from a plain program's by a relative error of at most 0.0028.
Values may be sent and summed in bfloat16 or wider, within the bound.
No kernel may reach another device: no remote copies, remote signals or barrier semaphores. Data moves between devices by JAX's collectives and lax.ppermute only.
A program may use at most 32 MiB of HBM per device.

v0:
```python
import jax
import jax.numpy as jnp
from jax import lax
from jax.sharding import PartitionSpec as P


def extended(cells, sides, width):
    for axis, dim in sides:
        count = lax.axis_size(axis)
        ends = count - 1
        head = lax.slice_in_dim(cells, 0, width, axis=dim)
        tail = lax.slice_in_dim(cells, cells.shape[dim] - width, cells.shape[dim], axis=dim)
        cells = jnp.concatenate(
            [
                lax.ppermute(tail, axis, [(i, (i + 1) % count) for i in range(ends)]),
                cells,
                lax.ppermute(head, axis, [((i + 1) % count, i) for i in range(ends)]),
            ],
            axis=dim,
        )
    return cells


def couple(blocks, gathered):
    f32 = jnp.float32
    x_re = jnp.einsum(
        "kij,kjle->kile", blocks[:, 0], gathered[:, 0], preferred_element_type=f32
    ) - jnp.einsum("kij,kjle->kile", blocks[:, 1], gathered[:, 1], preferred_element_type=f32)
    x_im = jnp.einsum(
        "kij,kjle->kile", blocks[:, 0], gathered[:, 1], preferred_element_type=f32
    ) + jnp.einsum("kij,kjle->kile", blocks[:, 1], gathered[:, 0], preferred_element_type=f32)
    x_re = x_re.astype(jnp.bfloat16)
    x_im = x_im.astype(jnp.bfloat16)
    p_re = jnp.einsum("kile,kml->ime", x_re, blocks[:, 0], preferred_element_type=f32) + jnp.einsum(
        "kile,kml->ime", x_im, blocks[:, 1], preferred_element_type=f32
    )
    p_im = jnp.einsum("kile,kml->ime", x_im, blocks[:, 0], preferred_element_type=f32) - jnp.einsum(
        "kile,kml->ime", x_re, blocks[:, 1], preferred_element_type=f32
    )
    return jnp.stack([p_re, p_im])


def make_kernel(spread_diff, offsets, w_emit, w_absorb):
    kernel = jnp.sum(
        jnp.where(spread_diff[:, :, None] == offsets, w_emit, jnp.float32(0.0)), axis=2
    )
    return kernel + jnp.sum(
        jnp.where(spread_diff[:, :, None] == -offsets, w_absorb, jnp.float32(0.0)), axis=2
    )


def shards(green, coupling, neighbours, offsets, w_emit, w_absorb):
    hi = lax.Precision.HIGHEST
    atoms_here = green.shape[0]
    points = green.shape[-1]
    reach = points * 3 // 8
    window = extended(green, (("atom", 0),), atoms_here)
    local_ids = neighbours - (lax.axis_index("atom") - 1) * atoms_here

    def one_atom(packed):
        blocks, listed = packed
        gathered = jnp.take(window, listed, axis=0)
        return couple(blocks, gathered)

    coupled = lax.map(one_atom, (coupling, local_ids))
    extent = points + 2 * reach
    spread_diff = (
        jnp.arange(extent, dtype=jnp.int32)[:, None]
        - reach
        - jnp.arange(points, dtype=jnp.int32)[None, :]
    )
    kernel = make_kernel(spread_diff, offsets, w_emit, w_absorb)
    widened = extended(coupled, (("energy", 4),), reach)
    result = jnp.dot(
        widened.reshape(-1, extent), kernel, precision=hi, preferred_element_type=jnp.float32
    )
    return result.reshape(coupled.shape)


def solution(mesh):
    return jax.shard_map(
        shards,
        mesh=mesh,
        in_specs=(
            P("atom", None, None, None, "energy"),
            P("atom", None, None, None, None),
            P("atom", None),
            P(),
            P(),
            P(),
        ),
        out_specs=P("atom", None, None, None, "energy"),
        check_vma=False,
    )
```

profile of v0, /device:TPU:57, one launch (start us, length us, event | category | flops | bytes accessed | tf_op | source)
XLA Modules:
  0.0 91.1 jit_solution(13283278839127116197)
XLA Ops:
  0.0 4.0 %collective-permute-start = (bf16[2,2,12,12,128]{4,1,3,2,0:T(2,128)(2,1)}, bf16[2,2,12,12,128]{4,1,3,2,0:T(2,128)(2,1)S(1)}, u32[]{:S(2)}, u32[]{:S(2)}) collective-permute-start(bf16[2,2,12,12,128]{4,1,3,2,0:T(2,128)(2,1)} %param.8), channel_id=1, source_target_pairs={{0,8},{8,16},{16,24},{24,32},{32,40},{40,48},{48,56},{56,64},{64,7... | collective-permute-start | bytes 442376 | tf_op jit(solution)/shard_map/ppermute | solution.py:15
  4.0 13.0 %collective-permute-start.1 = (bf16[2,2,12,12,128]{4,1,3,2,0:T(2,128)(2,1)}, bf16[2,2,12,12,128]{4,1,3,2,0:T(2,128)(2,1)S(1)}, u32[]{:S(2)}, u32[]{:S(2)}) collective-permute-start(bf16[2,2,12,12,128]{4,1,3,2,0:T(2,128)(2,1)} %param.8), channel_id=1, source_target_pairs={{8,0},{16,8},{24,16},{32,24},{40,32},{48,40},{56,48},{64,56},{72,6... | collective-permute-start | bytes 442376 | tf_op jit(solution)/shard_map/ppermute | solution.py:17
  19.8 1.5 %pad_maximum_fusion = bf16[6,2,12,12,128]{4,1,3,2,0:T(2,128)(2,1)S(1)} fusion(bf16[2,2,12,12,128]{4,1,3,2,0:T(2,128)(2,1)S(1)} %collective-permute-done.1, bf16[2,2,12,12,128]{4,1,3,2,0:T(2,128)(2,1)} %param.8, bf16[2,2,12,12,128]{4,1,3,2,0:T(2,128)(2,1)S(1)} %collective-permute-done), kind=kLoop, calls=%fused_computation.55 | loop fusion | flops 442368 | bytes 884736 | tf_op jit(solution)/shard_map/concatenate | solution.py:13
  21.4 51.8 %while.10 = (s32[]{:T(128)}, f32[2,2,12,12,128]{4,3,2,1,0:T(8,128)}, bf16[2,34,2,12,12]{1,2,4,3,0:T(2,128)(2,1)}, s32[2,34]{1,0:T(2,128)S(1)}, bf16[6,2,12,12,128]{4,1,3,2,0:T(2,128)(2,1)S(1)}, /*index=5*/s32[]{:T(128)}) while((s32[]{:T(128)}, f32[2,2,12,12,128]{4,3,2,1,0:T(8,128)}, bf16[2,34,2,12,12]{1,2,4,3,0:T(2,128)(2,1)}, ...), condition=%wide.region_1.2_spmd, body=%wide.region_0.1_spmd.sunk | while | flops 124159280 | bytes 48670468 | solution.py:65
  21.5 8.9 %gather_fusion = bf16[34,2,12,12,128]{4,1,3,2,0:T(2,128)(2,1)} fusion(bf16[6,2,12,12,128]{4,1,3,2,0:T(2,128)(2,1)S(1)} %get-tuple-element.115, s32[1024]{0:T(1024)S(1)} %pad_clamp_fusion.2), kind=kCustom, calls=%fused_computation.clone.1 | custom fusion | bytes 5013640 | tf_op jit(solution)/shard_map/while/body/eval_jaxpr/jit(_take)/gather | solution.py:62
  30.4 2.4 %copy_select_fusion.2 = bf16[34,2,12,12,128]{4,2,3,0,1:T(8,128)(2,1)S(1)} fusion(bf16[34,2,12,12,128]{4,1,3,2,0:T(2,128)(2,1)} %gather_fusion, pred[34]{0:T(512)(128)(4,1)S(1)} %compare_and_fusion.2), kind=kLoop, calls=%fused_computation.1.clone.1 | loop fusion | flops 1253376 | bytes 5013538 | tf_op jit(solution)/shard_map/while/body/eval_jaxpr/jit(_take)/select_n | solution.py:62
  33.9 1.5 %fusion.93 = f32[34,12,12,128]{3,1,2,0:T(8,128)S(1)} fusion(bf16[34,2,12,12,128]{4,2,3,0,1:T(8,128)(2,1)S(1)} %copy_select_fusion.2, bf16[34,2,12,12]{3,2,0,1:T(8,128)(2,1)} %bitcast.130), kind=kOutput, calls=%fused_computation.7.clone.1 | convolution fusion | flops 15040512 | bytes 4317184 | tf_op jit(solution)/shard_map/while/body/eval_jaxpr/kij,kjle->kile/dot_general | solution.py:29
  35.5 1.7 %add_convert_fusion.2 = bf16[34,12,12,128]{3,1,2,0:T(8,128)(2,1)} fusion(f32[34,12,12,128]{3,1,2,0:T(8,128)S(1)} %fusion.93, bf16[34,2,12,12,128]{4,2,3,0,1:T(8,128)(2,1)S(1)} %copy_select_fusion.2, bf16[34,2,12,12]{3,2,0,1:T(8,128)(2,1)S(1)} %bitcast.131), kind=kOutput, calls=%fused_computation.2.clone.1 | convolution fusion | flops 16293888 | bytes 6406144 | tf_op jit(solution)/shard_map/while/body/eval_jaxpr/kij,kjle->kile/dot_general | solution.py:31
  37.8 1.8 %subtract_convert_fusion.2 = bf16[34,12,12,128]{3,1,2,0:T(8,128)(2,1)} fusion(f32[34,12,12,128]{3,1,2,0:T(8,128)S(1)} %fusion.91, bf16[34,2,12,12,128]{4,2,3,0,1:T(8,128)(2,1)S(1)} %copy_select_fusion.2, bf16[34,2,12,12]{3,2,0,1:T(8,128)(2,1)S(1)} %bitcast.133), kind=kOutput, calls=%fused_computation.3.clone.1 | convolution fusion | flops 16293888 | bytes 6406144 | tf_op jit(solution)/shard_map/while/body/eval_jaxpr/kij,kjle->kile/dot_general | solution.py:28
  39.8 2.4 %fusion.95 = f32[12,12,128]{2,0,1:T(8,128)S(1)} fusion(bf16[34,12,12,128]{3,1,2,0:T(8,128)(2,1)} %subtract_convert_fusion.2, bf16[34,12,12]{0,1,2:T(8,128)(2,1)S(1)} %copy.90), kind=kOutput, calls=%fused_computation.16.clone.1 | convolution fusion | flops 15040512 | bytes 1336896 | tf_op jit(solution)/shard_map/while/body/eval_jaxpr/kile,kml->ime/dot_general | solution.py:34
  43.4 2.3 %fusion.92 = f32[12,12,128]{2,0,1:T(8,128)S(1)} fusion(bf16[34,12,12,128]{3,1,2,0:T(8,128)(2,1)} %subtract_convert_fusion.2, bf16[34,12,12]{0,1,2:T(8,128)(2,1)S(1)} %copy.89), kind=kOutput, calls=%fused_computation.17.clone.1 | convolution fusion | flops 15040512 | bytes 1336896 | tf_op jit(solution)/shard_map/while/body/eval_jaxpr/kile,kml->ime/dot_general | solution.py:37
  47.3 8.9 %gather_fusion = bf16[34,2,12,12,128]{4,1,3,2,0:T(2,128)(2,1)} fusion(bf16[6,2,12,12,128]{4,1,3,2,0:T(2,128)(2,1)S(1)} %get-tuple-element.115, s32[1024]{0:T(1024)S(1)} %pad_clamp_fusion.2), kind=kCustom, calls=%fused_computation.clone.1 | custom fusion | bytes 5013640 | tf_op jit(solution)/shard_map/while/body/eval_jaxpr/jit(_take)/gather | solution.py:62
  56.2 2.4 %copy_select_fusion.2 = bf16[34,2,12,12,128]{4,2,3,0,1:T(8,128)(2,1)S(1)} fusion(bf16[34,2,12,12,128]{4,1,3,2,0:T(2,128)(2,1)} %gather_fusion, pred[34]{0:T(512)(128)(4,1)S(1)} %compare_and_fusion.2), kind=kLoop, calls=%fused_computation.1.clone.1 | loop fusion | flops 1253376 | bytes 5013538 | tf_op jit(solution)/shard_map/while/body/eval_jaxpr/jit(_take)/select_n | solution.py:62
  59.8 1.5 %fusion.93 = f32[34,12,12,128]{3,1,2,0:T(8,128)S(1)} fusion(bf16[34,2,12,12,128]{4,2,3,0,1:T(8,128)(2,1)S(1)} %copy_select_fusion.2, bf16[34,2,12,12]{3,2,0,1:T(8,128)(2,1)} %bitcast.130), kind=kOutput, calls=%fused_computation.7.clone.1 | convolution fusion | flops 15040512 | bytes 4317184 | tf_op jit(solution)/shard_map/while/body/eval_jaxpr/kij,kjle->kile/dot_general | solution.py:29
  61.3 1.7 %add_convert_fusion.2 = bf16[34,12,12,128]{3,1,2,0:T(8,128)(2,1)} fusion(f32[34,12,12,128]{3,1,2,0:T(8,128)S(1)} %fusion.93, bf16[34,2,12,12,128]{4,2,3,0,1:T(8,128)(2,1)S(1)} %copy_select_fusion.2, bf16[34,2,12,12]{3,2,0,1:T(8,128)(2,1)S(1)} %bitcast.131), kind=kOutput, calls=%fused_computation.2.clone.1 | convolution fusion | flops 16293888 | bytes 6406144 | tf_op jit(solution)/shard_map/while/body/eval_jaxpr/kij,kjle->kile/dot_general | solution.py:31
  63.6 1.8 %subtract_convert_fusion.2 = bf16[34,12,12,128]{3,1,2,0:T(8,128)(2,1)} fusion(f32[34,12,12,128]{3,1,2,0:T(8,128)S(1)} %fusion.91, bf16[34,2,12,12,128]{4,2,3,0,1:T(8,128)(2,1)S(1)} %copy_select_fusion.2, bf16[34,2,12,12]{3,2,0,1:T(8,128)(2,1)S(1)} %bitcast.133), kind=kOutput, calls=%fused_computation.3.clone.1 | convolution fusion | flops 16293888 | bytes 6406144 | tf_op jit(solution)/shard_map/while/body/eval_jaxpr/kij,kjle->kile/dot_general | solution.py:28
  65.7 2.4 %fusion.95 = f32[12,12,128]{2,0,1:T(8,128)S(1)} fusion(bf16[34,12,12,128]{3,1,2,0:T(8,128)(2,1)} %subtract_convert_fusion.2, bf16[34,12,12]{0,1,2:T(8,128)(2,1)S(1)} %copy.90), kind=kOutput, calls=%fused_computation.16.clone.1 | convolution fusion | flops 15040512 | bytes 1336896 | tf_op jit(solution)/shard_map/while/body/eval_jaxpr/kile,kml->ime/dot_general | solution.py:34
  69.3 2.3 %fusion.92 = f32[12,12,128]{2,0,1:T(8,128)S(1)} fusion(bf16[34,12,12,128]{3,1,2,0:T(8,128)(2,1)} %subtract_convert_fusion.2, bf16[34,12,12]{0,1,2:T(8,128)(2,1)S(1)} %copy.89), kind=kOutput, calls=%fused_computation.17.clone.1 | convolution fusion | flops 15040512 | bytes 1336896 | tf_op jit(solution)/shard_map/while/body/eval_jaxpr/kile,kml->ime/dot_general | solution.py:37
  73.2 1.4 %fusion.57 = (f32[2,2,12,12,48]{4,3,2,1,0:T(8,128)S(1)}, f32[2,2,12,12,48]{4,3,2,1,0:T(8,128)S(1)}) fusion(f32[2,2,12,12,128]{4,3,2,1,0:T(8,128)} %get-tuple-element.32), kind=kLoop, calls=%fused_computation.62 | loop fusion | bytes 442368 | tf_op jit(solution)/shard_map/slice | solution.py:12
  74.6 4.5 %collective-permute-start.2 = (f32[2,2,12,12,48]{4,3,2,1,0:T(8,128)S(1)}, f32[2,2,12,12,48]{4,3,2,1,0:T(8,128)S(1)}, u32[]{:S(2)}, u32[]{:S(2)}) collective-permute-start(f32[2,2,12,12,48]{4,3,2,1,0:T(8,128)S(1)} %get-tuple-element.62), channel_id=1, source_target_pairs={{0,1},{1,2},{2,3},{3,4},{4,5},{5,6},{6,7},{8,9},{9,10},{10,11},{11... | collective-permute-start | bytes 331784 | tf_op jit(solution)/shard_map/ppermute | solution.py:15
  79.1 1.9 %collective-permute-start.3 = (f32[2,2,12,12,48]{4,3,2,1,0:T(8,128)S(1)}, f32[2,2,12,12,48]{4,3,2,1,0:T(8,128)S(1)}, u32[]{:S(2)}, u32[]{:S(2)}) collective-permute-start(f32[2,2,12,12,48]{4,3,2,1,0:T(8,128)S(1)} %get-tuple-element.63), channel_id=1, source_target_pairs={{1,0},{2,1},{3,2},{4,3},{5,4},{6,5},{7,6},{9,8},{10,9},{11,10},{12... | collective-permute-start | bytes 331784 | tf_op jit(solution)/shard_map/ppermute | solution.py:17
  81.1 1.8 %select_reduce_fusion = (f32[224,128]{1,0:T(8,128)S(1)}, f32[224,128]{1,0:T(8,128)S(1)}) fusion(f32[70]{0:T(128)S(1)} %copy-done.7, s32[224,128]{1,0:T(8,128)S(1)} %iota_subtract_fusion, s32[70]{0:T(128)S(1)} %neg.3, f32[70]{0:T(128)S(1)} %copy-done.9, s32[70]{0:T(128)S(1)} %copy-done.8), kind=kLoop, calls=%fused_computation.47 | loop fusion | flops 11984896 | bytes 345184 | tf_op jit(solution)/shard_map/reduce_sum | solution.py:47
  83.8 4.4 %collective-permute-done.3 = f32[2,2,12,12,48]{4,3,2,1,0:T(8,128)S(1)} collective-permute-done((f32[2,2,12,12,48]{4,3,2,1,0:T(8,128)S(1)}, f32[2,2,12,12,48]{4,3,2,1,0:T(8,128)S(1)}, u32[]{:S(2)}, u32[]{:S(2)}) %collective-permute-start.3) | collective-permute-done | bytes 110624 | tf_op jit(solution)/shard_map/ppermute | solution.py:17
  88.2 1.9 %fusion.48 = f32[2,2,12,12,128]{4,3,2,1,0:T(8,128)S(1)} fusion(f32[2,2,12,12,48]{4,3,2,1,0:T(8,128)S(1)} %collective-permute-done.3, f32[2,2,12,12,128]{4,3,2,1,0:T(8,128)} %get-tuple-element.32, f32[2,2,12,12,48]{4,3,2,1,0:T(8,128)S(1)} %collective-permute-done.2, f32[224,128]{1,0:T(8,128)S(1)} %get-tuple-element.49, f32[224,128]{1,0:T(8,128)S(1)} %get-tuple-element.48), kind=kOutput, calls=%fused_computation.49 | convolution fusion | flops 198467584 | bytes 1040384 | tf_op jit(solution)/shard_map/dot_general | solution.py:74
  (67 shorter events, 14.2 us)
Async XLA Ops:
  0.0 18.8 %collective-permute-start = (bf16[2,2,12,12,128]{4,1,3,2,0:T(2,128)(2,1)}, bf16[2,2,12,12,128]{4,1,3,2,0:T(2,128)(2,1)S(1)}, u32[]{:S(2)}, u32[]{:S(2)}) collective-permute-start(bf16[2,2,12,12,128]{4,1,3,2,0:T(2,128)(2,1)} %param.8), channel_id=1, source_target_pairs={{0,8},{8,16},{16,24},{24,32},{32,40},{40,48},{48,56},{56,64},{64,7... | collective-permute-start | bytes 442376 | tf_op jit(solution)/shard_map/ppermute | solution.py:15
  4.0 15.8 %collective-permute-start.1 = (bf16[2,2,12,12,128]{4,1,3,2,0:T(2,128)(2,1)}, bf16[2,2,12,12,128]{4,1,3,2,0:T(2,128)(2,1)S(1)}, u32[]{:S(2)}, u32[]{:S(2)}) collective-permute-start(bf16[2,2,12,12,128]{4,1,3,2,0:T(2,128)(2,1)} %param.8), channel_id=1, source_target_pairs={{8,0},{16,8},{24,16},{32,24},{40,32},{48,40},{56,48},{64,56},{72,6... | collective-permute-start | bytes 442376 | tf_op jit(solution)/shard_map/ppermute | solution.py:17
  21.4 59.7 %copy-start.7 = (f32[70]{0:T(128)S(1)}, f32[70]{0:T(128)}, u32[]{:S(2)}) copy-start(f32[70]{0:T(128)} %param.13) | copy-start | bytes 844
  21.4 59.7 %copy-start.8 = (s32[70]{0:T(128)S(1)}, s32[70]{0:T(128)}, u32[]{:S(2)}) copy-start(s32[70]{0:T(128)} %param.11) | copy-start | bytes 844
  21.4 59.7 %copy-start.9 = (f32[70]{0:T(128)S(1)}, f32[70]{0:T(128)}, u32[]{:S(2)}) copy-start(f32[70]{0:T(128)} %param.12) | copy-start | bytes 844
  21.4 8.9 %copy-start = (bf16[6,2,12,12,128]{4,1,3,2,0:T(2,128)(2,1)}, bf16[6,2,12,12,128]{4,1,3,2,0:T(2,128)(2,1)S(1)}, u32[]{:S(2)}) copy-start(bf16[6,2,12,12,128]{4,1,3,2,0:T(2,128)(2,1)S(1)} %get-tuple-element.115) | copy-start | bytes 1327108 | tf_op jit(solution)/shard_map/while
  30.3 2.4 %copy-start.6 = (bf16[2,34,2,12,12]{1,2,4,3,0:T(2,128)(2,1)S(1)}, bf16[2,34,2,12,12]{1,2,4,3,0:T(2,128)(2,1)}, u32[]{:S(2)}) copy-start(bf16[2,34,2,12,12]{1,2,4,3,0:T(2,128)(2,1)} %get-tuple-element.113) | copy-start | bytes 117508 | tf_op jit(solution)/shard_map/while
  33.9 1.6 %copy-start.3 = (bf16[1,34,2,12,12]{4,3,1,2,0:T(8,128)(2,1)S(1)}, bf16[1,34,2,12,12]{4,3,1,2,0:T(8,128)(2,1)}, u32[]{:S(2)}) copy-start(bf16[1,34,2,12,12]{4,3,1,2,0:T(8,128)(2,1)} %copy.88) | copy-start | bytes 58756 | tf_op jit(solution)/shard_map/while
  39.5 3.0 %copy-start.2 = (bf16[34,12,12,128]{3,1,2,0:T(8,128)(2,1)S(1)}, bf16[34,12,12,128]{3,1,2,0:T(8,128)(2,1)}, u32[]{:S(2)}) copy-start(bf16[34,12,12,128]{3,1,2,0:T(8,128)(2,1)} %add_convert_fusion.2) | copy-start | bytes 3760132 | tf_op jit(solution)/shard_map/while
  42.5 4.0 %copy-start.4 = (f32[2,2,12,12,128]{4,3,2,1,0:T(8,128)S(1)}, f32[2,2,12,12,128]{4,3,2,1,0:T(8,128)}, u32[]{:S(2)}) copy-start(f32[2,2,12,12,128]{4,3,2,1,0:T(8,128)} %get-tuple-element.106) | copy-start | bytes 884740 | tf_op jit(solution)/shard_map/while
  42.5 4.8 %copy-start.1 = (bf16[6,2,12,12,128]{4,1,3,2,0:T(2,128)(2,1)S(1)}, bf16[6,2,12,12,128]{4,1,3,2,0:T(2,128)(2,1)}, u32[]{:S(2)}) copy-start(bf16[6,2,12,12,128]{4,1,3,2,0:T(2,128)(2,1)} %copy-done) | copy-start | bytes 1327108 | tf_op jit(solution)/shard_map/while
  46.6 0.8 copy-start.5
  47.3 8.9 %copy-start = (bf16[6,2,12,12,128]{4,1,3,2,0:T(2,128)(2,1)}, bf16[6,2,12,12,128]{4,1,3,2,0:T(2,128)(2,1)S(1)}, u32[]{:S(2)}) copy-start(bf16[6,2,12,12,128]{4,1,3,2,0:T(2,128)(2,1)S(1)} %get-tuple-element.115) | copy-start | bytes 1327108 | tf_op jit(solution)/shard_map/while
  56.2 2.4 %copy-start.6 = (bf16[2,34,2,12,12]{1,2,4,3,0:T(2,128)(2,1)S(1)}, bf16[2,34,2,12,12]{1,2,4,3,0:T(2,128)(2,1)}, u32[]{:S(2)}) copy-start(bf16[2,34,2,12,12]{1,2,4,3,0:T(2,128)(2,1)} %get-tuple-element.113) | copy-start | bytes 117508 | tf_op jit(solution)/shard_map/while
  59.8 1.6 %copy-start.3 = (bf16[1,34,2,12,12]{4,3,1,2,0:T(8,128)(2,1)S(1)}, bf16[1,34,2,12,12]{4,3,1,2,0:T(8,128)(2,1)}, u32[]{:S(2)}) copy-start(bf16[1,34,2,12,12]{4,3,1,2,0:T(8,128)(2,1)} %copy.88) | copy-start | bytes 58756 | tf_op jit(solution)/shard_map/while
  65.4 3.0 %copy-start.2 = (bf16[34,12,12,128]{3,1,2,0:T(8,128)(2,1)S(1)}, bf16[34,12,12,128]{3,1,2,0:T(8,128)(2,1)}, u32[]{:S(2)}) copy-start(bf16[34,12,12,128]{3,1,2,0:T(8,128)(2,1)} %add_convert_fusion.2) | copy-start | bytes 3760132 | tf_op jit(solution)/shard_map/while
  68.4 4.0 %copy-start.4 = (f32[2,2,12,12,128]{4,3,2,1,0:T(8,128)S(1)}, f32[2,2,12,12,128]{4,3,2,1,0:T(8,128)}, u32[]{:S(2)}) copy-start(f32[2,2,12,12,128]{4,3,2,1,0:T(8,128)} %get-tuple-element.106) | copy-start | bytes 884740 | tf_op jit(solution)/shard_map/while
  68.4 4.8 %copy-start.1 = (bf16[6,2,12,12,128]{4,1,3,2,0:T(2,128)(2,1)S(1)}, bf16[6,2,12,12,128]{4,1,3,2,0:T(2,128)(2,1)}, u32[]{:S(2)}) copy-start(bf16[6,2,12,12,128]{4,1,3,2,0:T(2,128)(2,1)} %copy-done) | copy-start | bytes 1327108 | tf_op jit(solution)/shard_map/while
  72.4 0.8 copy-start.5
  74.6 9.2 %collective-permute-start.2 = (f32[2,2,12,12,48]{4,3,2,1,0:T(8,128)S(1)}, f32[2,2,12,12,48]{4,3,2,1,0:T(8,128)S(1)}, u32[]{:S(2)}, u32[]{:S(2)}) collective-permute-start(f32[2,2,12,12,48]{4,3,2,1,0:T(8,128)S(1)} %get-tuple-element.62), channel_id=1, source_target_pairs={{0,1},{1,2},{2,3},{3,4},{4,5},{5,6},{6,7},{8,9},{9,10},{10,11},{11... | collective-permute-start | bytes 331784 | tf_op jit(solution)/shard_map/ppermute | solution.py:15
  79.1 9.1 %collective-permute-start.3 = (f32[2,2,12,12,48]{4,3,2,1,0:T(8,128)S(1)}, f32[2,2,12,12,48]{4,3,2,1,0:T(8,128)S(1)}, u32[]{:S(2)}, u32[]{:S(2)}) collective-permute-start(f32[2,2,12,12,48]{4,3,2,1,0:T(8,128)S(1)} %get-tuple-element.63), channel_id=1, source_target_pairs={{1,0},{2,1},{3,2},{4,3},{5,4},{6,5},{7,6},{9,8},{10,9},{11,10},{12... | collective-permute-start | bytes 331784 | tf_op jit(solution)/shard_map/ppermute | solution.py:17
where the time goes:
time: 91.5 us; the launch traced here: 91.1 us
  matrix products  26 us (28%)
  local copies, waits for them, and re-layouts  25 us (27%)
  starting transfers between devices  23.4 us (26%)
  other arithmetic  9.62 us (11%)
  waiting for transfers between devices  6.67 us (7%)
    gather x2, local copies, waits for them, and re-layouts, one_atom(): gathered = jnp.take(window, listed, axis=0)  17.7 us
    ppermute x2, starting transfers between devices, extended(): lax.ppermute(head, axis, [((i + 1) % count, i) for i in range(ends)])  14.9 us
    ppermute x2, starting transfers between devices, extended(): lax.ppermute(tail, axis, [(i, (i + 1) % count) for i in range(ends)])  8.52 us
    ppermute x2, waiting for transfers between devices, extended(): lax.ppermute(head, axis, [((i + 1) % count, i) for i in range(ends)])  5.41 us
    dot_general x2, matrix products, couple(): jnp.einsum('kile,kml->ime', x_re, blocks[:, 0], preferred_element_type=f32)  4.87 us
    select_n x4, other arithmetic, one_atom(): gathered = jnp.take(window, listed, axis=0)  4.78 us
    dot_general x2, matrix products, couple(): jnp.einsum('kile,kml->ime', x_re, blocks[:, 1], preferred_element_type=f32)  4.58 us
    dot_general x2, matrix products, couple(): jnp.einsum('kij,kjle->kile', blocks[:, 1], gathered[:, 1], preferred_elem...  3.55 us
  transfers between devices with their start and end apart: 4, of which 4 were waited for; matrix products, arithmetic and copies ran while one was open for 4% of the time, Pallas kernels for 0%

commit v1 on v0

--- a/solution.py
+++ b/solution.py
@@ -21,25 +21,6 @@
     return cells
 
 
-def couple(blocks, gathered):
-    f32 = jnp.float32
-    x_re = jnp.einsum(
-        "kij,kjle->kile", blocks[:, 0], gathered[:, 0], preferred_element_type=f32
-    ) - jnp.einsum("kij,kjle->kile", blocks[:, 1], gathered[:, 1], preferred_element_type=f32)
-    x_im = jnp.einsum(
-        "kij,kjle->kile", blocks[:, 0], gathered[:, 1], preferred_element_type=f32
-    ) + jnp.einsum("kij,kjle->kile", blocks[:, 1], gathered[:, 0], preferred_element_type=f32)
-    x_re = x_re.astype(jnp.bfloat16)
-    x_im = x_im.astype(jnp.bfloat16)
-    p_re = jnp.einsum("kile,kml->ime", x_re, blocks[:, 0], preferred_element_type=f32) + jnp.einsum(
-        "kile,kml->ime", x_im, blocks[:, 1], preferred_element_type=f32
-    )
-    p_im = jnp.einsum("kile,kml->ime", x_im, blocks[:, 0], preferred_element_type=f32) - jnp.einsum(
-        "kile,kml->ime", x_re, blocks[:, 1], preferred_element_type=f32
-    )
-    return jnp.stack([p_re, p_im])
-
-
 def make_kernel(spread_diff, offsets, w_emit, w_absorb):
     kernel = jnp.sum(
         jnp.where(spread_diff[:, :, None] == offsets, w_emit, jnp.float32(0.0)), axis=2
@@ -49,6 +30,20 @@
     )
 
 
+def coupled_blocks(window, coupling, local_ids):
+    f32, bf16 = jnp.float32, jnp.bfloat16
+    nwin = window.shape[0]
+    onehot = (local_ids[:, :, None] == jnp.arange(nwin, dtype=local_ids.dtype)).astype(bf16)
+    mr = coupling[:, :, 0]
+    mi = coupling[:, :, 1]
+    mbig = jnp.stack([jnp.stack([mr, -mi], axis=2), jnp.stack([mi, mr], axis=2)], axis=2)
+    left = mbig[:, :, :, None] * onehot[:, :, None, :, None, None, None]
+    x = jnp.einsum("akqwpij,wpjle->akqile", left, window, preferred_element_type=f32).astype(bf16)
+    x = x.transpose(0, 1, 2, 4, 3, 5)
+    right = jnp.stack([jnp.stack([mr, mi], axis=2), jnp.stack([-mi, mr], axis=2)], axis=2)
+    return jnp.einsum("akplie,akqpml->aqime", x, right, preferred_element_type=f32)
+
+
 def shards(green, coupling, neighbours, offsets, w_emit, w_absorb):
     hi = lax.Precision.HIGHEST
     atoms_here = green.shape[0]
@@ -56,13 +51,8 @@
     reach = points * 3 // 8
     window = extended(green, (("atom", 0),), atoms_here)
     local_ids = neighbours - (lax.axis_index("atom") - 1) * atoms_here
+    coupled = coupled_blocks(window, coupling, local_ids)
 
-    def one_atom(packed):
-        blocks, listed = packed
-        gathered = jnp.take(window, listed, axis=0)
-        return couple(blocks, gathered)
-
-    coupled = lax.map(one_atom, (coupling, local_ids))
     extent = points + 2 * reach
     spread_diff = (
         jnp.arange(extent, dtype=jnp.int32)[:, None]

time: 91.5 us -> 40.8 us (0.45)
  matrix products: 26 us -> 4.23 us
  local copies, waits for them, and re-layouts: 25 us -> 3.3 us
  other arithmetic: 9.62 us -> 3.43 us
    dot_general x16 -> x1, matrix products: 24.1 us -> 3.33 us  [coupled_blocks(): jnp.einsum('akplie,akqpml->aqime', x, right, preferred_element_type=f32)]
    gather x2 -> x0, local copies, waits for them, and re-layouts: 17.7 us -> none  [one_atom(): gathered = jnp.take(window, listed, axis=0)]
    select_n x4 -> x0, other arithmetic: 4.78 us -> none  [one_atom(): gathered = jnp.take(window, listed, axis=0)]
    dynamic_slice x4 -> x0, local copies, waits for them, and re-layouts: 2.26 us -> none  [shards(): coupled = lax.map(one_atom, (coupling, local_ids))]
    unnamed x6 -> x10, local copies, waits for them, and re-layouts: 0.02 us -> 1.94 us
    while x28 -> x0, local copies, waits for them, and re-layouts: 1.55 us -> none
    concatenate x1 -> x0, other arithmetic: 1.52 us -> none  [extended(): jnp.concatenate([lax.ppermute(tail, axis, [(i, (i + 1) % count) for i in...]
    mul x0 -> x1, other arithmetic: none -> 1.31 us  [coupled_blocks(): left = mbig[:, :, :, None] * onehot[:, :, None, :, None, None, None]]
  transfers between devices with their start and end apart: 4 -> 4, of which waited for: 4 -> 3; matrix products, arithmetic and copies ran while one was open for 4% -> 11% of each run, Pallas kernels for 0% -> 0%
where the time goes in v1:
time: 40.8 us; the launch traced here: 40.6 us
  starting transfers between devices  23.5 us (58%)
  waiting for transfers between devices  5.97 us (15%)
  matrix products  4.23 us (10%)
  other arithmetic  3.43 us (8%)
  local copies, waits for them, and re-layouts  3.3 us (8%)
    ppermute x2, starting transfers between devices, extended(): lax.ppermute(head, axis, [((i + 1) % count, i) for i in range(ends)])  14.9 us
    ppermute x2, starting transfers between devices, extended(): lax.ppermute(tail, axis, [(i, (i + 1) % count) for i in range(ends)])  8.53 us
    ppermute x2, waiting for transfers between devices, extended(): lax.ppermute(head, axis, [((i + 1) % count, i) for i in range(ends)])  5.03 us
    dot_general x1, matrix products, coupled_blocks(): jnp.einsum('akplie,akqpml->aqime', x, right, preferred_element_type=f32)  3.33 us
    unnamed x10, local copies, waits for them, and re-layouts  1.94 us
    reduce_sum x1, other arithmetic, make_kernel(): jnp.sum(jnp.where(spread_diff[:, :, None] == -offsets, w_absorb, jnp.floa...  1.81 us
    mul x1, other arithmetic, coupled_blocks(): left = mbig[:, :, :, None] * onehot[:, :, None, :, None, None, None]  1.31 us
    dot_general x1, local copies, waits for them, and re-layouts, shards(): jnp.dot(widened.reshape(-1, extent), kernel, precision=hi, preferred_elem...  0.94 us
  transfers between devices with their start and end apart: 4, of which 3 were waited for; matrix products, arithmetic and copies ran while one was open for 11% of the time, Pallas kernels for 0%

profile of v1, /device:TPU:57, one launch (start us, length us, event | category | flops | bytes accessed | tf_op | source)
XLA Modules:
  0.0 40.6 jit_solution(392575050743611791)
XLA Ops:
  0.0 1.0 %copy.21 = bf16[2,2,12,12,128]{4,2,0,1,3:T(8,128)(2,1)S(1)} copy(bf16[2,2,12,12,128]{4,1,3,2,0:T(2,128)(2,1)} %param.6) | data formatting | bytes 294912 | tf_op args[0]
  1.0 4.0 %collective-permute-start = (bf16[2,2,12,12,128]{4,2,0,1,3:T(8,128)(2,1)S(1)}, bf16[2,2,12,12,128]{4,2,0,1,3:T(8,128)(2,1)S(1)}, u32[]{:S(2)}, u32[]{:S(2)}) collective-permute-start(bf16[2,2,12,12,128]{4,2,0,1,3:T(8,128)(2,1)S(1)} %copy.21), channel_id=1, source_target_pairs={{0,8},{8,16},{16,24},{24,32},{32,40},{40,48},{48,56},{56,64},{64,7... | collective-permute-start | bytes 442376 | tf_op jit(solution)/shard_map/ppermute | solution.py:15
  5.0 13.0 %collective-permute-start.1 = (bf16[2,2,12,12,128]{4,2,0,1,3:T(8,128)(2,1)S(1)}, bf16[2,2,12,12,128]{4,2,0,1,3:T(8,128)(2,1)S(1)}, u32[]{:S(2)}, u32[]{:S(2)}) collective-permute-start(bf16[2,2,12,12,128]{4,2,0,1,3:T(8,128)(2,1)S(1)} %copy.21), channel_id=1, source_target_pairs={{8,0},{16,8},{24,16},{32,24},{40,32},{48,40},{56,48},{64,56},{72,6... | collective-permute-start | bytes 442376 | tf_op jit(solution)/shard_map/ppermute | solution.py:17
  18.0 0.9 %copy.42 = bf16[2,34,2,12,12]{1,3,2,4,0:T(8,128)(2,1)S(1)} copy(bf16[2,34,2,12,12]{1,2,4,3,0:T(2,128)(2,1)} %param.7) | data formatting | bytes 78336 | tf_op args[1]
  19.0 0.1 fusion.28
  19.1 0.1 pad_maximum_fusion
  19.2 0.2 copy.20
  19.5 0.0 copy-done
  19.5 0.0 copy-done.2
  19.5 1.3 %multiply_bitcast_fusion = bf16[2,34,2,6,2,12,12,1]{1,4,6,5,3,2,0,7:T(2,128)(2,1)S(1)} fusion(bf16[2,34,6]{1,2,0:T(8,128)(2,1)S(1)} %fusion.32, bf16[2,34,2,2,12,12]{1,3,5,4,2,0:T(2,128)(2,1)S(1)} %copy.20), kind=kLoop, calls=%fused_computation.7 | loop fusion | flops 235008 | bytes 549168 | tf_op jit(solution)/shard_map/mul | solution.py:40
  20.8 0.1 iota_subtract_fusion
  20.9 0.0 collective-permute-done
  20.9 0.6 %collective-permute-done.1 = bf16[2,2,12,12,128]{4,2,0,1,3:T(8,128)(2,1)S(1)} collective-permute-done((bf16[2,2,12,12,128]{4,2,0,1,3:T(8,128)(2,1)S(1)}, bf16[2,2,12,12,128]{4,2,0,1,3:T(8,128)(2,1)S(1)}, u32[]{:S(2)}, u32[]{:S(2)}) %collective-permute-start.1) | collective-permute-done | bytes 147488 | tf_op jit(solution)/shard_map/ppermute | solution.py:17
  21.6 3.3 %fusion.7 = f32[2,2,12,12,128]{4,3,2,1,0:T(8,128)S(1)} fusion(bf16[2,34,2,6,2,12,12,1]{1,4,6,5,3,2,0,7:T(2,128)(2,1)S(1)} %multiply_bitcast_fusion, bf16[2,2,12,12,128]{4,2,0,1,3:T(8,128)(2,1)S(1)} %collective-permute-done.1, bf16[2,2,12,12,128]{4,2,0,1,3:T(8,128)(2,1)S(1)} %copy.21, bf16[2,2,12,12,128]{4,2,0,1,3:T(8,128)(2,1)S(1)} %collective-permute-done, ...), kind=kOutput, calls=%fused_computation.8 | convolution fusion | flops 846259200 | bytes 1285632 | tf_op jit(solution)/shard_map/akplie,akqpml->aqime/dot_general | solution.py:44
  24.9 0.2 fusion.36
  25.1 4.5 %collective-permute-start.2 = (f32[2,2,12,12,48]{4,3,2,1,0:T(8,128)S(1)}, f32[2,2,12,12,48]{4,3,2,1,0:T(8,128)S(1)}, u32[]{:S(2)}, u32[]{:S(2)}) collective-permute-start(f32[2,2,12,12,48]{4,3,2,1,0:T(8,128)S(1)} %get-tuple-element.7), channel_id=1, source_target_pairs={{0,1},{1,2},{2,3},{3,4},{4,5},{5,6},{6,7},{8,9},{9,10},{10,11},{11... | collective-permute-start | bytes 331784 | tf_op jit(solution)/shard_map/ppermute | solution.py:15
  29.6 1.9 %collective-permute-start.3 = (f32[2,2,12,12,48]{4,3,2,1,0:T(8,128)S(1)}, f32[2,2,12,12,48]{4,3,2,1,0:T(8,128)S(1)}, u32[]{:S(2)}, u32[]{:S(2)}) collective-permute-start(f32[2,2,12,12,48]{4,3,2,1,0:T(8,128)S(1)} %get-tuple-element.8), channel_id=1, source_target_pairs={{1,0},{2,1},{3,2},{4,3},{5,4},{6,5},{7,6},{9,8},{10,9},{11,10},{12... | collective-permute-start | bytes 331784 | tf_op jit(solution)/shard_map/ppermute | solution.py:17
  31.6 0.0 copy-done.1
  31.6 0.0 copy-done.3
  31.6 1.8 %select_reduce_fusion = (f32[224,128]{1,0:T(8,128)S(1)}, f32[224,128]{1,0:T(8,128)S(1)}) fusion(f32[70]{0:T(128)S(1)} %copy-done.1, s32[224,128]{1,0:T(8,128)S(1)} %iota_subtract_fusion, s32[70]{0:T(128)S(1)} %neg.9, f32[70]{0:T(128)S(1)} %copy-done.3, s32[70]{0:T(128)S(1)} %copy-done.2), kind=kLoop, calls=%fused_computation.1 | loop fusion | flops 11984896 | bytes 345184 | tf_op jit(solution)/shard_map/reduce_sum | solution.py:28
  33.4 0.9 %collective-permute-done.2 = f32[2,2,12,12,48]{4,3,2,1,0:T(8,128)S(1)} collective-permute-done((f32[2,2,12,12,48]{4,3,2,1,0:T(8,128)S(1)}, f32[2,2,12,12,48]{4,3,2,1,0:T(8,128)S(1)}, u32[]{:S(2)}, u32[]{:S(2)}) %collective-permute-start.2) | collective-permute-done | bytes 110624 | tf_op jit(solution)/shard_map/ppermute | solution.py:15
  34.3 4.4 %collective-permute-done.3 = f32[2,2,12,12,48]{4,3,2,1,0:T(8,128)S(1)} collective-permute-done((f32[2,2,12,12,48]{4,3,2,1,0:T(8,128)S(1)}, f32[2,2,12,12,48]{4,3,2,1,0:T(8,128)S(1)}, u32[]{:S(2)}, u32[]{:S(2)}) %collective-permute-start.3) | collective-permute-done | bytes 110624 | tf_op jit(solution)/shard_map/ppermute | solution.py:17
  38.7 0.9 %fusion.12 = f32[2,2,12,12,128]{4,3,2,1,0:T(8,128)S(1)} fusion(f32[2,2,12,12,48]{4,3,2,1,0:T(8,128)S(1)} %collective-permute-done.3, f32[2,2,12,12,128]{4,3,2,1,0:T(8,128)S(1)} %fusion.7, f32[2,2,12,12,48]{4,3,2,1,0:T(8,128)S(1)} %collective-permute-done.2, f32[224,128]{1,0:T(8,128)S(1)} %get-tuple-element.6, f32[224,128]{1,0:T(8,128)S(1)} %get-tuple-element.5), kind=kOutput, calls=%fused_computation.9 | convolution fusion | flops 198467584 | bytes 1040384 | tf_op jit(solution)/shard_map/dot_general | solution.py:64
  39.6 0.9 %copy.25 = f32[2,2,12,12,128]{4,1,3,2,0:T(2,128)} copy(f32[2,2,12,12,128]{4,3,2,1,0:T(8,128)S(1)} %fusion.12) | data formatting | bytes 589824 | tf_op jit(solution)/shard_map/dot_general | solution.py:64
  (9 shorter events, 0.1 us)
Async XLA Ops:
  0.0 19.5 %copy-start = (s32[2,34]{1,0:T(2,128)S(1)}, s32[2,34]{1,0:T(2,128)}, u32[]{:S(2)}) copy-start(s32[2,34]{1,0:T(2,128)} %param.8) | copy-start | bytes 820
  0.0 19.5 %copy-start.2 = (s32[70]{0:T(128)S(1)}, s32[70]{0:T(128)}, u32[]{:S(2)}) copy-start(s32[70]{0:T(128)} %param.9) | copy-start | bytes 844
  1.0 19.9 %collective-permute-start = (bf16[2,2,12,12,128]{4,2,0,1,3:T(8,128)(2,1)S(1)}, bf16[2,2,12,12,128]{4,2,0,1,3:T(8,128)(2,1)S(1)}, u32[]{:S(2)}, u32[]{:S(2)}) collective-permute-start(bf16[2,2,12,12,128]{4,2,0,1,3:T(8,128)(2,1)S(1)} %copy.21), channel_id=1, source_target_pairs={{0,8},{8,16},{16,24},{24,32},{32,40},{40,48},{48,56},{56,64},{64,7... | collective-permute-start | bytes 442376 | tf_op jit(solution)/shard_map/ppermute | solution.py:15
  5.0 16.6 %collective-permute-start.1 = (bf16[2,2,12,12,128]{4,2,0,1,3:T(8,128)(2,1)S(1)}, bf16[2,2,12,12,128]{4,2,0,1,3:T(8,128)(2,1)S(1)}, u32[]{:S(2)}, u32[]{:S(2)}) collective-permute-start(bf16[2,2,12,12,128]{4,2,0,1,3:T(8,128)(2,1)S(1)} %copy.21), channel_id=1, source_target_pairs={{8,0},{16,8},{24,16},{32,24},{40,32},{48,40},{56,48},{64,56},{72,6... | collective-permute-start | bytes 442376 | tf_op jit(solution)/shard_map/ppermute | solution.py:17
  21.6 10.0 %copy-start.1 = (f32[70]{0:T(128)S(1)}, f32[70]{0:T(128)}, u32[]{:S(2)}) copy-start(f32[70]{0:T(128)} %param.11) | copy-start | bytes 844
  21.6 10.0 %copy-start.3 = (f32[70]{0:T(128)S(1)}, f32[70]{0:T(128)}, u32[]{:S(2)}) copy-start(f32[70]{0:T(128)} %param.10) | copy-start | bytes 844
  25.1 9.2 %collective-permute-start.2 = (f32[2,2,12,12,48]{4,3,2,1,0:T(8,128)S(1)}, f32[2,2,12,12,48]{4,3,2,1,0:T(8,128)S(1)}, u32[]{:S(2)}, u32[]{:S(2)}) collective-permute-start(f32[2,2,12,12,48]{4,3,2,1,0:T(8,128)S(1)} %get-tuple-element.7), channel_id=1, source_target_pairs={{0,1},{1,2},{2,3},{3,4},{4,5},{5,6},{6,7},{8,9},{9,10},{10,11},{11... | collective-permute-start | bytes 331784 | tf_op jit(solution)/shard_map/ppermute | solution.py:15
  29.6 9.1 %collective-permute-start.3 = (f32[2,2,12,12,48]{4,3,2,1,0:T(8,128)S(1)}, f32[2,2,12,12,48]{4,3,2,1,0:T(8,128)S(1)}, u32[]{:S(2)}, u32[]{:S(2)}) collective-permute-start(f32[2,2,12,12,48]{4,3,2,1,0:T(8,128)S(1)} %get-tuple-element.8), channel_id=1, source_target_pairs={{1,0},{2,1},{3,2},{4,3},{5,4},{6,5},{7,6},{9,8},{10,9},{11,10},{12... | collective-permute-start | bytes 331784 | tf_op jit(solution)/shard_map/ppermute | solution.py:17

commit v2 on v1

--- a/solution.py
+++ b/solution.py
@@ -7,15 +7,18 @@
 def extended(cells, sides, width):
     for axis, dim in sides:
         count = lax.axis_size(axis)
-        ends = count - 1
+        even = lax.axis_index(axis) % 2 == 0
         head = lax.slice_in_dim(cells, 0, width, axis=dim)
         tail = lax.slice_in_dim(cells, cells.shape[dim] - width, cells.shape[dim], axis=dim)
+        edges = {
+            parity: [(i, i + 1) for i in range(parity, count - 1, 2)]
+            + [(i + 1, i) for i in range(parity, count - 1, 2)]
+            for parity in (0, 1)
+        }
+        from_even = lax.ppermute(jnp.where(even, tail, head), axis, edges[0])
+        from_odd = lax.ppermute(jnp.where(even, head, tail), axis, edges[1])
         cells = jnp.concatenate(
-            [
-                lax.ppermute(tail, axis, [(i, (i + 1) % count) for i in range(ends)]),
-                cells,
-                lax.ppermute(head, axis, [((i + 1) % count, i) for i in range(ends)]),
-            ],
+            [jnp.where(even, from_odd, from_even), cells, jnp.where(even, from_even, from_odd)],
             axis=dim,
         )
     return cells

time: 40.8 us -> 39.7 us (0.973)
  waiting for transfers between devices: 5.97 us -> 4.21 us
    ppermute x4, waiting for transfers between devices: 5.97 us -> 4.21 us  [the longest x2 2.52 us: extended(): from_even = lax.ppermute(jnp.where(even, tail, head), axis, edges[0])]
  transfers between devices with their start and end apart: 4 -> 4, of which waited for: 3 -> 2; matrix products, arithmetic and copies ran while one was open for 11% -> 12% of each run, Pallas kernels for 0% -> 0%
where the time goes in v2:
time: 39.7 us; the launch traced here: 39.2 us
  starting transfers between devices  23.7 us (60%)
  matrix products  4.24 us (11%)
  waiting for transfers between devices  4.21 us (11%)
  other arithmetic  3.7 us (9%)
  local copies, waits for them, and re-layouts  3.11 us (8%)
    ppermute x2, starting transfers between devices, extended(): from_odd = lax.ppermute(jnp.where(even, head, tail), axis, edges[1])  19.9 us
    ppermute x2, starting transfers between devices, extended(): from_even = lax.ppermute(jnp.where(even, tail, head), axis, edges[0])  3.84 us
    dot_general x1, matrix products, coupled_blocks(): jnp.einsum('akplie,akqpml->aqime', x, right, preferred_element_type=f32)  3.33 us
    ppermute x2, waiting for transfers between devices, extended(): from_even = lax.ppermute(jnp.where(even, tail, head), axis, edges[0])  2.52 us
    unnamed x10, local copies, waits for them, and re-layouts  1.94 us
    reduce_sum x1, other arithmetic, make_kernel(): jnp.sum(jnp.where(spread_diff[:, :, None] == -offsets, w_absorb, jnp.floa...  1.81 us
    ppermute x2, waiting for transfers between devices, extended(): from_odd = lax.ppermute(jnp.where(even, head, tail), axis, edges[1])  1.68 us
    mul x1, other arithmetic, coupled_blocks(): left = mbig[:, :, :, None] * onehot[:, :, None, :, None, None, None]  1.31 us
  transfers between devices with their start and end apart: 4, of which 2 were waited for; matrix products, arithmetic and copies ran while one was open for 12% of the time, Pallas kernels for 0%

profile of v2, /device:TPU:57, one launch (start us, length us, event | category | flops | bytes accessed | tf_op | source)
XLA Modules:
  0.0 39.2 jit_solution(11948229167500974947)
XLA Ops:
  0.0 1.0 %copy.21 = bf16[2,2,12,12,128]{4,2,0,1,3:T(8,128)(2,1)S(1)} copy(bf16[2,2,12,12,128]{4,1,3,2,0:T(2,128)(2,1)} %param.6) | data formatting | bytes 294912 | tf_op args[0]
  1.0 15.1 %collective-permute-start = (bf16[2,2,12,12,128]{4,2,0,1,3:T(8,128)(2,1)S(1)}, bf16[2,2,12,12,128]{4,2,0,1,3:T(8,128)(2,1)S(1)}, u32[]{:S(2)}, u32[]{:S(2)}) collective-permute-start(bf16[2,2,12,12,128]{4,2,0,1,3:T(8,128)(2,1)S(1)} %copy.21), channel_id=1, source_target_pairs={{8,16},{24,32},{40,48},{56,64},{72,80},{88,96},{104,112},{120,128}... | collective-permute-start | bytes 442376 | tf_op jit(solution)/shard_map/ppermute | solution.py:19
  16.1 1.9 %collective-permute-start.1 = (bf16[2,2,12,12,128]{4,2,0,1,3:T(8,128)(2,1)S(1)}, bf16[2,2,12,12,128]{4,2,0,1,3:T(8,128)(2,1)S(1)}, u32[]{:S(2)}, u32[]{:S(2)}) collective-permute-start(bf16[2,2,12,12,128]{4,2,0,1,3:T(8,128)(2,1)S(1)} %copy.21), channel_id=1, source_target_pairs={{0,8},{16,24},{32,40},{48,56},{64,72},{80,88},{96,104},{112,120},{... | collective-permute-start | bytes 442376 | tf_op jit(solution)/shard_map/ppermute | solution.py:18
  18.1 0.9 %copy.42 = bf16[2,34,2,12,12]{1,3,2,4,0:T(8,128)(2,1)S(1)} copy(bf16[2,34,2,12,12]{1,2,4,3,0:T(2,128)(2,1)} %param.7) | data formatting | bytes 78336 | tf_op args[1]
  19.0 0.1 fusion.28
  19.1 0.1 pad_maximum_fusion
  19.2 0.2 copy.20
  19.5 0.0 copy-done.2
  19.5 1.3 %multiply_bitcast_fusion = bf16[2,34,2,6,2,12,12,1]{1,4,6,5,3,2,0,7:T(2,128)(2,1)S(1)} fusion(bf16[2,34,6]{1,2,0:T(8,128)(2,1)S(1)} %fusion.32, bf16[2,34,2,2,12,12]{1,3,5,4,2,0:T(2,128)(2,1)S(1)} %copy.20), kind=kLoop, calls=%fused_computation.7 | loop fusion | flops 235008 | bytes 549168 | tf_op jit(solution)/shard_map/mul | solution.py:43
  20.9 0.1 iota_subtract_fusion
  21.0 0.0 collective-permute-done
  21.0 2.5 %collective-permute-done.1 = bf16[2,2,12,12,128]{4,2,0,1,3:T(8,128)(2,1)S(1)} collective-permute-done((bf16[2,2,12,12,128]{4,2,0,1,3:T(8,128)(2,1)S(1)}, bf16[2,2,12,12,128]{4,2,0,1,3:T(8,128)(2,1)S(1)}, u32[]{:S(2)}, u32[]{:S(2)}) %collective-permute-start.1) | collective-permute-done | bytes 147488 | tf_op jit(solution)/shard_map/ppermute | solution.py:18
  23.5 0.0 copy-start.1
  23.5 0.0 copy-start.3
  23.5 3.3 %fusion.7 = f32[2,2,12,12,128]{4,3,2,1,0:T(8,128)S(1)} fusion(bf16[2,34,2,6,2,12,12,1]{1,4,6,5,3,2,0,7:T(2,128)(2,1)S(1)} %multiply_bitcast_fusion, bf16[2,2,12,12,128]{4,2,0,1,3:T(8,128)(2,1)S(1)} %get-tuple-element.12, bf16[2,2,12,12,128]{4,2,0,1,3:T(8,128)(2,1)S(1)} %copy.21, bf16[2,2,12,12,128]{4,2,0,1,3:T(8,128)(2,1)S(1)} %get-tuple-element.11, ...), kind=kOutput, calls=%fused_computation.8 | convolution fusion | flops 846259200 | bytes 1285632 | tf_op jit(solution)/shard_map/akplie,akqpml->aqime/dot_general | solution.py:47
  26.9 0.2 slice_select_fusion.1
  27.1 4.8 %collective-permute-start.2 = (f32[2,2,12,12,48]{4,3,2,1,0:T(8,128)S(1)}, f32[2,2,12,12,48]{4,3,2,1,0:T(8,128)S(1)}, u32[]{:S(2)}, u32[]{:S(2)}) collective-permute-start(f32[2,2,12,12,48]{4,3,2,1,0:T(8,128)S(1)} %get-tuple-element.9), channel_id=1, source_target_pairs={{1,2},{3,4},{5,6},{2,1},{4,3},{6,5},{9,10},{11,12},{13,14},{10,9},... | collective-permute-start | bytes 331784 | tf_op jit(solution)/shard_map/ppermute | solution.py:19
  31.9 1.9 %collective-permute-start.3 = (f32[2,2,12,12,48]{4,3,2,1,0:T(8,128)S(1)}, f32[2,2,12,12,48]{4,3,2,1,0:T(8,128)S(1)}, u32[]{:S(2)}, u32[]{:S(2)}) collective-permute-start(f32[2,2,12,12,48]{4,3,2,1,0:T(8,128)S(1)} %get-tuple-element.10), channel_id=1, source_target_pairs={{0,1},{2,3},{4,5},{6,7},{1,0},{3,2},{5,4},{7,6},{8,9},{10,11},{12,... | collective-permute-start | bytes 331784 | tf_op jit(solution)/shard_map/ppermute | solution.py:18
  33.8 1.8 %select_reduce_fusion = (f32[224,128]{1,0:T(8,128)S(1)}, f32[224,128]{1,0:T(8,128)S(1)}) fusion(f32[70]{0:T(128)S(1)} %copy-done.1, s32[224,128]{1,0:T(8,128)S(1)} %iota_subtract_fusion, s32[70]{0:T(128)S(1)} %neg.9, f32[70]{0:T(128)S(1)} %copy-done.3, s32[70]{0:T(128)S(1)} %copy-done.2), kind=kLoop, calls=%fused_computation.1 | loop fusion | flops 11984896 | bytes 345184 | tf_op jit(solution)/shard_map/reduce_sum | solution.py:31
  35.6 1.7 %collective-permute-done.2 = f32[2,2,12,12,48]{4,3,2,1,0:T(8,128)S(1)} collective-permute-done((f32[2,2,12,12,48]{4,3,2,1,0:T(8,128)S(1)}, f32[2,2,12,12,48]{4,3,2,1,0:T(8,128)S(1)}, u32[]{:S(2)}, u32[]{:S(2)}) %collective-permute-start.2) | collective-permute-done | bytes 110624 | tf_op jit(solution)/shard_map/ppermute | solution.py:19
  37.3 0.0 collective-permute-done.3
  37.3 0.1 broadcast_select_fusion.3
  37.4 0.9 %fusion.12 = f32[2,2,12,12,128]{4,3,2,1,0:T(8,128)S(1)} fusion(f32[2,2,12,12,48]{4,3,2,1,0:T(8,128)S(1)} %get-tuple-element.8, f32[2,2,12,12,128]{4,3,2,1,0:T(8,128)S(1)} %fusion.7, f32[2,2,12,12,48]{4,3,2,1,0:T(8,128)S(1)} %get-tuple-element.7, f32[224,128]{1,0:T(8,128)S(1)} %get-tuple-element.6, f32[224,128]{1,0:T(8,128)S(1)} %get-tuple-element.5), kind=kOutput, calls=%fused_computation.9 | convolution fusion | flops 198467584 | bytes 1040384 | tf_op jit(solution)/shard_map/dot_general | solution.py:67
  38.3 0.9 %copy.25 = f32[2,2,12,12,128]{4,1,3,2,0:T(2,128)} copy(f32[2,2,12,12,128]{4,3,2,1,0:T(8,128)S(1)} %fusion.12) | data formatting | bytes 589824 | tf_op jit(solution)/shard_map/dot_general | solution.py:67
  (11 shorter events, 0.1 us)
Async XLA Ops:
  0.0 19.5 %copy-start = (s32[2,34]{1,0:T(2,128)S(1)}, s32[2,34]{1,0:T(2,128)}, u32[]{:S(2)}) copy-start(s32[2,34]{1,0:T(2,128)} %param.8) | copy-start | bytes 820
  0.0 19.5 %copy-start.2 = (s32[70]{0:T(128)S(1)}, s32[70]{0:T(128)}, u32[]{:S(2)}) copy-start(s32[70]{0:T(128)} %param.9) | copy-start | bytes 844
  1.0 20.0 %collective-permute-start = (bf16[2,2,12,12,128]{4,2,0,1,3:T(8,128)(2,1)S(1)}, bf16[2,2,12,12,128]{4,2,0,1,3:T(8,128)(2,1)S(1)}, u32[]{:S(2)}, u32[]{:S(2)}) collective-permute-start(bf16[2,2,12,12,128]{4,2,0,1,3:T(8,128)(2,1)S(1)} %copy.21), channel_id=1, source_target_pairs={{8,16},{24,32},{40,48},{56,64},{72,80},{88,96},{104,112},{120,128}... | collective-permute-start | bytes 442376 | tf_op jit(solution)/shard_map/ppermute | solution.py:19
  16.1 7.4 %collective-permute-start.1 = (bf16[2,2,12,12,128]{4,2,0,1,3:T(8,128)(2,1)S(1)}, bf16[2,2,12,12,128]{4,2,0,1,3:T(8,128)(2,1)S(1)}, u32[]{:S(2)}, u32[]{:S(2)}) collective-permute-start(bf16[2,2,12,12,128]{4,2,0,1,3:T(8,128)(2,1)S(1)} %copy.21), channel_id=1, source_target_pairs={{0,8},{16,24},{32,40},{48,56},{64,72},{80,88},{96,104},{112,120},{... | collective-permute-start | bytes 442376 | tf_op jit(solution)/shard_map/ppermute | solution.py:18
  23.5 10.3 %copy-start.1 = (f32[70]{0:T(128)S(1)}, f32[70]{0:T(128)}, u32[]{:S(2)}) copy-start(f32[70]{0:T(128)} %param.11) | copy-start | bytes 844
  23.5 10.3 %copy-start.3 = (f32[70]{0:T(128)S(1)}, f32[70]{0:T(128)}, u32[]{:S(2)}) copy-start(f32[70]{0:T(128)} %param.10) | copy-start | bytes 844
  27.1 10.3 %collective-permute-start.2 = (f32[2,2,12,12,48]{4,3,2,1,0:T(8,128)S(1)}, f32[2,2,12,12,48]{4,3,2,1,0:T(8,128)S(1)}, u32[]{:S(2)}, u32[]{:S(2)}) collective-permute-start(f32[2,2,12,12,48]{4,3,2,1,0:T(8,128)S(1)} %get-tuple-element.9), channel_id=1, source_target_pairs={{1,2},{3,4},{5,6},{2,1},{4,3},{6,5},{9,10},{11,12},{13,14},{10,9},... | collective-permute-start | bytes 331784 | tf_op jit(solution)/shard_map/ppermute | solution.py:19
  31.9 5.4 %collective-permute-start.3 = (f32[2,2,12,12,48]{4,3,2,1,0:T(8,128)S(1)}, f32[2,2,12,12,48]{4,3,2,1,0:T(8,128)S(1)}, u32[]{:S(2)}, u32[]{:S(2)}) collective-permute-start(f32[2,2,12,12,48]{4,3,2,1,0:T(8,128)S(1)} %get-tuple-element.10), channel_id=1, source_target_pairs={{0,1},{2,3},{4,5},{6,7},{1,0},{3,2},{5,4},{7,6},{8,9},{10,11},{12,... | collective-permute-start | bytes 331784 | tf_op jit(solution)/shard_map/ppermute | solution.py:18

commit v3 on v2

--- a/solution.py
+++ b/solution.py
@@ -52,9 +52,10 @@
     atoms_here = green.shape[0]
     points = green.shape[-1]
     reach = points * 3 // 8
-    window = extended(green, (("atom", 0),), atoms_here)
+    window = extended(green, (("energy", 4),), reach)
+    window = extended(window, (("atom", 0),), atoms_here)
     local_ids = neighbours - (lax.axis_index("atom") - 1) * atoms_here
-    coupled = coupled_blocks(window, coupling, local_ids)
+    widened = coupled_blocks(window, coupling, local_ids)
 
     extent = points + 2 * reach
     spread_diff = (
@@ -63,11 +64,10 @@
         - jnp.arange(points, dtype=jnp.int32)[None, :]
     )
     kernel = make_kernel(spread_diff, offsets, w_emit, w_absorb)
-    widened = extended(coupled, (("energy", 4),), reach)
     result = jnp.dot(
         widened.reshape(-1, extent), kernel, precision=hi, preferred_element_type=jnp.float32
     )
-    return result.reshape(coupled.shape)
+    return result.reshape(widened.shape[:-1] + (points,))
 
 
 def solution(mesh):

time: 39.7 us -> 46.3 us (1.17)
  the two profiles are of different devices: /device:TPU:57 before, /device:TPU:58 now
where the time goes in v3:
time: 46.3 us; the launch traced here: 46.1 us
  starting transfers between devices  22.7 us (49%)
  waiting for transfers between devices  8.89 us (19%)
  matrix products  7.2 us (16%)
  other arithmetic  3.91 us (8%)
  local copies, waits for them, and re-layouts  3.1 us (7%)
    ppermute x2, starting transfers between devices, extended(): from_odd = lax.ppermute(jnp.where(even, head, tail), axis, edges[1])  17.3 us
    ppermute x2, waiting for transfers between devices, extended(): from_odd = lax.ppermute(jnp.where(even, head, tail), axis, edges[1])  5.51 us
    ppermute x2, starting transfers between devices, extended(): from_even = lax.ppermute(jnp.where(even, tail, head), axis, edges[0])  5.42 us
    dot_general x1, matrix products, coupled_blocks(): jnp.einsum('akqwpij,wpjle->akqile', left, window, preferred_element_type=...  4.11 us
    ppermute x2, waiting for transfers between devices, extended(): from_even = lax.ppermute(jnp.where(even, tail, head), axis, edges[0])  3.37 us
    dot_general x1, matrix products, coupled_blocks(): jnp.einsum('akplie,akqpml->aqime', x, right, preferred_element_type=f32)  2.3 us
    unnamed x10, local copies, waits for them, and re-layouts  1.93 us
    reduce_sum x1, other arithmetic, make_kernel(): jnp.sum(jnp.where(spread_diff[:, :, None] == -offsets, w_absorb, jnp.floa...  1.81 us
  transfers between devices with their start and end apart: 4, of which 2 were waited for; matrix products, arithmetic and copies ran while one was open for 10% of the time, Pallas kernels for 0%

profile of v3, /device:TPU:58, one launch (start us, length us, event | category | flops | bytes accessed | tf_op | source)
XLA Modules:
  0.0 46.1 jit_solution(17403796166392334008)
XLA Ops:
  0.0 1.0 %copy.15 = bf16[2,2,12,12,128]{4,2,0,1,3:T(8,128)(2,1)S(1)} copy(bf16[2,2,12,12,128]{4,1,3,2,0:T(2,128)(2,1)} %param.6) | data formatting | bytes 294912 | tf_op args[0]
  1.0 0.1 broadcast_select_fusion.5
  1.1 1.9 %collective-permute-start = (bf16[2,2,12,12,48]{4,2,0,1,3:T(8,128)(2,1)S(1)}, bf16[2,2,12,12,48]{4,2,0,1,3:T(8,128)(2,1)S(1)}, u32[]{:S(2)}, u32[]{:S(2)}) collective-permute-start(bf16[2,2,12,12,48]{4,2,0,1,3:T(8,128)(2,1)S(1)} %get-tuple-element.13), channel_id=1, source_target_pairs={{1,2},{3,4},{5,6},{2,1},{4,3},{6,5},{9,10},{11,12},{13,14},{10,9},... | collective-permute-start | bytes 165896 | tf_op jit(solution)/shard_map/ppermute | solution.py:19
  3.0 3.5 %collective-permute-start.1 = (bf16[2,2,12,12,48]{4,2,0,1,3:T(8,128)(2,1)S(1)}, bf16[2,2,12,12,48]{4,2,0,1,3:T(8,128)(2,1)S(1)}, u32[]{:S(2)}, u32[]{:S(2)}) collective-permute-start(bf16[2,2,12,12,48]{4,2,0,1,3:T(8,128)(2,1)S(1)} %get-tuple-element.14), channel_id=1, source_target_pairs={{0,1},{2,3},{4,5},{6,7},{1,0},{3,2},{5,4},{7,6},{8,9},{10,11},{12,... | collective-permute-start | bytes 165896 | tf_op jit(solution)/shard_map/ppermute | solution.py:18
  6.6 0.9 %copy.40 = bf16[2,34,2,12,12]{1,3,2,4,0:T(8,128)(2,1)S(1)} copy(bf16[2,34,2,12,12]{1,2,4,3,0:T(2,128)(2,1)} %param.7) | data formatting | bytes 78336 | tf_op args[1]
  7.5 0.0 copy-start.2
  7.6 0.1 fusion.17
  7.6 0.1 pad_maximum_fusion
  7.7 0.0 copy-start.1
  7.8 0.0 copy-start.3
  7.8 0.2 copy.14
  8.0 1.3 %multiply_bitcast_fusion = bf16[2,34,2,6,2,12,12,1]{1,4,6,5,3,2,0,7:T(2,128)(2,1)S(1)} fusion(bf16[2,34,6]{1,2,0:T(8,128)(2,1)S(1)} %fusion.22, bf16[2,34,2,2,12,12]{1,3,5,4,2,0:T(2,128)(2,1)S(1)} %copy.14), kind=kLoop, calls=%fused_computation.7 | loop fusion | flops 235008 | bytes 549168 | tf_op jit(solution)/shard_map/mul | solution.py:43
  9.4 0.1 iota_subtract_fusion
  9.6 0.3 pad_maximum_fusion.1
  9.8 15.4 %collective-permute-start.2 = (bf16[2,2,12,12,224]{4,2,0,1,3:T(8,128)(2,1)S(1)}, bf16[2,2,12,12,224]{4,2,0,1,3:T(8,128)(2,1)S(1)}, u32[]{:S(2)}, u32[]{:S(2)}) collective-permute-start(bf16[2,2,12,12,224]{4,2,0,1,3:T(8,128)(2,1)S(1)} %pad_maximum_fusion.1), channel_id=1, source_target_pairs={{8,16},{24,32},{40,48},{56,64},{72,80},{88,96},{104,112},{120,128}... | collective-permute-start | bytes 774152 | tf_op jit(solution)/shard_map/ppermute | solution.py:19
  25.2 1.9 %collective-permute-start.3 = (bf16[2,2,12,12,224]{4,2,0,1,3:T(8,128)(2,1)S(1)}, bf16[2,2,12,12,224]{4,2,0,1,3:T(8,128)(2,1)S(1)}, u32[]{:S(2)}, u32[]{:S(2)}) collective-permute-start(bf16[2,2,12,12,224]{4,2,0,1,3:T(8,128)(2,1)S(1)} %pad_maximum_fusion.1), channel_id=1, source_target_pairs={{0,8},{16,24},{32,40},{48,56},{64,72},{80,88},{96,104},{112,120},{... | collective-permute-start | bytes 774152 | tf_op jit(solution)/shard_map/ppermute | solution.py:18
  27.2 1.8 %select_reduce_fusion = (f32[224,128]{1,0:T(8,128)S(1)}, f32[224,128]{1,0:T(8,128)S(1)}) fusion(f32[70]{0:T(128)S(1)} %copy-done.1, s32[224,128]{1,0:T(8,128)S(1)} %iota_subtract_fusion, s32[70]{0:T(128)S(1)} %neg.9, f32[70]{0:T(128)S(1)} %copy-done.3, s32[70]{0:T(128)S(1)} %copy-done.2), kind=kLoop, calls=%fused_computation.4 | loop fusion | flops 11984896 | bytes 345184 | tf_op jit(solution)/shard_map/reduce_sum | solution.py:31
  29.0 5.5 %collective-permute-done.2 = bf16[2,2,12,12,224]{4,2,0,1,3:T(8,128)(2,1)S(1)} collective-permute-done((bf16[2,2,12,12,224]{4,2,0,1,3:T(8,128)(2,1)S(1)}, bf16[2,2,12,12,224]{4,2,0,1,3:T(8,128)(2,1)S(1)}, u32[]{:S(2)}, u32[]{:S(2)}) %collective-permute-start.2) | collective-permute-done | bytes 258080 | tf_op jit(solution)/shard_map/ppermute | solution.py:19
  34.5 3.4 %collective-permute-done.3 = bf16[2,2,12,12,224]{4,2,0,1,3:T(8,128)(2,1)S(1)} collective-permute-done((bf16[2,2,12,12,224]{4,2,0,1,3:T(8,128)(2,1)S(1)}, bf16[2,2,12,12,224]{4,2,0,1,3:T(8,128)(2,1)S(1)}, u32[]{:S(2)}, u32[]{:S(2)}) %collective-permute-start.3) | collective-permute-done | bytes 258080 | tf_op jit(solution)/shard_map/ppermute | solution.py:18
  37.9 0.1 broadcast_select_fusion.1
  37.9 4.1 %fusion = bf16[2,34,2,12,12,224,1]{5,1,3,4,2,0,6:T(8,128)(2,1)S(1)} fusion(bf16[2,34,2,6,2,12,12,1]{1,4,6,5,3,2,0,7:T(2,128)(2,1)S(1)} %multiply_bitcast_fusion, bf16[2,2,12,12,224]{4,2,0,1,3:T(8,128)(2,1)S(1)} %get-tuple-element.8, bf16[2,2,12,12,48]{4,2,0,1,3:T(8,128)(2,1)S(1)} %get-tuple-element.10, bf16[2,2,12,12,128]{4,2,0,1,3:T(8,128)(2,1)S(1)} %copy.15, ...), kind=kOutput, calls=%fused_computation.1 | convolution fusion | flops 1271660544 | bytes 10017792 | tf_op jit(solution)/shard_map/akqwpij,wpjle->akqile/dot_general | solution.py:44
  42.0 2.3 %fusion.4 = f32[2,2,12,12,224]{4,3,2,1,0:T(8,128)S(1)} fusion(bf16[2,34,2,12,12,224,1]{5,1,3,4,2,0,6:T(8,128)(2,1)S(1)} %fusion, bf16[2,34,1,2,12,12]{1,4,3,5,2,0:T(8,128)(2,1)S(1)} %get-tuple-element.11, bf16[2,34,1,2,12,12]{1,4,3,5,2,0:T(8,128)(2,1)S(1)} %bitcast.43), kind=kOutput, calls=%fused_computation.8 | convolution fusion | flops 210723840 | bytes 9368064 | tf_op jit(solution)/shard_map/akplie,akqpml->aqime/dot_general | solution.py:47
  44.3 0.8 %fusion.19 = f32[2,2,12,12,128]{4,3,2,1,0:T(8,128)S(1)} fusion(f32[2,2,12,12,224]{4,3,2,1,0:T(8,128)S(1)} %fusion.4, f32[224,128]{1,0:T(8,128)S(1)} %get-tuple-element.6, f32[224,128]{1,0:T(8,128)S(1)} %get-tuple-element.5), kind=kOutput, calls=%fused_computation.34 | convolution fusion | flops 198209536 | bytes 1040384 | tf_op jit(solution)/shard_map/dot_general | solution.py:67
  45.1 0.9 %copy.20 = f32[2,2,12,12,128]{4,1,3,2,0:T(2,128)} copy(f32[2,2,12,12,128]{4,3,2,1,0:T(8,128)S(1)} %fusion.19) | data formatting | bytes 589824 | tf_op jit(solution)/shard_map/dot_general | solution.py:67
  (13 shorter events, 0.1 us)
Async XLA Ops:
  0.0 8.0 %copy-start = (s32[2,34]{1,0:T(2,128)S(1)}, s32[2,34]{1,0:T(2,128)}, u32[]{:S(2)}) copy-start(s32[2,34]{1,0:T(2,128)} %param.8) | copy-start | bytes 820
  1.1 8.4 %collective-permute-start = (bf16[2,2,12,12,48]{4,2,0,1,3:T(8,128)(2,1)S(1)}, bf16[2,2,12,12,48]{4,2,0,1,3:T(8,128)(2,1)S(1)}, u32[]{:S(2)}, u32[]{:S(2)}) collective-permute-start(bf16[2,2,12,12,48]{4,2,0,1,3:T(8,128)(2,1)S(1)} %get-tuple-element.13), channel_id=1, source_target_pairs={{1,2},{3,4},{5,6},{2,1},{4,3},{6,5},{9,10},{11,12},{13,14},{10,9},... | collective-permute-start | bytes 165896 | tf_op jit(solution)/shard_map/ppermute | solution.py:19
  3.0 6.5 %collective-permute-start.1 = (bf16[2,2,12,12,48]{4,2,0,1,3:T(8,128)(2,1)S(1)}, bf16[2,2,12,12,48]{4,2,0,1,3:T(8,128)(2,1)S(1)}, u32[]{:S(2)}, u32[]{:S(2)}) collective-permute-start(bf16[2,2,12,12,48]{4,2,0,1,3:T(8,128)(2,1)S(1)} %get-tuple-element.14), channel_id=1, source_target_pairs={{0,1},{2,3},{4,5},{6,7},{1,0},{3,2},{5,4},{7,6},{8,9},{10,11},{12,... | collective-permute-start | bytes 165896 | tf_op jit(solution)/shard_map/ppermute | solution.py:18
  7.5 1.9 %copy-start.2 = (s32[70]{0:T(128)S(1)}, s32[70]{0:T(128)}, u32[]{:S(2)}) copy-start(s32[70]{0:T(128)} %param.9) | copy-start | bytes 844
  7.7 19.4 %copy-start.1 = (f32[70]{0:T(128)S(1)}, f32[70]{0:T(128)}, u32[]{:S(2)}) copy-start(f32[70]{0:T(128)} %param.11) | copy-start | bytes 844
  7.8 19.4 %copy-start.3 = (f32[70]{0:T(128)S(1)}, f32[70]{0:T(128)}, u32[]{:S(2)}) copy-start(f32[70]{0:T(128)} %param.10) | copy-start | bytes 844
  9.8 24.7 %collective-permute-start.2 = (bf16[2,2,12,12,224]{4,2,0,1,3:T(8,128)(2,1)S(1)}, bf16[2,2,12,12,224]{4,2,0,1,3:T(8,128)(2,1)S(1)}, u32[]{:S(2)}, u32[]{:S(2)}) collective-permute-start(bf16[2,2,12,12,224]{4,2,0,1,3:T(8,128)(2,1)S(1)} %pad_maximum_fusion.1), channel_id=1, source_target_pairs={{8,16},{24,32},{40,48},{56,64},{72,80},{88,96},{104,112},{120,128}... | collective-permute-start | bytes 774152 | tf_op jit(solution)/shard_map/ppermute | solution.py:19
  25.2 12.6 %collective-permute-start.3 = (bf16[2,2,12,12,224]{4,2,0,1,3:T(8,128)(2,1)S(1)}, bf16[2,2,12,12,224]{4,2,0,1,3:T(8,128)(2,1)S(1)}, u32[]{:S(2)}, u32[]{:S(2)}) collective-permute-start(bf16[2,2,12,12,224]{4,2,0,1,3:T(8,128)(2,1)S(1)} %pad_maximum_fusion.1), channel_id=1, source_target_pairs={{0,8},{16,24},{32,40},{48,56},{64,72},{80,88},{96,104},{112,120},{... | collective-permute-start | bytes 774152 | tf_op jit(solution)/shard_map/ppermute | solution.py:18

commit v4 on v2

--- a/solution.py
+++ b/solution.py
@@ -54,8 +54,6 @@
     reach = points * 3 // 8
     window = extended(green, (("atom", 0),), atoms_here)
     local_ids = neighbours - (lax.axis_index("atom") - 1) * atoms_here
-    coupled = coupled_blocks(window, coupling, local_ids)
-
     extent = points + 2 * reach
     spread_diff = (
         jnp.arange(extent, dtype=jnp.int32)[:, None]
@@ -63,6 +61,8 @@
         - jnp.arange(points, dtype=jnp.int32)[None, :]
     )
     kernel = make_kernel(spread_diff, offsets, w_emit, w_absorb)
+    coupled = coupled_blocks(window, coupling, local_ids)
+    coupled, kernel = lax.optimization_barrier((coupled, kernel))
     widened = extended(coupled, (("energy", 4),), reach)
     result = jnp.dot(
         widened.reshape(-1, extent), kernel, precision=hi, preferred_element_type=jnp.float32

time: 39.7 us -> 39.7 us (level)
    ppermute x2, waiting for transfers between devices: 2.52 us -> 0.63 us  [extended(): from_even = lax.ppermute(jnp.where(even, tail, head), axis, edges[0])]
    ppermute x2, waiting for transfers between devices: 1.68 us -> 3.52 us  [extended(): from_odd = lax.ppermute(jnp.where(even, head, tail), axis, edges[1])]
where the time goes in v4:
time: 39.7 us; the launch traced here: 39.2 us
  starting transfers between devices  23.7 us (60%)
  matrix products  4.24 us (11%)
  waiting for transfers between devices  4.15 us (10%)
  other arithmetic  3.72 us (9%)
  local copies, waits for them, and re-layouts  3.11 us (8%)
    ppermute x2, starting transfers between devices, extended(): from_odd = lax.ppermute(jnp.where(even, head, tail), axis, edges[1])  19.9 us
    ppermute x2, starting transfers between devices, extended(): from_even = lax.ppermute(jnp.where(even, tail, head), axis, edges[0])  3.84 us
    ppermute x2, waiting for transfers between devices, extended(): from_odd = lax.ppermute(jnp.where(even, head, tail), axis, edges[1])  3.52 us
    dot_general x1, matrix products, coupled_blocks(): jnp.einsum('akplie,akqpml->aqime', x, right, preferred_element_type=f32)  3.33 us
    unnamed x10, local copies, waits for them, and re-layouts  1.94 us
    reduce_sum x1, other arithmetic, make_kernel(): jnp.sum(jnp.where(spread_diff[:, :, None] == -offsets, w_absorb, jnp.floa...  1.82 us
    mul x1, other arithmetic, coupled_blocks(): left = mbig[:, :, :, None] * onehot[:, :, None, :, None, None, None]  1.31 us
    dot_general x1, local copies, waits for them, and re-layouts, shards(): jnp.dot(widened.reshape(-1, extent), kernel, precision=hi, preferred_elem...  0.94 us
  transfers between devices with their start and end apart: 4, of which 2 were waited for; matrix products, arithmetic and copies ran while one was open for 12% of the time, Pallas kernels for 0%

profile of v4, /device:TPU:57, one launch (start us, length us, event | category | flops | bytes accessed | tf_op | source)
XLA Modules:
  0.0 39.2 jit_solution(11950514595946075578)
XLA Ops:
  0.0 1.0 %copy.21 = bf16[2,2,12,12,128]{4,2,0,1,3:T(8,128)(2,1)S(1)} copy(bf16[2,2,12,12,128]{4,1,3,2,0:T(2,128)(2,1)} %param.6) | data formatting | bytes 294912 | tf_op args[0]
  1.0 15.1 %collective-permute-start = (bf16[2,2,12,12,128]{4,2,0,1,3:T(8,128)(2,1)S(1)}, bf16[2,2,12,12,128]{4,2,0,1,3:T(8,128)(2,1)S(1)}, u32[]{:S(2)}, u32[]{:S(2)}) collective-permute-start(bf16[2,2,12,12,128]{4,2,0,1,3:T(8,128)(2,1)S(1)} %copy.21), channel_id=1, source_target_pairs={{8,16},{24,32},{40,48},{56,64},{72,80},{88,96},{104,112},{120,128}... | collective-permute-start | bytes 442376 | tf_op jit(solution)/shard_map/ppermute | solution.py:19
  16.1 1.9 %collective-permute-start.1 = (bf16[2,2,12,12,128]{4,2,0,1,3:T(8,128)(2,1)S(1)}, bf16[2,2,12,12,128]{4,2,0,1,3:T(8,128)(2,1)S(1)}, u32[]{:S(2)}, u32[]{:S(2)}) collective-permute-start(bf16[2,2,12,12,128]{4,2,0,1,3:T(8,128)(2,1)S(1)} %copy.21), channel_id=1, source_target_pairs={{0,8},{16,24},{32,40},{48,56},{64,72},{80,88},{96,104},{112,120},{... | collective-permute-start | bytes 442376 | tf_op jit(solution)/shard_map/ppermute | solution.py:18
  18.0 0.9 %copy.42 = bf16[2,34,2,12,12]{1,3,2,4,0:T(8,128)(2,1)S(1)} copy(bf16[2,34,2,12,12]{1,2,4,3,0:T(2,128)(2,1)} %param.7) | data formatting | bytes 78336 | tf_op args[1]
  19.0 0.1 fusion.28
  19.1 0.0 copy-start.1
  19.1 0.0 copy-start.3
  19.1 0.1 pad_maximum_fusion
  19.2 0.2 copy.20
  19.5 0.1 iota_subtract_fusion
  19.6 1.3 %multiply_bitcast_fusion = bf16[2,34,2,6,2,12,12,1]{1,4,6,5,3,2,0,7:T(2,128)(2,1)S(1)} fusion(bf16[2,34,6]{1,2,0:T(8,128)(2,1)S(1)} %fusion.31, bf16[2,34,2,2,12,12]{1,3,5,4,2,0:T(2,128)(2,1)S(1)} %copy.20), kind=kLoop, calls=%fused_computation.7 | loop fusion | flops 235008 | bytes 549168 | tf_op jit(solution)/shard_map/mul | solution.py:43
  21.0 0.0 copy-done.1
  21.0 1.8 %select_reduce_fusion = (f32[224,128]{1,0:T(8,128)S(1)}, f32[224,128]{1,0:T(8,128)S(1)}) fusion(f32[70]{0:T(128)S(1)} %copy-done.1, s32[224,128]{1,0:T(8,128)S(1)} %iota_subtract_fusion, s32[70]{0:T(128)S(1)} %neg.9, f32[70]{0:T(128)S(1)} %copy-done.3, s32[70]{0:T(128)S(1)} %copy-done.2), kind=kLoop, calls=%fused_computation.1 | loop fusion | flops 11984896 | bytes 345184 | tf_op jit(solution)/shard_map/reduce_sum | solution.py:31
  22.8 0.0 collective-permute-done
  22.9 0.6 %collective-permute-done.1 = bf16[2,2,12,12,128]{4,2,0,1,3:T(8,128)(2,1)S(1)} collective-permute-done((bf16[2,2,12,12,128]{4,2,0,1,3:T(8,128)(2,1)S(1)}, bf16[2,2,12,12,128]{4,2,0,1,3:T(8,128)(2,1)S(1)}, u32[]{:S(2)}, u32[]{:S(2)}) %collective-permute-start.1) | collective-permute-done | bytes 147488 | tf_op jit(solution)/shard_map/ppermute | solution.py:18
  23.5 3.3 %fusion.7 = f32[2,2,12,12,128]{4,3,2,1,0:T(8,128)S(1)} fusion(bf16[2,34,2,6,2,12,12,1]{1,4,6,5,3,2,0,7:T(2,128)(2,1)S(1)} %multiply_bitcast_fusion, bf16[2,2,12,12,128]{4,2,0,1,3:T(8,128)(2,1)S(1)} %get-tuple-element.16, bf16[2,2,12,12,128]{4,2,0,1,3:T(8,128)(2,1)S(1)} %copy.21, bf16[2,2,12,12,128]{4,2,0,1,3:T(8,128)(2,1)S(1)} %get-tuple-element.15, ...), kind=kOutput, calls=%fused_computation.8 | convolution fusion | flops 846259200 | bytes 1285632 | tf_op jit(solution)/shard_map/akplie,akqpml->aqime/dot_general | solution.py:47
  26.9 0.2 slice_select_fusion.1
  27.0 4.8 %collective-permute-start.2 = (f32[2,2,12,12,48]{4,3,2,1,0:T(8,128)S(1)}, f32[2,2,12,12,48]{4,3,2,1,0:T(8,128)S(1)}, u32[]{:S(2)}, u32[]{:S(2)}) collective-permute-start(f32[2,2,12,12,48]{4,3,2,1,0:T(8,128)S(1)} %get-tuple-element.13), channel_id=1, source_target_pairs={{1,2},{3,4},{5,6},{2,1},{4,3},{6,5},{9,10},{11,12},{13,14},{10,9},... | collective-permute-start | bytes 331784 | tf_op jit(solution)/shard_map/ppermute | solution.py:19
  31.8 1.9 %collective-permute-start.3 = (f32[2,2,12,12,48]{4,3,2,1,0:T(8,128)S(1)}, f32[2,2,12,12,48]{4,3,2,1,0:T(8,128)S(1)}, u32[]{:S(2)}, u32[]{:S(2)}) collective-permute-start(f32[2,2,12,12,48]{4,3,2,1,0:T(8,128)S(1)} %get-tuple-element.14), channel_id=1, source_target_pairs={{0,1},{2,3},{4,5},{6,7},{1,0},{3,2},{5,4},{7,6},{8,9},{10,11},{12,... | collective-permute-start | bytes 331784 | tf_op jit(solution)/shard_map/ppermute | solution.py:18
  33.8 3.5 %collective-permute-done.2 = f32[2,2,12,12,48]{4,3,2,1,0:T(8,128)S(1)} collective-permute-done((f32[2,2,12,12,48]{4,3,2,1,0:T(8,128)S(1)}, f32[2,2,12,12,48]{4,3,2,1,0:T(8,128)S(1)}, u32[]{:S(2)}, u32[]{:S(2)}) %collective-permute-start.2) | collective-permute-done | bytes 110624 | tf_op jit(solution)/shard_map/ppermute | solution.py:19
  37.3 0.0 collective-permute-done.3
  37.3 0.1 broadcast_select_fusion.3
  37.4 0.9 %fusion.12 = f32[2,2,12,12,128]{4,3,2,1,0:T(8,128)S(1)} fusion(f32[2,2,12,12,48]{4,3,2,1,0:T(8,128)S(1)} %get-tuple-element.12, f32[2,2,12,12,128]{4,3,2,1,0:T(8,128)S(1)} %fusion.7, f32[2,2,12,12,48]{4,3,2,1,0:T(8,128)S(1)} %get-tuple-element.11, f32[224,128]{1,0:T(8,128)S(1)} %add.19), kind=kOutput, calls=%fused_computation.9 | convolution fusion | flops 198438912 | bytes 925696 | tf_op jit(solution)/shard_map/dot_general | solution.py:67
  38.3 0.9 %copy.25 = f32[2,2,12,12,128]{4,1,3,2,0:T(2,128)} copy(f32[2,2,12,12,128]{4,3,2,1,0:T(8,128)S(1)} %fusion.12) | data formatting | bytes 589824 | tf_op jit(solution)/shard_map/dot_general | solution.py:67
  (12 shorter events, 0.1 us)
Async XLA Ops:
  0.0 19.5 %copy-start = (s32[2,34]{1,0:T(2,128)S(1)}, s32[2,34]{1,0:T(2,128)}, u32[]{:S(2)}) copy-start(s32[2,34]{1,0:T(2,128)} %param.8) | copy-start | bytes 820
  0.0 19.6 %copy-start.2 = (s32[70]{0:T(128)S(1)}, s32[70]{0:T(128)}, u32[]{:S(2)}) copy-start(s32[70]{0:T(128)} %param.9) | copy-start | bytes 844
  1.0 21.9 %collective-permute-start = (bf16[2,2,12,12,128]{4,2,0,1,3:T(8,128)(2,1)S(1)}, bf16[2,2,12,12,128]{4,2,0,1,3:T(8,128)(2,1)S(1)}, u32[]{:S(2)}, u32[]{:S(2)}) collective-permute-start(bf16[2,2,12,12,128]{4,2,0,1,3:T(8,128)(2,1)S(1)} %copy.21), channel_id=1, source_target_pairs={{8,16},{24,32},{40,48},{56,64},{72,80},{88,96},{104,112},{120,128}... | collective-permute-start | bytes 442376 | tf_op jit(solution)/shard_map/ppermute | solution.py:19
  16.1 7.4 %collective-permute-start.1 = (bf16[2,2,12,12,128]{4,2,0,1,3:T(8,128)(2,1)S(1)}, bf16[2,2,12,12,128]{4,2,0,1,3:T(8,128)(2,1)S(1)}, u32[]{:S(2)}, u32[]{:S(2)}) collective-permute-start(bf16[2,2,12,12,128]{4,2,0,1,3:T(8,128)(2,1)S(1)} %copy.21), channel_id=1, source_target_pairs={{0,8},{16,24},{32,40},{48,56},{64,72},{80,88},{96,104},{112,120},{... | collective-permute-start | bytes 442376 | tf_op jit(solution)/shard_map/ppermute | solution.py:18
  19.1 1.9 %copy-start.1 = (f32[70]{0:T(128)S(1)}, f32[70]{0:T(128)}, u32[]{:S(2)}) copy-start(f32[70]{0:T(128)} %param.11) | copy-start | bytes 844
  19.1 1.9 %copy-start.3 = (f32[70]{0:T(128)S(1)}, f32[70]{0:T(128)}, u32[]{:S(2)}) copy-start(f32[70]{0:T(128)} %param.10) | copy-start | bytes 844
  27.0 10.3 %collective-permute-start.2 = (f32[2,2,12,12,48]{4,3,2,1,0:T(8,128)S(1)}, f32[2,2,12,12,48]{4,3,2,1,0:T(8,128)S(1)}, u32[]{:S(2)}, u32[]{:S(2)}) collective-permute-start(f32[2,2,12,12,48]{4,3,2,1,0:T(8,128)S(1)} %get-tuple-element.13), channel_id=1, source_target_pairs={{1,2},{3,4},{5,6},{2,1},{4,3},{6,5},{9,10},{11,12},{13,14},{10,9},... | collective-permute-start | bytes 331784 | tf_op jit(solution)/shard_map/ppermute | solution.py:19
  31.8 5.4 %collective-permute-start.3 = (f32[2,2,12,12,48]{4,3,2,1,0:T(8,128)S(1)}, f32[2,2,12,12,48]{4,3,2,1,0:T(8,128)S(1)}, u32[]{:S(2)}, u32[]{:S(2)}) collective-permute-start(f32[2,2,12,12,48]{4,3,2,1,0:T(8,128)S(1)} %get-tuple-element.14), channel_id=1, source_target_pairs={{0,1},{2,3},{4,5},{6,7},{1,0},{3,2},{5,4},{7,6},{8,9},{10,11},{12,... | collective-permute-start | bytes 331784 | tf_op jit(solution)/shard_map/ppermute | solution.py:18

commit v5 on v4

--- a/solution.py
+++ b/solution.py
@@ -63,7 +63,15 @@
     kernel = make_kernel(spread_diff, offsets, w_emit, w_absorb)
     coupled = coupled_blocks(window, coupling, local_ids)
     coupled, kernel = lax.optimization_barrier((coupled, kernel))
-    widened = extended(coupled, (("energy", 4),), reach)
+    halo = extended(coupled.astype(jnp.bfloat16), (("energy", 4),), reach)
+    widened = jnp.concatenate(
+        [
+            lax.slice_in_dim(halo, 0, reach, axis=4).astype(jnp.float32),
+            coupled,
+            lax.slice_in_dim(halo, halo.shape[4] - reach, halo.shape[4], axis=4).astype(jnp.float32),
+        ],
+        axis=4,
+    )
     result = jnp.dot(
         widened.reshape(-1, extent), kernel, precision=hi, preferred_element_type=jnp.float32
     )

time: 39.7 us -> 37.6 us (0.947)
  waiting for transfers between devices: 4.15 us -> 2.04 us
    ppermute x2, waiting for transfers between devices: 3.52 us -> 1.41 us  [extended(): from_odd = lax.ppermute(jnp.where(even, head, tail), axis, edges[1])]
where the time goes in v5:
time: 37.6 us; the launch traced here: 37.1 us
  starting transfers between devices  23.7 us (63%)
  matrix products  4.24 us (11%)
  other arithmetic  3.7 us (10%)
  local copies, waits for them, and re-layouts  3.11 us (8%)
  waiting for transfers between devices  2.04 us (5%)
    ppermute x2, starting transfers between devices, extended(): from_odd = lax.ppermute(jnp.where(even, head, tail), axis, edges[1])  19.9 us
    ppermute x2, starting transfers between devices, extended(): from_even = lax.ppermute(jnp.where(even, tail, head), axis, edges[0])  3.84 us
    dot_general x1, matrix products, coupled_blocks(): jnp.einsum('akplie,akqpml->aqime', x, right, preferred_element_type=f32)  3.33 us
    unnamed x10, local copies, waits for them, and re-layouts  1.94 us
    reduce_sum x1, other arithmetic, make_kernel(): jnp.sum(jnp.where(spread_diff[:, :, None] == -offsets, w_absorb, jnp.floa...  1.82 us
    ppermute x2, waiting for transfers between devices, extended(): from_odd = lax.ppermute(jnp.where(even, head, tail), axis, edges[1])  1.41 us
    mul x1, other arithmetic, coupled_blocks(): left = mbig[:, :, :, None] * onehot[:, :, None, :, None, None, None]  1.31 us
    dot_general x1, local copies, waits for them, and re-layouts, shards(): jnp.dot(widened.reshape(-1, extent), kernel, precision=hi, preferred_elem...  0.94 us
  transfers between devices with their start and end apart: 4, of which 2 were waited for; matrix products, arithmetic and copies ran while one was open for 12% of the time, Pallas kernels for 0%

profile of v5, /device:TPU:57, one launch (start us, length us, event | category | flops | bytes accessed | tf_op | source)
XLA Modules:
  0.0 37.1 jit_solution(13538057004537527713)
XLA Ops:
  0.0 1.0 %copy.21 = bf16[2,2,12,12,128]{4,2,0,1,3:T(8,128)(2,1)S(1)} copy(bf16[2,2,12,12,128]{4,1,3,2,0:T(2,128)(2,1)} %param.6) | data formatting | bytes 294912 | tf_op args[0]
  1.0 15.1 %collective-permute-start = (bf16[2,2,12,12,128]{4,2,0,1,3:T(8,128)(2,1)S(1)}, bf16[2,2,12,12,128]{4,2,0,1,3:T(8,128)(2,1)S(1)}, u32[]{:S(2)}, u32[]{:S(2)}) collective-permute-start(bf16[2,2,12,12,128]{4,2,0,1,3:T(8,128)(2,1)S(1)} %copy.21), channel_id=1, source_target_pairs={{8,16},{24,32},{40,48},{56,64},{72,80},{88,96},{104,112},{120,128}... | collective-permute-start | bytes 442376 | tf_op jit(solution)/shard_map/ppermute | solution.py:19
  16.1 1.9 %collective-permute-start.1 = (bf16[2,2,12,12,128]{4,2,0,1,3:T(8,128)(2,1)S(1)}, bf16[2,2,12,12,128]{4,2,0,1,3:T(8,128)(2,1)S(1)}, u32[]{:S(2)}, u32[]{:S(2)}) collective-permute-start(bf16[2,2,12,12,128]{4,2,0,1,3:T(8,128)(2,1)S(1)} %copy.21), channel_id=1, source_target_pairs={{0,8},{16,24},{32,40},{48,56},{64,72},{80,88},{96,104},{112,120},{... | collective-permute-start | bytes 442376 | tf_op jit(solution)/shard_map/ppermute | solution.py:18
  18.0 0.9 %copy.42 = bf16[2,34,2,12,12]{1,3,2,4,0:T(8,128)(2,1)S(1)} copy(bf16[2,34,2,12,12]{1,2,4,3,0:T(2,128)(2,1)} %param.7) | data formatting | bytes 78336 | tf_op args[1]
  19.0 0.1 fusion.28
  19.1 0.0 copy-start.1
  19.1 0.0 copy-start.3
  19.1 0.1 pad_maximum_fusion
  19.2 0.2 copy.20
  19.5 0.1 iota_subtract_fusion
  19.6 1.3 %multiply_bitcast_fusion = bf16[2,34,2,6,2,12,12,1]{1,4,6,5,3,2,0,7:T(2,128)(2,1)S(1)} fusion(bf16[2,34,6]{1,2,0:T(8,128)(2,1)S(1)} %fusion.31, bf16[2,34,2,2,12,12]{1,3,5,4,2,0:T(2,128)(2,1)S(1)} %copy.20), kind=kLoop, calls=%fused_computation.7 | loop fusion | flops 235008 | bytes 549168 | tf_op jit(solution)/shard_map/mul | solution.py:43
  21.0 0.0 copy-done.1
  21.0 1.8 %select_reduce_fusion = (f32[224,128]{1,0:T(8,128)S(1)}, f32[224,128]{1,0:T(8,128)S(1)}) fusion(f32[70]{0:T(128)S(1)} %copy-done.1, s32[224,128]{1,0:T(8,128)S(1)} %iota_subtract_fusion, s32[70]{0:T(128)S(1)} %neg.9, f32[70]{0:T(128)S(1)} %copy-done.3, s32[70]{0:T(128)S(1)} %copy-done.2), kind=kLoop, calls=%fused_computation.1 | loop fusion | flops 11984896 | bytes 345184 | tf_op jit(solution)/shard_map/reduce_sum | solution.py:31
  22.8 0.0 collective-permute-done
  22.9 0.6 %collective-permute-done.1 = bf16[2,2,12,12,128]{4,2,0,1,3:T(8,128)(2,1)S(1)} collective-permute-done((bf16[2,2,12,12,128]{4,2,0,1,3:T(8,128)(2,1)S(1)}, bf16[2,2,12,12,128]{4,2,0,1,3:T(8,128)(2,1)S(1)}, u32[]{:S(2)}, u32[]{:S(2)}) %collective-permute-start.1) | collective-permute-done | bytes 147488 | tf_op jit(solution)/shard_map/ppermute | solution.py:18
  23.5 3.3 %fusion.7 = f32[2,2,12,12,128]{4,3,2,1,0:T(8,128)S(1)} fusion(bf16[2,34,2,6,2,12,12,1]{1,4,6,5,3,2,0,7:T(2,128)(2,1)S(1)} %multiply_bitcast_fusion, bf16[2,2,12,12,128]{4,2,0,1,3:T(8,128)(2,1)S(1)} %get-tuple-element.14, bf16[2,2,12,12,128]{4,2,0,1,3:T(8,128)(2,1)S(1)} %copy.21, bf16[2,2,12,12,128]{4,2,0,1,3:T(8,128)(2,1)S(1)} %get-tuple-element.13, ...), kind=kOutput, calls=%fused_computation.8 | convolution fusion | flops 846259200 | bytes 1285632 | tf_op jit(solution)/shard_map/akplie,akqpml->aqime/dot_general | solution.py:47
  26.9 0.1 broadcast_select_fusion.3
  27.0 4.8 %collective-permute-start.2 = (bf16[2,2,12,12,48]{4,3,2,1,0:T(8,128)(2,1)S(1)}, bf16[2,2,12,12,48]{4,3,2,1,0:T(8,128)(2,1)S(1)}, u32[]{:S(2)}, u32[]{:S(2)}) collective-permute-start(bf16[2,2,12,12,48]{4,3,2,1,0:T(8,128)(2,1)S(1)} %get-tuple-element.15), channel_id=1, source_target_pairs={{1,2},{3,4},{5,6},{2,1},{4,3},{6,5},{9,10},{11,12},{13,14},{10,9},... | collective-permute-start | bytes 165896 | tf_op jit(solution)/shard_map/ppermute | solution.py:19
  31.8 1.9 %collective-permute-start.3 = (bf16[2,2,12,12,48]{4,3,2,1,0:T(8,128)(2,1)S(1)}, bf16[2,2,12,12,48]{4,3,2,1,0:T(8,128)(2,1)S(1)}, u32[]{:S(2)}, u32[]{:S(2)}) collective-permute-start(bf16[2,2,12,12,48]{4,3,2,1,0:T(8,128)(2,1)S(1)} %get-tuple-element.16), channel_id=1, source_target_pairs={{0,1},{2,3},{4,5},{6,7},{1,0},{3,2},{5,4},{7,6},{8,9},{10,11},{12,... | collective-permute-start | bytes 165896 | tf_op jit(solution)/shard_map/ppermute | solution.py:18
  33.8 1.4 %collective-permute-done.2 = bf16[2,2,12,12,48]{4,3,2,1,0:T(8,128)(2,1)S(1)} collective-permute-done((bf16[2,2,12,12,48]{4,3,2,1,0:T(8,128)(2,1)S(1)}, bf16[2,2,12,12,48]{4,3,2,1,0:T(8,128)(2,1)S(1)}, u32[]{:S(2)}, u32[]{:S(2)}) %collective-permute-start.2) | collective-permute-done | bytes 55328 | tf_op jit(solution)/shard_map/ppermute | solution.py:19
  35.2 0.0 collective-permute-done.3
  35.2 0.1 select_convert_fusion.1
  35.2 0.9 %fusion.12 = f32[2,2,12,12,128]{4,3,2,1,0:T(8,128)S(1)} fusion(f32[2,2,12,12,48]{4,3,2,1,0:T(8,128)S(1)} %get-tuple-element.12, f32[2,2,12,12,128]{4,3,2,1,0:T(8,128)S(1)} %fusion.7, f32[2,2,12,12,48]{4,3,2,1,0:T(8,128)S(1)} %get-tuple-element.11, f32[224,128]{1,0:T(8,128)S(1)} %add.19), kind=kOutput, calls=%fused_computation.9 | convolution fusion | flops 198438912 | bytes 925696 | tf_op jit(solution)/shard_map/dot_general | solution.py:75
  36.2 0.9 %copy.25 = f32[2,2,12,12,128]{4,1,3,2,0:T(2,128)} copy(f32[2,2,12,12,128]{4,3,2,1,0:T(8,128)S(1)} %fusion.12) | data formatting | bytes 589824 | tf_op jit(solution)/shard_map/dot_general | solution.py:75
  (13 shorter events, 0.1 us)
Async XLA Ops:
  0.0 19.5 %copy-start = (s32[2,34]{1,0:T(2,128)S(1)}, s32[2,34]{1,0:T(2,128)}, u32[]{:S(2)}) copy-start(s32[2,34]{1,0:T(2,128)} %param.8) | copy-start | bytes 820
  0.0 19.6 %copy-start.2 = (s32[70]{0:T(128)S(1)}, s32[70]{0:T(128)}, u32[]{:S(2)}) copy-start(s32[70]{0:T(128)} %param.9) | copy-start | bytes 844
  1.0 21.9 %collective-permute-start = (bf16[2,2,12,12,128]{4,2,0,1,3:T(8,128)(2,1)S(1)}, bf16[2,2,12,12,128]{4,2,0,1,3:T(8,128)(2,1)S(1)}, u32[]{:S(2)}, u32[]{:S(2)}) collective-permute-start(bf16[2,2,12,12,128]{4,2,0,1,3:T(8,128)(2,1)S(1)} %copy.21), channel_id=1, source_target_pairs={{8,16},{24,32},{40,48},{56,64},{72,80},{88,96},{104,112},{120,128}... | collective-permute-start | bytes 442376 | tf_op jit(solution)/shard_map/ppermute | solution.py:19
  16.1 7.4 %collective-permute-start.1 = (bf16[2,2,12,12,128]{4,2,0,1,3:T(8,128)(2,1)S(1)}, bf16[2,2,12,12,128]{4,2,0,1,3:T(8,128)(2,1)S(1)}, u32[]{:S(2)}, u32[]{:S(2)}) collective-permute-start(bf16[2,2,12,12,128]{4,2,0,1,3:T(8,128)(2,1)S(1)} %copy.21), channel_id=1, source_target_pairs={{0,8},{16,24},{32,40},{48,56},{64,72},{80,88},{96,104},{112,120},{... | collective-permute-start | bytes 442376 | tf_op jit(solution)/shard_map/ppermute | solution.py:18
  19.1 1.9 %copy-start.1 = (f32[70]{0:T(128)S(1)}, f32[70]{0:T(128)}, u32[]{:S(2)}) copy-start(f32[70]{0:T(128)} %param.11) | copy-start | bytes 844
  19.1 1.9 %copy-start.3 = (f32[70]{0:T(128)S(1)}, f32[70]{0:T(128)}, u32[]{:S(2)}) copy-start(f32[70]{0:T(128)} %param.10) | copy-start | bytes 844
  27.0 8.2 %collective-permute-start.2 = (bf16[2,2,12,12,48]{4,3,2,1,0:T(8,128)(2,1)S(1)}, bf16[2,2,12,12,48]{4,3,2,1,0:T(8,128)(2,1)S(1)}, u32[]{:S(2)}, u32[]{:S(2)}) collective-permute-start(bf16[2,2,12,12,48]{4,3,2,1,0:T(8,128)(2,1)S(1)} %get-tuple-element.15), channel_id=1, source_target_pairs={{1,2},{3,4},{5,6},{2,1},{4,3},{6,5},{9,10},{11,12},{13,14},{10,9},... | collective-permute-start | bytes 165896 | tf_op jit(solution)/shard_map/ppermute | solution.py:19
  31.8 3.3 %collective-permute-start.3 = (bf16[2,2,12,12,48]{4,3,2,1,0:T(8,128)(2,1)S(1)}, bf16[2,2,12,12,48]{4,3,2,1,0:T(8,128)(2,1)S(1)}, u32[]{:S(2)}, u32[]{:S(2)}) collective-permute-start(bf16[2,2,12,12,48]{4,3,2,1,0:T(8,128)(2,1)S(1)} %get-tuple-element.16), channel_id=1, source_target_pairs={{0,1},{2,3},{4,5},{6,7},{1,0},{3,2},{5,4},{7,6},{8,9},{10,11},{12,... | collective-permute-start | bytes 165896 | tf_op jit(solution)/shard_map/ppermute | solution.py:18

commit v6 on v4

--- a/solution.py
+++ b/solution.py
@@ -22,6 +22,19 @@
             axis=dim,
         )
     return cells
+
+
+def swapped(head, tail, axis):
+    count = lax.axis_size(axis)
+    even = lax.axis_index(axis) % 2 == 0
+    edges = {
+        parity: [(i, i + 1) for i in range(parity, count - 1, 2)]
+        + [(i + 1, i) for i in range(parity, count - 1, 2)]
+        for parity in (0, 1)
+    }
+    from_even = lax.ppermute(jnp.where(even, tail, head), axis, edges[0])
+    from_odd = lax.ppermute(jnp.where(even, head, tail), axis, edges[1])
+    return jnp.where(even, from_odd, from_even), jnp.where(even, from_even, from_odd)
 
 
 def make_kernel(spread_diff, offsets, w_emit, w_absorb):
@@ -63,7 +76,18 @@
     kernel = make_kernel(spread_diff, offsets, w_emit, w_absorb)
     coupled = coupled_blocks(window, coupling, local_ids)
     coupled, kernel = lax.optimization_barrier((coupled, kernel))
-    widened = extended(coupled, (("energy", 4),), reach)
+    rows = coupled.size // points
+    flat = coupled.reshape(rows, points)
+    packed = (rows * reach) // 128
+
+    def pack(part):
+        return part.astype(jnp.bfloat16).reshape(packed, 128)
+
+    def unpack(part):
+        return part.reshape(rows, reach).astype(jnp.float32)
+
+    lower, upper = swapped(pack(flat[:, :reach]), pack(flat[:, points - reach:]), "energy")
+    widened = jnp.concatenate([unpack(lower), flat, unpack(upper)], axis=1)
     result = jnp.dot(
         widened.reshape(-1, extent), kernel, precision=hi, preferred_element_type=jnp.float32
     )

time: 39.7 us -> 37.7 us (0.950)
  other arithmetic: 3.72 us -> 2.3 us
    ppermute x0 -> x2, starting transfers between devices: none -> 6.74 us  [the longest x1 4.82 us: swapped(): from_odd = lax.ppermute(jnp.where(even, head, tail), axis, edges[1])]
    ppermute x2 -> x1, starting transfers between devices: 19.9 us -> 15.1 us  [extended(): from_odd = lax.ppermute(jnp.where(even, head, tail), axis, edges[1])]
    ppermute x2 -> x1, waiting for transfers between devices: 3.52 us -> 0.01 us  [extended(): from_odd = lax.ppermute(jnp.where(even, head, tail), axis, edges[1])]
    ppermute x2 -> x1, waiting for transfers between devices: 0.63 us -> 2.58 us  [extended(): from_even = lax.ppermute(jnp.where(even, tail, head), axis, edges[0])]
    ppermute x2 -> x1, starting transfers between devices: 3.84 us -> 1.92 us  [extended(): from_even = lax.ppermute(jnp.where(even, tail, head), axis, edges[0])]
    mul x1 -> x0, other arithmetic: 1.31 us -> none  [coupled_blocks(): left = mbig[:, :, :, None] * onehot[:, :, None, :, None, None, None]]
    ppermute x0 -> x2, waiting for transfers between devices: none -> 1.2 us  [the longest x1 1.19 us: swapped(): from_even = lax.ppermute(jnp.where(even, tail, head), axis, edges[0])]
    reshape x0 -> x3, local copies, waits for them, and re-layouts: none -> 1 us  [the longest x2 0.97 us: shards(): return result.reshape(coupled.shape)]
  transfers between devices with their start and end apart: 4 -> 4, of which waited for: 2 -> 2; matrix products, arithmetic and copies ran while one was open for 12% -> 7% of each run, Pallas kernels for 0% -> 0%
where the time goes in v6:
time: 37.7 us; the launch traced here: 37.4 us
  starting transfers between devices  23.7 us (63%)
  matrix products  4.06 us (11%)
  waiting for transfers between devices  3.78 us (10%)
  local copies, waits for them, and re-layouts  3.26 us (9%)
  other arithmetic  2.3 us (6%)
    ppermute x1, starting transfers between devices, extended(): from_odd = lax.ppermute(jnp.where(even, head, tail), axis, edges[1])  15.1 us
    ppermute x1, starting transfers between devices, swapped(): from_odd = lax.ppermute(jnp.where(even, head, tail), axis, edges[1])  4.82 us
    dot_general x1, matrix products, coupled_blocks(): jnp.einsum('akplie,akqpml->aqime', x, right, preferred_element_type=f32)  3.33 us
    ppermute x1, waiting for transfers between devices, extended(): from_even = lax.ppermute(jnp.where(even, tail, head), axis, edges[0])  2.58 us
    ppermute x1, starting transfers between devices, extended(): from_even = lax.ppermute(jnp.where(even, tail, head), axis, edges[0])  1.92 us
    ppermute x1, starting transfers between devices, swapped(): from_even = lax.ppermute(jnp.where(even, tail, head), axis, edges[0])  1.92 us
    reduce_sum x1, other arithmetic, make_kernel(): jnp.sum(jnp.where(spread_diff[:, :, None] == -offsets, w_absorb, jnp.floa...  1.8 us
    unnamed x12, local copies, waits for them, and re-layouts  1.45 us
  transfers between devices with their start and end apart: 4, of which 2 were waited for; matrix products, arithmetic and copies ran while one was open for 7% of the time, Pallas kernels for 0%

profile of v6, /device:TPU:57, one launch (start us, length us, event | category | flops | bytes accessed | tf_op | source)
XLA Modules:
  0.0 37.4 jit_solution(3736148845701024581)
XLA Ops:
  0.0 1.0 %copy.21 = bf16[2,2,12,12,128]{4,2,0,1,3:T(8,128)(2,1)S(1)} copy(bf16[2,2,12,12,128]{4,1,3,2,0:T(2,128)(2,1)} %param.6) | data formatting | bytes 294912 | tf_op args[0]
  1.0 15.1 %collective-permute-start = (bf16[2,2,12,12,128]{4,2,0,1,3:T(8,128)(2,1)S(1)}, bf16[2,2,12,12,128]{4,2,0,1,3:T(8,128)(2,1)S(1)}, u32[]{:S(2)}, u32[]{:S(2)}) collective-permute-start(bf16[2,2,12,12,128]{4,2,0,1,3:T(8,128)(2,1)S(1)} %copy.21), channel_id=1, source_target_pairs={{8,16},{24,32},{40,48},{56,64},{72,80},{88,96},{104,112},{120,128}... | collective-permute-start | bytes 442376 | tf_op jit(solution)/shard_map/ppermute | solution.py:19
  16.1 1.9 %collective-permute-start.1 = (bf16[2,2,12,12,128]{4,2,0,1,3:T(8,128)(2,1)S(1)}, bf16[2,2,12,12,128]{4,2,0,1,3:T(8,128)(2,1)S(1)}, u32[]{:S(2)}, u32[]{:S(2)}) collective-permute-start(bf16[2,2,12,12,128]{4,2,0,1,3:T(8,128)(2,1)S(1)} %copy.21), channel_id=1, source_target_pairs={{0,8},{16,24},{32,40},{48,56},{64,72},{80,88},{96,104},{112,120},{... | collective-permute-start | bytes 442376 | tf_op jit(solution)/shard_map/ppermute | solution.py:18
  18.2 0.1 fusion.34
  18.2 0.1 pad_maximum_fusion
  18.3 0.0 copy-start.3
  18.4 0.0 copy-start.1
  18.4 0.1 copy.20
  18.5 0.1 iota_subtract_fusion
  18.6 0.4 copy-done.3
  19.0 0.0 copy-done.1
  19.1 1.8 %select_reduce_fusion = (f32[224,128]{1,0:T(8,128)S(1)}, f32[224,128]{1,0:T(8,128)S(1)}) fusion(f32[70]{0:T(128)S(1)} %copy-done.2, s32[224,128]{1,0:T(8,128)S(1)} %iota_subtract_fusion, s32[70]{0:T(128)S(1)} %neg.9, f32[70]{0:T(128)S(1)} %copy-done.4, s32[70]{0:T(128)S(1)} %copy-done.3), kind=kLoop, calls=%fused_computation.1 | loop fusion | flops 11984896 | bytes 345184 | tf_op jit(solution)/shard_map/reduce_sum | solution.py:44
  20.9 2.6 %collective-permute-done.1 = bf16[2,2,12,12,128]{4,2,0,1,3:T(8,128)(2,1)S(1)} collective-permute-done((bf16[2,2,12,12,128]{4,2,0,1,3:T(8,128)(2,1)S(1)}, bf16[2,2,12,12,128]{4,2,0,1,3:T(8,128)(2,1)S(1)}, u32[]{:S(2)}, u32[]{:S(2)}) %collective-permute-start.1) | collective-permute-done | bytes 147488 | tf_op jit(solution)/shard_map/ppermute | solution.py:18
  23.5 3.3 %fusion.9 = f32[2,2,12,12,128]{4,3,2,1,0:T(8,128)S(1)} fusion(bf16[2,34,6]{1,2,0:T(8,128)(2,1)S(1)} %fusion.36, bf16[2,34,2,2,12,12]{1,5,3,2,4,0:T(8,128)(2,1)S(1)} %copy.20, bf16[2,2,12,12,128]{4,2,0,1,3:T(8,128)(2,1)S(1)} %get-tuple-element.12, bf16[2,2,12,12,128]{4,2,0,1,3:T(8,128)(2,1)S(1)} %copy.21, ...), kind=kOutput, calls=%fused_computation.8 | convolution fusion | flops 847199232 | bytes 894768 | tf_op jit(solution)/shard_map/akplie,akqpml->aqime/dot_general | solution.py:60
  26.9 0.1 broadcast_select_fusion.3
  27.0 0.2 select_n.72
  27.2 4.8 %collective-permute-start.2 = (bf16[216,128]{1,0:T(8,128)(2,1)S(1)}, bf16[216,128]{1,0:T(8,128)(2,1)S(1)}, u32[]{:S(2)}, u32[]{:S(2)}) collective-permute-start(bf16[216,128]{1,0:T(8,128)(2,1)S(1)} %select_n.72), channel_id=1, source_target_pairs={{1,2},{3,4},{5,6},{2,1},{4,3},{6,5},{9,10},{11,12},{13,14},{10,9},... | collective-permute-start | bytes 165896 | tf_op jit(solution)/shard_map/ppermute | solution.py:36
  32.1 0.2 select_n.74
  32.3 1.9 %collective-permute-start.3 = (bf16[216,128]{1,0:T(8,128)(2,1)S(1)}, bf16[216,128]{1,0:T(8,128)(2,1)S(1)}, u32[]{:S(2)}, u32[]{:S(2)}) collective-permute-start(bf16[216,128]{1,0:T(8,128)(2,1)S(1)} %select_n.74), channel_id=1, source_target_pairs={{0,1},{2,3},{4,5},{6,7},{1,0},{3,2},{5,4},{7,6},{8,9},{10,11},{12,... | collective-permute-start | bytes 165896 | tf_op jit(solution)/shard_map/ppermute | solution.py:35
  34.2 1.2 %collective-permute-done.3 = bf16[216,128]{1,0:T(8,128)(2,1)S(1)} collective-permute-done((bf16[216,128]{1,0:T(8,128)(2,1)S(1)}, bf16[216,128]{1,0:T(8,128)(2,1)S(1)}, u32[]{:S(2)}, u32[]{:S(2)}) %collective-permute-start.3) | collective-permute-done | bytes 55328 | tf_op jit(solution)/shard_map/ppermute | solution.py:35
  35.4 0.1 reshape.53
  35.6 0.1 reshape.54
  35.7 0.7 %fusion.26 = f32[576,128]{1,0:T(8,128)S(1)} fusion(f32[224,128]{1,0:T(8,128)S(1)} %add.19, f32[576,48]{1,0:T(8,128)S(1)} %reshape.54, f32[576,128]{1,0:T(8,128)S(1)} %reshape.51, f32[576,48]{1,0:T(8,128)S(1)} %reshape.53), kind=kOutput, calls=%fused_computation.16 | convolution fusion | flops 198438912 | bytes 925696 | tf_op jit(solution)/shard_map/dot_general | solution.py:91
  36.5 0.9 %copy.24 = f32[2,2,12,12,128]{4,1,3,2,0:T(2,128)} copy(f32[2,2,12,12,128]{4,3,2,1,0:T(8,128)S(1)} %reshape.52) | data formatting | bytes 589824 | tf_op jit(solution)/shard_map/reshape | solution.py:94
  (20 shorter events, 0.2 us)
Async XLA Ops:
  0.0 18.1 %copy-start = (bf16[2,34,2,12,12]{1,2,4,3,0:T(2,128)(2,1)S(1)}, bf16[2,34,2,12,12]{1,2,4,3,0:T(2,128)(2,1)}, u32[]{:S(2)}) copy-start(bf16[2,34,2,12,12]{1,2,4,3,0:T(2,128)(2,1)} %param.7) | copy-start | bytes 117508
  1.0 19.9 %collective-permute-start = (bf16[2,2,12,12,128]{4,2,0,1,3:T(8,128)(2,1)S(1)}, bf16[2,2,12,12,128]{4,2,0,1,3:T(8,128)(2,1)S(1)}, u32[]{:S(2)}, u32[]{:S(2)}) collective-permute-start(bf16[2,2,12,12,128]{4,2,0,1,3:T(8,128)(2,1)S(1)} %copy.21), channel_id=1, source_target_pairs={{8,16},{24,32},{40,48},{56,64},{72,80},{88,96},{104,112},{120,128}... | collective-permute-start | bytes 442376 | tf_op jit(solution)/shard_map/ppermute | solution.py:19
  16.1 7.4 %collective-permute-start.1 = (bf16[2,2,12,12,128]{4,2,0,1,3:T(8,128)(2,1)S(1)}, bf16[2,2,12,12,128]{4,2,0,1,3:T(8,128)(2,1)S(1)}, u32[]{:S(2)}, u32[]{:S(2)}) collective-permute-start(bf16[2,2,12,12,128]{4,2,0,1,3:T(8,128)(2,1)S(1)} %copy.21), channel_id=1, source_target_pairs={{0,8},{16,24},{32,40},{48,56},{64,72},{80,88},{96,104},{112,120},{... | collective-permute-start | bytes 442376 | tf_op jit(solution)/shard_map/ppermute | solution.py:18
  18.3 0.7 %copy-start.3 = (s32[70]{0:T(128)S(1)}, s32[70]{0:T(128)}, u32[]{:S(2)}) copy-start(s32[70]{0:T(128)} %param.9) | copy-start | bytes 844
  18.4 0.7 %copy-start.1 = (s32[2,34]{1,0:T(2,128)S(1)}, s32[2,34]{1,0:T(2,128)}, u32[]{:S(2)}) copy-start(s32[2,34]{1,0:T(2,128)} %param.8) | copy-start | bytes 820
  18.4 0.7 %copy-start.2 = (f32[70]{0:T(128)S(1)}, f32[70]{0:T(128)}, u32[]{:S(2)}) copy-start(f32[70]{0:T(128)} %param.11) | copy-start | bytes 844
  18.4 0.7 %copy-start.4 = (f32[70]{0:T(128)S(1)}, f32[70]{0:T(128)}, u32[]{:S(2)}) copy-start(f32[70]{0:T(128)} %param.10) | copy-start | bytes 844
  27.2 7.0 %collective-permute-start.2 = (bf16[216,128]{1,0:T(8,128)(2,1)S(1)}, bf16[216,128]{1,0:T(8,128)(2,1)S(1)}, u32[]{:S(2)}, u32[]{:S(2)}) collective-permute-start(bf16[216,128]{1,0:T(8,128)(2,1)S(1)} %select_n.72), channel_id=1, source_target_pairs={{1,2},{3,4},{5,6},{2,1},{4,3},{6,5},{9,10},{11,12},{13,14},{10,9},... | collective-permute-start | bytes 165896 | tf_op jit(solution)/shard_map/ppermute | solution.py:36
  32.3 3.1 %collective-permute-start.3 = (bf16[216,128]{1,0:T(8,128)(2,1)S(1)}, bf16[216,128]{1,0:T(8,128)(2,1)S(1)}, u32[]{:S(2)}, u32[]{:S(2)}) collective-permute-start(bf16[216,128]{1,0:T(8,128)(2,1)S(1)} %select_n.74), channel_id=1, source_target_pairs={{0,1},{2,3},{4,5},{6,7},{1,0},{3,2},{5,4},{7,6},{8,9},{10,11},{12,... | collective-permute-start | bytes 165896 | tf_op jit(solution)/shard_map/ppermute | solution.py:35

commit v7 on v6

--- a/solution.py
+++ b/solution.py
@@ -48,13 +48,15 @@
 
 def coupled_blocks(window, coupling, local_ids):
     f32, bf16 = jnp.float32, jnp.bfloat16
-    nwin = window.shape[0]
+    nwin = window.shape[1]
+    atoms, nb, _, orb, _ = coupling.shape
     onehot = (local_ids[:, :, None] == jnp.arange(nwin, dtype=local_ids.dtype)).astype(bf16)
     mr = coupling[:, :, 0]
     mi = coupling[:, :, 1]
-    mbig = jnp.stack([jnp.stack([mr, -mi], axis=2), jnp.stack([mi, mr], axis=2)], axis=2)
-    left = mbig[:, :, :, None] * onehot[:, :, None, :, None, None, None]
-    x = jnp.einsum("akqwpij,wpjle->akqile", left, window, preferred_element_type=f32).astype(bf16)
+    mbig = jnp.stack([jnp.stack([mr, -mi], axis=4), jnp.stack([mi, mr], axis=4)], axis=2)
+    mbig = mbig.reshape(atoms, nb, 2, orb, 2 * orb)
+    left = mbig[:, :, :, None] * onehot[:, :, None, :, None, None]
+    x = jnp.einsum("akqwis,lwse->akqile", left, window, preferred_element_type=f32).astype(bf16)
     x = x.transpose(0, 1, 2, 4, 3, 5)
     right = jnp.stack([jnp.stack([mr, mi], axis=2), jnp.stack([-mi, mr], axis=2)], axis=2)
     return jnp.einsum("akplie,akqpml->aqime", x, right, preferred_element_type=f32)
@@ -65,7 +67,8 @@
     atoms_here = green.shape[0]
     points = green.shape[-1]
     reach = points * 3 // 8
-    window = extended(green, (("atom", 0),), atoms_here)
+    merged = green.transpose(3, 0, 2, 1, 4).reshape(green.shape[3], atoms_here, -1, points)
+    window = extended(merged, (("atom", 1),), atoms_here)
     local_ids = neighbours - (lax.axis_index("atom") - 1) * atoms_here
     extent = points + 2 * reach
     spread_diff = (

time: 37.7 us -> 36.6 us (0.971)
  waiting for transfers between devices: 3.78 us -> 1.49 us
  other arithmetic: 2.3 us -> 3.48 us
    ppermute x1, waiting for transfers between devices: 2.58 us -> 0.29 us  [extended(): from_even = lax.ppermute(jnp.where(even, tail, head), axis, edges[0])]
    unnamed x12 -> x11, local copies, waits for them, and re-layouts: 1.45 us -> 0.38 us
    transpose x0 -> x1, local copies, waits for them, and re-layouts: none -> 1.05 us  [shards(): green.transpose(3, 0, 2, 1, 4)]
    another operation x1 -> x2, other arithmetic: 0.07 us -> 0.74 us  [coupled_blocks(): jnp.stack([jnp.stack([mr, mi], axis=2), jnp.stack([-mi, mr], axis=2)], ax...]
  transfers between devices with their start and end apart: 4 -> 4, of which waited for: 2 -> 2; matrix products, arithmetic and copies ran while one was open for 7% -> 11% of each run, Pallas kernels for 0% -> 0%
where the time goes in v7:
time: 36.6 us; the launch traced here: 36.3 us
  starting transfers between devices  23.7 us (65%)
  matrix products  3.97 us (11%)
  other arithmetic  3.48 us (10%)
  local copies, waits for them, and re-layouts  3.34 us (9%)
  waiting for transfers between devices  1.49 us (4%)
    ppermute x1, starting transfers between devices, extended(): from_odd = lax.ppermute(jnp.where(even, head, tail), axis, edges[1])  15.1 us
    ppermute x1, starting transfers between devices, swapped(): from_odd = lax.ppermute(jnp.where(even, head, tail), axis, edges[1])  4.82 us
    dot_general x1, matrix products, coupled_blocks(): jnp.einsum('akplie,akqpml->aqime', x, right, preferred_element_type=f32)  3.25 us
    ppermute x1, starting transfers between devices, extended(): from_even = lax.ppermute(jnp.where(even, tail, head), axis, edges[0])  1.92 us
    ppermute x1, starting transfers between devices, swapped(): from_even = lax.ppermute(jnp.where(even, tail, head), axis, edges[0])  1.92 us
    reduce_sum x1, other arithmetic, make_kernel(): jnp.sum(jnp.where(spread_diff[:, :, None] == -offsets, w_absorb, jnp.floa...  1.81 us
    ppermute x1, waiting for transfers between devices, swapped(): from_even = lax.ppermute(jnp.where(even, tail, head), axis, edges[0])  1.19 us
    transpose x1, local copies, waits for them, and re-layouts, shards(): green.transpose(3, 0, 2, 1, 4)  1.05 us
  transfers between devices with their start and end apart: 4, of which 2 were waited for; matrix products, arithmetic and copies ran while one was open for 11% of the time, Pallas kernels for 0%

profile of v7, /device:TPU:57, one launch (start us, length us, event | category | flops | bytes accessed | tf_op | source)
XLA Modules:
  0.0 36.3 jit_solution(17869798489496611397)
XLA Ops:
  0.0 1.0 %copy.36 = bf16[12,2,12,2,128]{4,3,2,1,0:T(2,128)(2,1)S(1)} copy(bf16[12,2,12,2,128]{4,3,0,2,1:T(2,128)(2,1)} %bitcast.62) | data formatting | bytes 294912 | tf_op jit(solution)/shard_map/transpose | solution.py:70
  1.1 15.1 %collective-permute-start = (bf16[12,2,24,128]{3,2,1,0:T(8,128)(2,1)S(1)}, bf16[12,2,24,128]{3,2,1,0:T(8,128)(2,1)S(1)}, u32[]{:S(2)}, u32[]{:S(2)}) collective-permute-start(bf16[12,2,24,128]{3,2,1,0:T(8,128)(2,1)S(1)} %bitcast.63), channel_id=1, source_target_pairs={{8,16},{24,32},{40,48},{56,64},{72,80},{88,96},{104,112},{120,128}... | collective-permute-start | bytes 442376 | tf_op jit(solution)/shard_map/ppermute | solution.py:19
  16.2 1.9 %collective-permute-start.1 = (bf16[12,2,24,128]{3,2,1,0:T(8,128)(2,1)S(1)}, bf16[12,2,24,128]{3,2,1,0:T(8,128)(2,1)S(1)}, u32[]{:S(2)}, u32[]{:S(2)}) collective-permute-start(bf16[12,2,24,128]{3,2,1,0:T(8,128)(2,1)S(1)} %bitcast.64), channel_id=1, source_target_pairs={{0,8},{16,24},{32,40},{48,56},{64,72},{80,88},{96,104},{112,120},{... | collective-permute-start | bytes 442376 | tf_op jit(solution)/shard_map/ppermute | solution.py:18
  18.1 0.1 copy.55
  18.2 0.2 slice_negate_fusion
  18.5 0.2 copy-done.1
  18.9 0.4 %pad_maximum_fusion = (bf16[2,34,12,12,2]{1,0,3,2,4:T(2,128)(2,1)S(1)}, bf16[2,34,12,12,2]{1,0,3,2,4:T(2,128)(2,1)S(1)}) fusion(bf16[2,34,12,12,1]{1,0,3,2,4:T(2,128)(2,1)S(1)} %fusion.37, bf16[2,34,12,12,1]{1,0,3,2,4:T(2,128)(2,1)S(1)} %get-tuple-element.20, bf16[2,34,12,12,1]{1,0,3,2,4:T(2,128)(2,1)S(1)} %get-tuple-element.18), kind=kLoop, calls=%fused_computation.26 | loop fusion | flops 39168 | bytes 137088 | tf_op jit(solution)/shard_map/stack | solution.py:56
  19.3 1.8 %select_reduce_fusion = (f32[224,128]{1,0:T(8,128)S(1)}, f32[224,128]{1,0:T(8,128)S(1)}) fusion(f32[70]{0:T(128)S(1)} %copy-done.2, s32[224,128]{1,0:T(8,128)S(1)} %iota_subtract_fusion, s32[70]{0:T(128)S(1)} %neg.19, f32[70]{0:T(128)S(1)} %copy-done.4, s32[70]{0:T(128)S(1)} %copy-done.3), kind=kLoop, calls=%fused_computation.1 | loop fusion | flops 11984896 | bytes 345184 | tf_op jit(solution)/shard_map/reduce_sum | solution.py:44
  21.1 0.2 maximum_bitcast_fusion.5
  21.4 0.1 copy.33
  21.5 0.1 copy.34
  21.7 0.5 %maximum_bitcast_fusion.3 = bf16[2,34,2,2,12,12,1]{1,0,5,4,3,2,6:T(2,128)(2,1)S(1)} fusion(bf16[2,34,1,2,12,12]{1,0,5,4,3,2:T(2,128)(2,1)S(1)} %maximum_bitcast_fusion.5, bf16[2,34,1,2,12,12]{1,0,5,4,3,2:T(2,128)(2,1)S(1)} %bitcast.61), kind=kLoop, calls=%fused_computation.23 | loop fusion | flops 39168 | bytes 156672 | tf_op jit(solution)/shard_map/stack | solution.py:61
  22.2 0.3 collective-permute-done.1
  22.5 3.2 %fusion.9 = f32[2,2,12,12,128]{4,3,2,1,0:T(8,128)S(1)} fusion(bf16[2,34,6]{1,2,0:T(8,128)(2,1)S(1)} %fusion.33, bf16[12,2,24,128]{3,2,1,0:T(8,128)(2,1)S(1)} %get-tuple-element.12, bf16[12,2,24,128]{3,2,1,0:T(8,128)(2,1)S(1)} %bitcast.65, bf16[12,2,24,128]{3,2,1,0:T(8,128)(2,1)S(1)} %get-tuple-element.11, ...), kind=kOutput, calls=%fused_computation.8 | convolution fusion | flops 847081728 | bytes 894768 | tf_op jit(solution)/shard_map/akplie,akqpml->aqime/dot_general | solution.py:62
  25.8 0.1 broadcast_select_fusion.3
  26.0 0.2 select_n.72
  26.2 4.8 %collective-permute-start.2 = (bf16[216,128]{1,0:T(8,128)(2,1)S(1)}, bf16[216,128]{1,0:T(8,128)(2,1)S(1)}, u32[]{:S(2)}, u32[]{:S(2)}) collective-permute-start(bf16[216,128]{1,0:T(8,128)(2,1)S(1)} %select_n.72), channel_id=1, source_target_pairs={{1,2},{3,4},{5,6},{2,1},{4,3},{6,5},{9,10},{11,12},{13,14},{10,9},... | collective-permute-start | bytes 165896 | tf_op jit(solution)/shard_map/ppermute | solution.py:36
  31.0 0.2 select_n.74
  31.2 1.9 %collective-permute-start.3 = (bf16[216,128]{1,0:T(8,128)(2,1)S(1)}, bf16[216,128]{1,0:T(8,128)(2,1)S(1)}, u32[]{:S(2)}, u32[]{:S(2)}) collective-permute-start(bf16[216,128]{1,0:T(8,128)(2,1)S(1)} %select_n.74), channel_id=1, source_target_pairs={{0,1},{2,3},{4,5},{6,7},{1,0},{3,2},{5,4},{7,6},{8,9},{10,11},{12,... | collective-permute-start | bytes 165896 | tf_op jit(solution)/shard_map/ppermute | solution.py:35
  33.1 1.2 %collective-permute-done.3 = bf16[216,128]{1,0:T(8,128)(2,1)S(1)} collective-permute-done((bf16[216,128]{1,0:T(8,128)(2,1)S(1)}, bf16[216,128]{1,0:T(8,128)(2,1)S(1)}, u32[]{:S(2)}, u32[]{:S(2)}) %collective-permute-start.3) | collective-permute-done | bytes 55328 | tf_op jit(solution)/shard_map/ppermute | solution.py:35
  34.3 0.1 reshape.70
  34.5 0.1 reshape.71
  34.6 0.7 %fusion.18 = f32[576,128]{1,0:T(8,128)S(1)} fusion(f32[224,128]{1,0:T(8,128)S(1)} %add.19, f32[576,48]{1,0:T(8,128)S(1)} %reshape.71, f32[576,128]{1,0:T(8,128)S(1)} %reshape.68, f32[576,48]{1,0:T(8,128)S(1)} %reshape.70), kind=kOutput, calls=%fused_computation.11 | convolution fusion | flops 198438912 | bytes 925696 | tf_op jit(solution)/shard_map/dot_general | solution.py:94
  35.4 0.9 %copy.38 = f32[2,2,12,12,128]{4,1,3,2,0:T(2,128)} copy(f32[2,2,12,12,128]{4,3,2,1,0:T(8,128)S(1)} %reshape.69) | data formatting | bytes 589824 | tf_op jit(solution)/shard_map/reshape | solution.py:97
  (23 shorter events, 0.3 us)
Async XLA Ops:
  0.0 18.1 %copy-start = (bf16[2,34,2,12,12]{1,2,4,3,0:T(2,128)(2,1)S(1)}, bf16[2,34,2,12,12]{1,2,4,3,0:T(2,128)(2,1)}, u32[]{:S(2)}) copy-start(bf16[2,34,2,12,12]{1,2,4,3,0:T(2,128)(2,1)} %param.7) | copy-start | bytes 117508
  1.1 21.2 %collective-permute-start = (bf16[12,2,24,128]{3,2,1,0:T(8,128)(2,1)S(1)}, bf16[12,2,24,128]{3,2,1,0:T(8,128)(2,1)S(1)}, u32[]{:S(2)}, u32[]{:S(2)}) collective-permute-start(bf16[12,2,24,128]{3,2,1,0:T(8,128)(2,1)S(1)} %bitcast.63), channel_id=1, source_target_pairs={{8,16},{24,32},{40,48},{56,64},{72,80},{88,96},{104,112},{120,128}... | collective-permute-start | bytes 442376 | tf_op jit(solution)/shard_map/ppermute | solution.py:19
  16.2 6.3 %collective-permute-start.1 = (bf16[12,2,24,128]{3,2,1,0:T(8,128)(2,1)S(1)}, bf16[12,2,24,128]{3,2,1,0:T(8,128)(2,1)S(1)}, u32[]{:S(2)}, u32[]{:S(2)}) collective-permute-start(bf16[12,2,24,128]{3,2,1,0:T(8,128)(2,1)S(1)} %bitcast.64), channel_id=1, source_target_pairs={{0,8},{16,24},{32,40},{48,56},{64,72},{80,88},{96,104},{112,120},{... | collective-permute-start | bytes 442376 | tf_op jit(solution)/shard_map/ppermute | solution.py:18
  18.1 0.7 %copy-start.1 = (s32[2,34]{1,0:T(2,128)S(1)}, s32[2,34]{1,0:T(2,128)}, u32[]{:S(2)}) copy-start(s32[2,34]{1,0:T(2,128)} %param.8) | copy-start | bytes 820
  18.2 0.7 %copy-start.3 = (s32[70]{0:T(128)S(1)}, s32[70]{0:T(128)}, u32[]{:S(2)}) copy-start(s32[70]{0:T(128)} %param.9) | copy-start | bytes 844
  18.4 0.9 %copy-start.2 = (f32[70]{0:T(128)S(1)}, f32[70]{0:T(128)}, u32[]{:S(2)}) copy-start(f32[70]{0:T(128)} %param.11) | copy-start | bytes 844
  18.4 0.9 %copy-start.4 = (f32[70]{0:T(128)S(1)}, f32[70]{0:T(128)}, u32[]{:S(2)}) copy-start(f32[70]{0:T(128)} %param.10) | copy-start | bytes 844
  26.2 7.0 %collective-permute-start.2 = (bf16[216,128]{1,0:T(8,128)(2,1)S(1)}, bf16[216,128]{1,0:T(8,128)(2,1)S(1)}, u32[]{:S(2)}, u32[]{:S(2)}) collective-permute-start(bf16[216,128]{1,0:T(8,128)(2,1)S(1)} %select_n.72), channel_id=1, source_target_pairs={{1,2},{3,4},{5,6},{2,1},{4,3},{6,5},{9,10},{11,12},{13,14},{10,9},... | collective-permute-start | bytes 165896 | tf_op jit(solution)/shard_map/ppermute | solution.py:36
  31.2 3.1 %collective-permute-start.3 = (bf16[216,128]{1,0:T(8,128)(2,1)S(1)}, bf16[216,128]{1,0:T(8,128)(2,1)S(1)}, u32[]{:S(2)}, u32[]{:S(2)}) collective-permute-start(bf16[216,128]{1,0:T(8,128)(2,1)S(1)} %select_n.74), channel_id=1, source_target_pairs={{0,1},{2,3},{4,5},{6,7},{1,0},{3,2},{5,4},{7,6},{8,9},{10,11},{12,... | collective-permute-start | bytes 165896 | tf_op jit(solution)/shard_map/ppermute | solution.py:35

commit v8 on v7

--- a/solution.py
+++ b/solution.py
@@ -24,7 +24,7 @@
     return cells
 
 
-def swapped(head, tail, axis):
+def swapped(head, tail, axis, between=None):
     count = lax.axis_size(axis)
     even = lax.axis_index(axis) % 2 == 0
     edges = {
@@ -33,7 +33,10 @@
         for parity in (0, 1)
     }
     from_even = lax.ppermute(jnp.where(even, tail, head), axis, edges[0])
-    from_odd = lax.ppermute(jnp.where(even, head, tail), axis, edges[1])
+    second = jnp.where(even, head, tail)
+    if between is not None:
+        second, _ = lax.optimization_barrier((second, between))
+    from_odd = lax.ppermute(second, axis, edges[1])
     return jnp.where(even, from_odd, from_even), jnp.where(even, from_even, from_odd)
 
 
@@ -68,8 +71,6 @@
     points = green.shape[-1]
     reach = points * 3 // 8
     merged = green.transpose(3, 0, 2, 1, 4).reshape(green.shape[3], atoms_here, -1, points)
-    window = extended(merged, (("atom", 1),), atoms_here)
-    local_ids = neighbours - (lax.axis_index("atom") - 1) * atoms_here
     extent = points + 2 * reach
     spread_diff = (
         jnp.arange(extent, dtype=jnp.int32)[:, None]
@@ -77,6 +78,9 @@
         - jnp.arange(points, dtype=jnp.int32)[None, :]
     )
     kernel = make_kernel(spread_diff, offsets, w_emit, w_absorb)
+    before, after = swapped(merged, merged, "atom", kernel)
+    window = jnp.concatenate([before, merged, after], axis=1)
+    local_ids = neighbours - (lax.axis_index("atom") - 1) * atoms_here
     coupled = coupled_blocks(window, coupling, local_ids)
     coupled, kernel = lax.optimization_barrier((coupled, kernel))
     rows = coupled.size // points

time: 36.6 us -> 39.3 us (1.074)
  waiting for transfers between devices: 1.49 us -> 3.57 us
  other arithmetic: 3.48 us -> 4.13 us
    ppermute x3 -> x2, starting transfers between devices: 21.8 us -> 16.3 us  [swapped(): from_odd = lax.ppermute(second, axis, edges[1])]
    ppermute x1 -> x2, starting transfers between devices: 1.92 us -> 7.44 us  [swapped(): from_even = lax.ppermute(jnp.where(even, tail, head), axis, edges[0])]
    ppermute x3 -> x2, waiting for transfers between devices: 0.29 us -> 3.56 us  [swapped(): from_odd = lax.ppermute(second, axis, edges[1])]
    ppermute x1 -> x2, waiting for transfers between devices: 1.19 us -> 0.01 us  [swapped(): from_even = lax.ppermute(jnp.where(even, tail, head), axis, edges[0])]
    neg x1, other arithmetic: 0.01 us -> 0.66 us  [make_kernel(): -offsets]
where the time goes in v8:
time: 39.3 us; the launch traced here: 39.1 us
  starting transfers between devices  23.7 us (60%)
  other arithmetic  4.13 us (11%)
  matrix products  3.97 us (10%)
  waiting for transfers between devices  3.57 us (9%)
  local copies, waits for them, and re-layouts  3.38 us (9%)
    ppermute x2, starting transfers between devices, swapped(): from_odd = lax.ppermute(second, axis, edges[1])  16.3 us
    ppermute x2, starting transfers between devices, swapped(): from_even = lax.ppermute(jnp.where(even, tail, head), axis, edges[0])  7.44 us
    ppermute x2, waiting for transfers between devices, swapped(): from_odd = lax.ppermute(second, axis, edges[1])  3.56 us
    dot_general x1, matrix products, coupled_blocks(): jnp.einsum('akplie,akqpml->aqime', x, right, preferred_element_type=f32)  3.25 us
    reduce_sum x1, other arithmetic, make_kernel(): jnp.sum(jnp.where(spread_diff[:, :, None] == -offsets, w_absorb, jnp.floa...  1.81 us
    transpose x1, local copies, waits for them, and re-layouts, shards(): green.transpose(3, 0, 2, 1, 4)  1.05 us
    reshape x2, local copies, waits for them, and re-layouts, shards(): return result.reshape(coupled.shape)  0.97 us
  transfers between devices with their start and end apart: 4, of which 2 were waited for; matrix products, arithmetic and copies ran while one was open for 11% of the time, Pallas kernels for 0%

profile of v8, /device:TPU:57, one launch (start us, length us, event | category | flops | bytes accessed | tf_op | source)
XLA Modules:
  0.0 39.1 jit_solution(12377408383036311913)
XLA Ops:
  0.0 1.1 %copy.36 = bf16[12,2,12,2,128]{4,3,2,1,0:T(2,128)(2,1)S(1)} copy(bf16[12,2,12,2,128]{4,3,0,2,1:T(2,128)(2,1)} %bitcast.62) | data formatting | bytes 294912 | tf_op jit(solution)/shard_map/transpose | solution.py:73
  1.1 4.0 %collective-permute-start.1 = (bf16[12,2,24,128]{3,2,1,0:T(8,128)(2,1)S(1)}, bf16[12,2,24,128]{3,2,1,0:T(8,128)(2,1)S(1)}, u32[]{:S(2)}, u32[]{:S(2)}) collective-permute-start(bf16[12,2,24,128]{3,2,1,0:T(8,128)(2,1)S(1)} %bitcast.63), channel_id=1, source_target_pairs={{0,8},{16,24},{32,40},{48,56},{64,72},{80,88},{96,104},{112,120},{... | collective-permute-start | bytes 442376 | tf_op jit(solution)/shard_map/ppermute | solution.py:35
  5.1 0.7 %neg.19 = s32[70]{0:T(128)S(1)} negate(s32[70]{0:T(128)} %param.9) | non-fusion elementwise | flops 70 | bytes 560 | tf_op jit(solution)/shard_map/neg | solution.py:48
  5.9 1.8 %select_reduce_fusion = (f32[224,128]{1,0:T(8,128)S(1)}, f32[224,128]{1,0:T(8,128)S(1)}) fusion(f32[70]{0:T(128)S(1)} %copy-done.2, s32[224,128]{1,0:T(8,128)S(1)} %iota_subtract_fusion, s32[70]{0:T(128)S(1)} %neg.19, f32[70]{0:T(128)S(1)} %copy-done.4, s32[70]{0:T(128)S(1)} %copy-done.3), kind=kLoop, calls=%fused_computation.1 | loop fusion | flops 11984896 | bytes 345184 | tf_op jit(solution)/shard_map/reduce_sum | solution.py:47
  7.7 13.3 %collective-permute-start = (bf16[12,2,24,128]{3,2,1,0:T(8,128)(2,1)S(1)}, bf16[12,2,24,128]{3,2,1,0:T(8,128)(2,1)S(1)}, u32[]{:S(2)}, u32[]{:S(2)}) collective-permute-start(bf16[12,2,24,128]{3,2,1,0:T(8,128)(2,1)S(1)} %bitcast.64), channel_id=1, source_target_pairs={{8,16},{24,32},{40,48},{56,64},{72,80},{88,96},{104,112},{120,128}... | collective-permute-start | bytes 442376 | tf_op jit(solution)/shard_map/ppermute | solution.py:39
  21.0 0.1 copy.55
  21.2 0.2 slice_negate_fusion
  21.4 0.3 copy-done.1
  21.7 0.4 %pad_maximum_fusion = (bf16[2,34,12,12,2]{1,0,3,2,4:T(2,128)(2,1)S(1)}, bf16[2,34,12,12,2]{1,0,3,2,4:T(2,128)(2,1)S(1)}) fusion(bf16[2,34,12,12,1]{1,0,3,2,4:T(2,128)(2,1)S(1)} %fusion.37, bf16[2,34,12,12,1]{1,0,3,2,4:T(2,128)(2,1)S(1)} %get-tuple-element.22, bf16[2,34,12,12,1]{1,0,3,2,4:T(2,128)(2,1)S(1)} %get-tuple-element.20), kind=kLoop, calls=%fused_computation.26 | loop fusion | flops 39168 | bytes 137088 | tf_op jit(solution)/shard_map/stack | solution.py:59
  22.1 0.2 maximum_bitcast_fusion.5
  22.4 0.1 copy.33
  22.5 0.1 copy.34
  22.6 0.5 %maximum_bitcast_fusion.3 = bf16[2,34,2,2,12,12,1]{1,0,5,4,3,2,6:T(2,128)(2,1)S(1)} fusion(bf16[2,34,1,2,12,12]{1,0,5,4,3,2:T(2,128)(2,1)S(1)} %maximum_bitcast_fusion.5, bf16[2,34,1,2,12,12]{1,0,5,4,3,2:T(2,128)(2,1)S(1)} %bitcast.61), kind=kLoop, calls=%fused_computation.23 | loop fusion | flops 39168 | bytes 156672 | tf_op jit(solution)/shard_map/stack | solution.py:64
  23.1 1.1 %collective-permute-done = bf16[12,2,24,128]{3,2,1,0:T(8,128)(2,1)S(1)} collective-permute-done((bf16[12,2,24,128]{3,2,1,0:T(8,128)(2,1)S(1)}, bf16[12,2,24,128]{3,2,1,0:T(8,128)(2,1)S(1)}, u32[]{:S(2)}, u32[]{:S(2)}) %collective-permute-start) | collective-permute-done | bytes 147488 | tf_op jit(solution)/shard_map/ppermute | solution.py:39
  24.3 3.2 %fusion.9 = f32[2,2,12,12,128]{4,3,2,1,0:T(8,128)S(1)} fusion(bf16[2,34,6]{1,2,0:T(8,128)(2,1)S(1)} %fusion.33, bf16[12,2,24,128]{3,2,1,0:T(8,128)(2,1)S(1)} %get-tuple-element.14, bf16[12,2,24,128]{3,2,1,0:T(8,128)(2,1)S(1)} %bitcast.65, bf16[12,2,24,128]{3,2,1,0:T(8,128)(2,1)S(1)} %get-tuple-element.13, ...), kind=kOutput, calls=%fused_computation.8 | convolution fusion | flops 847081728 | bytes 894768 | tf_op jit(solution)/shard_map/akplie,akqpml->aqime/dot_general | solution.py:65
  27.7 0.2 select_n.72
  27.9 0.2 select_n.74
  28.1 3.4 %collective-permute-start.3 = (bf16[216,128]{1,0:T(8,128)(2,1)S(1)}, bf16[216,128]{1,0:T(8,128)(2,1)S(1)}, u32[]{:S(2)}, u32[]{:S(2)}) collective-permute-start(bf16[216,128]{1,0:T(8,128)(2,1)S(1)} %select_n.74), channel_id=1, source_target_pairs={{0,1},{2,3},{4,5},{6,7},{1,0},{3,2},{5,4},{7,6},{8,9},{10,11},{12,... | collective-permute-start | bytes 165896 | tf_op jit(solution)/shard_map/ppermute | solution.py:35
  31.5 3.0 %collective-permute-start.2 = (bf16[216,128]{1,0:T(8,128)(2,1)S(1)}, bf16[216,128]{1,0:T(8,128)(2,1)S(1)}, u32[]{:S(2)}, u32[]{:S(2)}) collective-permute-start(bf16[216,128]{1,0:T(8,128)(2,1)S(1)} %select_n.72), channel_id=1, source_target_pairs={{1,2},{3,4},{5,6},{2,1},{4,3},{6,5},{9,10},{11,12},{13,14},{10,9},... | collective-permute-start | bytes 165896 | tf_op jit(solution)/shard_map/ppermute | solution.py:39
  34.6 2.4 %collective-permute-done.2 = bf16[216,128]{1,0:T(8,128)(2,1)S(1)} collective-permute-done((bf16[216,128]{1,0:T(8,128)(2,1)S(1)}, bf16[216,128]{1,0:T(8,128)(2,1)S(1)}, u32[]{:S(2)}, u32[]{:S(2)}) %collective-permute-start.2) | collective-permute-done | bytes 55328 | tf_op jit(solution)/shard_map/ppermute | solution.py:39
  37.0 0.1 reshape.70
  37.2 0.1 reshape.71
  37.3 0.7 %fusion.18 = f32[576,128]{1,0:T(8,128)S(1)} fusion(f32[224,128]{1,0:T(8,128)S(1)} %add.19, f32[576,48]{1,0:T(8,128)S(1)} %reshape.71, f32[576,128]{1,0:T(8,128)S(1)} %reshape.68, f32[576,48]{1,0:T(8,128)S(1)} %reshape.70), kind=kOutput, calls=%fused_computation.11 | convolution fusion | flops 198438912 | bytes 925696 | tf_op jit(solution)/shard_map/dot_general | solution.py:98
  38.1 0.9 %copy.38 = f32[2,2,12,12,128]{4,1,3,2,0:T(2,128)} copy(f32[2,2,12,12,128]{4,3,2,1,0:T(8,128)S(1)} %reshape.69) | data formatting | bytes 589824 | tf_op jit(solution)/shard_map/reshape | solution.py:101
  (23 shorter events, 0.4 us)
Async XLA Ops:
  0.0 5.8 %copy-start.3 = (s32[70]{0:T(128)S(1)}, s32[70]{0:T(128)}, u32[]{:S(2)}) copy-start(s32[70]{0:T(128)} %param.9) | copy-start | bytes 844
  0.0 5.9 %copy-start.2 = (f32[70]{0:T(128)S(1)}, f32[70]{0:T(128)}, u32[]{:S(2)}) copy-start(f32[70]{0:T(128)} %param.11) | copy-start | bytes 844
  0.0 5.9 %copy-start.4 = (f32[70]{0:T(128)S(1)}, f32[70]{0:T(128)}, u32[]{:S(2)}) copy-start(f32[70]{0:T(128)} %param.10) | copy-start | bytes 844
  1.1 23.2 %collective-permute-start.1 = (bf16[12,2,24,128]{3,2,1,0:T(8,128)(2,1)S(1)}, bf16[12,2,24,128]{3,2,1,0:T(8,128)(2,1)S(1)}, u32[]{:S(2)}, u32[]{:S(2)}) collective-permute-start(bf16[12,2,24,128]{3,2,1,0:T(8,128)(2,1)S(1)} %bitcast.63), channel_id=1, source_target_pairs={{0,8},{16,24},{32,40},{48,56},{64,72},{80,88},{96,104},{112,120},{... | collective-permute-start | bytes 442376 | tf_op jit(solution)/shard_map/ppermute | solution.py:35
  5.7 15.3 %copy-start = (bf16[2,34,2,12,12]{1,2,4,3,0:T(2,128)(2,1)S(1)}, bf16[2,34,2,12,12]{1,2,4,3,0:T(2,128)(2,1)}, u32[]{:S(2)}) copy-start(bf16[2,34,2,12,12]{1,2,4,3,0:T(2,128)(2,1)} %param.7) | copy-start | bytes 117508
  7.7 16.5 %collective-permute-start = (bf16[12,2,24,128]{3,2,1,0:T(8,128)(2,1)S(1)}, bf16[12,2,24,128]{3,2,1,0:T(8,128)(2,1)S(1)}, u32[]{:S(2)}, u32[]{:S(2)}) collective-permute-start(bf16[12,2,24,128]{3,2,1,0:T(8,128)(2,1)S(1)} %bitcast.64), channel_id=1, source_target_pairs={{8,16},{24,32},{40,48},{56,64},{72,80},{88,96},{104,112},{120,128}... | collective-permute-start | bytes 442376 | tf_op jit(solution)/shard_map/ppermute | solution.py:39
  21.0 0.7 %copy-start.1 = (s32[2,34]{1,0:T(2,128)S(1)}, s32[2,34]{1,0:T(2,128)}, u32[]{:S(2)}) copy-start(s32[2,34]{1,0:T(2,128)} %param.8) | copy-start | bytes 820
  28.1 6.5 %collective-permute-start.3 = (bf16[216,128]{1,0:T(8,128)(2,1)S(1)}, bf16[216,128]{1,0:T(8,128)(2,1)S(1)}, u32[]{:S(2)}, u32[]{:S(2)}) collective-permute-start(bf16[216,128]{1,0:T(8,128)(2,1)S(1)} %select_n.74), channel_id=1, source_target_pairs={{0,1},{2,3},{4,5},{6,7},{1,0},{3,2},{5,4},{7,6},{8,9},{10,11},{12,... | collective-permute-start | bytes 165896 | tf_op jit(solution)/shard_map/ppermute | solution.py:35
  31.5 5.5 %collective-permute-start.2 = (bf16[216,128]{1,0:T(8,128)(2,1)S(1)}, bf16[216,128]{1,0:T(8,128)(2,1)S(1)}, u32[]{:S(2)}, u32[]{:S(2)}) collective-permute-start(bf16[216,128]{1,0:T(8,128)(2,1)S(1)} %select_n.72), channel_id=1, source_target_pairs={{1,2},{3,4},{5,6},{2,1},{4,3},{6,5},{9,10},{11,12},{13,14},{10,9},... | collective-permute-start | bytes 165896 | tf_op jit(solution)/shard_map/ppermute | solution.py:39

commit v9 on v7

--- a/solution.py
+++ b/solution.py
@@ -4,37 +4,19 @@
 from jax.sharding import PartitionSpec as P
 
 
-def extended(cells, sides, width):
-    for axis, dim in sides:
-        count = lax.axis_size(axis)
-        even = lax.axis_index(axis) % 2 == 0
-        head = lax.slice_in_dim(cells, 0, width, axis=dim)
-        tail = lax.slice_in_dim(cells, cells.shape[dim] - width, cells.shape[dim], axis=dim)
-        edges = {
-            parity: [(i, i + 1) for i in range(parity, count - 1, 2)]
-            + [(i + 1, i) for i in range(parity, count - 1, 2)]
-            for parity in (0, 1)
-        }
-        from_even = lax.ppermute(jnp.where(even, tail, head), axis, edges[0])
-        from_odd = lax.ppermute(jnp.where(even, head, tail), axis, edges[1])
-        cells = jnp.concatenate(
-            [jnp.where(even, from_odd, from_even), cells, jnp.where(even, from_even, from_odd)],
-            axis=dim,
-        )
-    return cells
-
-
 def swapped(head, tail, axis):
     count = lax.axis_size(axis)
-    even = lax.axis_index(axis) % 2 == 0
-    edges = {
-        parity: [(i, i + 1) for i in range(parity, count - 1, 2)]
-        + [(i + 1, i) for i in range(parity, count - 1, 2)]
-        for parity in (0, 1)
-    }
+    index = lax.axis_index(axis)
+    even = index % 2 == 0
+    pairs = {parity: [(i, (i + 1) % count) for i in range(parity, count - 1 + parity, 2)] for parity in (0, 1)}
+    edges = {parity: pairs[parity] + [(b, a) for a, b in pairs[parity]] for parity in (0, 1)}
     from_even = lax.ppermute(jnp.where(even, tail, head), axis, edges[0])
     from_odd = lax.ppermute(jnp.where(even, head, tail), axis, edges[1])
-    return jnp.where(even, from_odd, from_even), jnp.where(even, from_even, from_odd)
+    lower = jnp.where(even, from_odd, from_even)
+    upper = jnp.where(even, from_even, from_odd)
+    lower = jnp.where(index == 0, jnp.zeros_like(lower), lower)
+    upper = jnp.where(index == count - 1, jnp.zeros_like(upper), upper)
+    return lower, upper
 
 
 def make_kernel(spread_diff, offsets, w_emit, w_absorb):
@@ -68,7 +50,8 @@
     points = green.shape[-1]
     reach = points * 3 // 8
     merged = green.transpose(3, 0, 2, 1, 4).reshape(green.shape[3], atoms_here, -1, points)
-    window = extended(merged, (("atom", 1),), atoms_here)
+    before, after = swapped(merged, merged, "atom")
+    window = jnp.concatenate([before, merged, after], axis=1)
     local_ids = neighbours - (lax.axis_index("atom") - 1) * atoms_here
     extent = points + 2 * reach
     spread_diff = (

time: 36.6 us -> 39.5 us (1.079)
  the two profiles are of different devices: /device:TPU:57 before, /device:TPU:1 now
where the time goes in v9:
time: 39.5 us; the launch traced here: 39.3 us
  starting transfers between devices  26.7 us (68%)
  matrix products  3.97 us (10%)
  other arithmetic  3.48 us (9%)
  local copies, waits for them, and re-layouts  3.34 us (8%)
  waiting for transfers between devices  1.48 us (4%)
    ppermute x2, starting transfers between devices, swapped(): from_odd = lax.ppermute(jnp.where(even, head, tail), axis, edges[1])  22.8 us
    ppermute x2, starting transfers between devices, swapped(): from_even = lax.ppermute(jnp.where(even, tail, head), axis, edges[0])  3.84 us
    dot_general x1, matrix products, coupled_blocks(): jnp.einsum('akplie,akqpml->aqime', x, right, preferred_element_type=f32)  3.25 us
    reduce_sum x1, other arithmetic, make_kernel(): jnp.sum(jnp.where(spread_diff[:, :, None] == -offsets, w_absorb, jnp.floa...  1.81 us
    ppermute x2, waiting for transfers between devices, swapped(): from_even = lax.ppermute(jnp.where(even, tail, head), axis, edges[0])  1.47 us
    transpose x1, local copies, waits for them, and re-layouts, shards(): green.transpose(3, 0, 2, 1, 4)  1.05 us
    reshape x2, local copies, waits for them, and re-layouts, shards(): return result.reshape(coupled.shape)  0.97 us
  transfers between devices with their start and end apart: 4, of which 2 were waited for; matrix products, arithmetic and copies ran while one was open for 10% of the time, Pallas kernels for 0%

profile of v9, /device:TPU:1, one launch (start us, length us, event | category | flops | bytes accessed | tf_op | source)
XLA Modules:
  0.0 39.3 jit_solution(7559734861045992931)
XLA Ops:
  0.0 1.0 %copy.36 = bf16[12,2,12,2,128]{4,3,2,1,0:T(2,128)(2,1)S(1)} copy(bf16[12,2,12,2,128]{4,3,0,2,1:T(2,128)(2,1)} %bitcast.62) | data formatting | bytes 294912 | tf_op jit(solution)/shard_map/transpose | solution.py:52
  1.1 18.0 %collective-permute-start = (bf16[12,2,24,128]{3,2,1,0:T(8,128)(2,1)S(1)}, bf16[12,2,24,128]{3,2,1,0:T(8,128)(2,1)S(1)}, u32[]{:S(2)}, u32[]{:S(2)}) collective-permute-start(bf16[12,2,24,128]{3,2,1,0:T(8,128)(2,1)S(1)} %bitcast.63), channel_id=1, source_target_pairs={{8,16},{24,32},{40,48},{56,64},{72,80},{88,96},{104,112},{120,128}... | collective-permute-start | bytes 442376 | tf_op jit(solution)/shard_map/ppermute | solution.py:14
  19.1 1.9 %collective-permute-start.1 = (bf16[12,2,24,128]{3,2,1,0:T(8,128)(2,1)S(1)}, bf16[12,2,24,128]{3,2,1,0:T(8,128)(2,1)S(1)}, u32[]{:S(2)}, u32[]{:S(2)}) collective-permute-start(bf16[12,2,24,128]{3,2,1,0:T(8,128)(2,1)S(1)} %bitcast.64), channel_id=1, source_target_pairs={{0,8},{16,24},{32,40},{48,56},{64,72},{80,88},{96,104},{112,120},{... | collective-permute-start | bytes 442376 | tf_op jit(solution)/shard_map/ppermute | solution.py:13
  21.0 0.1 copy.55
  21.2 0.2 slice_negate_fusion
  21.5 0.2 copy-done.1
  21.8 0.4 %pad_maximum_fusion = (bf16[2,34,12,12,2]{1,0,3,2,4:T(2,128)(2,1)S(1)}, bf16[2,34,12,12,2]{1,0,3,2,4:T(2,128)(2,1)S(1)}) fusion(bf16[2,34,12,12,1]{1,0,3,2,4:T(2,128)(2,1)S(1)} %fusion.37, bf16[2,34,12,12,1]{1,0,3,2,4:T(2,128)(2,1)S(1)} %get-tuple-element.20, bf16[2,34,12,12,1]{1,0,3,2,4:T(2,128)(2,1)S(1)} %get-tuple-element.18), kind=kLoop, calls=%fused_computation.26 | loop fusion | flops 39168 | bytes 137088 | tf_op jit(solution)/shard_map/stack | solution.py:38
  22.3 1.8 %select_reduce_fusion = (f32[224,128]{1,0:T(8,128)S(1)}, f32[224,128]{1,0:T(8,128)S(1)}) fusion(f32[70]{0:T(128)S(1)} %copy-done.2, s32[224,128]{1,0:T(8,128)S(1)} %iota_subtract_fusion, s32[70]{0:T(128)S(1)} %neg.19, f32[70]{0:T(128)S(1)} %copy-done.4, s32[70]{0:T(128)S(1)} %copy-done.3), kind=kLoop, calls=%fused_computation.1 | loop fusion | flops 11984896 | bytes 345184 | tf_op jit(solution)/shard_map/reduce_sum | solution.py:26
  24.1 0.2 maximum_bitcast_fusion.5
  24.4 0.1 copy.33
  24.5 0.1 copy.34
  24.6 0.5 %maximum_bitcast_fusion.3 = bf16[2,34,2,2,12,12,1]{1,0,5,4,3,2,6:T(2,128)(2,1)S(1)} fusion(bf16[2,34,1,2,12,12]{1,0,5,4,3,2:T(2,128)(2,1)S(1)} %maximum_bitcast_fusion.5, bf16[2,34,1,2,12,12]{1,0,5,4,3,2:T(2,128)(2,1)S(1)} %bitcast.61), kind=kLoop, calls=%fused_computation.23 | loop fusion | flops 39168 | bytes 156672 | tf_op jit(solution)/shard_map/stack | solution.py:43
  25.2 0.3 collective-permute-done.1
  25.5 3.2 %fusion.9 = f32[2,2,12,12,128]{4,3,2,1,0:T(8,128)S(1)} fusion(bf16[2,34,6]{1,2,0:T(8,128)(2,1)S(1)} %fusion.33, bf16[12,2,24,128]{3,2,1,0:T(8,128)(2,1)S(1)} %get-tuple-element.12, bf16[12,2,24,128]{3,2,1,0:T(8,128)(2,1)S(1)} %bitcast.65, bf16[12,2,24,128]{3,2,1,0:T(8,128)(2,1)S(1)} %get-tuple-element.11, ...), kind=kOutput, calls=%fused_computation.8 | convolution fusion | flops 847081728 | bytes 894768 | tf_op jit(solution)/shard_map/akplie,akqpml->aqime/dot_general | solution.py:44
  28.8 0.1 broadcast_select_fusion.1
  28.9 0.2 select_n.101
  29.1 4.8 %collective-permute-start.2 = (bf16[216,128]{1,0:T(8,128)(2,1)S(1)}, bf16[216,128]{1,0:T(8,128)(2,1)S(1)}, u32[]{:S(2)}, u32[]{:S(2)}) collective-permute-start(bf16[216,128]{1,0:T(8,128)(2,1)S(1)} %select_n.101), channel_id=1, source_target_pairs={{1,2},{3,4},{5,6},{7,0},{2,1},{4,3},{6,5},{0,7},{9,10},{11,12},{13... | collective-permute-start | bytes 165896 | tf_op jit(solution)/shard_map/ppermute | solution.py:14
  33.9 0.2 select_n.103
  34.1 1.9 %collective-permute-start.3 = (bf16[216,128]{1,0:T(8,128)(2,1)S(1)}, bf16[216,128]{1,0:T(8,128)(2,1)S(1)}, u32[]{:S(2)}, u32[]{:S(2)}) collective-permute-start(bf16[216,128]{1,0:T(8,128)(2,1)S(1)} %select_n.103), channel_id=1, source_target_pairs={{0,1},{2,3},{4,5},{6,7},{1,0},{3,2},{5,4},{7,6},{8,9},{10,11},{12,... | collective-permute-start | bytes 165896 | tf_op jit(solution)/shard_map/ppermute | solution.py:13
  36.1 1.2 %collective-permute-done.3 = bf16[216,128]{1,0:T(8,128)(2,1)S(1)} collective-permute-done((bf16[216,128]{1,0:T(8,128)(2,1)S(1)}, bf16[216,128]{1,0:T(8,128)(2,1)S(1)}, u32[]{:S(2)}, u32[]{:S(2)}) %collective-permute-start.3) | collective-permute-done | bytes 55328 | tf_op jit(solution)/shard_map/ppermute | solution.py:13
  37.3 0.1 reshape.70
  37.4 0.1 reshape.71
  37.6 0.7 %fusion.18 = f32[576,128]{1,0:T(8,128)S(1)} fusion(f32[224,128]{1,0:T(8,128)S(1)} %add.19, f32[576,48]{1,0:T(8,128)S(1)} %reshape.71, f32[576,128]{1,0:T(8,128)S(1)} %reshape.68, f32[576,48]{1,0:T(8,128)S(1)} %reshape.70), kind=kOutput, calls=%fused_computation.11 | convolution fusion | flops 198438912 | bytes 925696 | tf_op jit(solution)/shard_map/dot_general | solution.py:77
  38.4 0.9 %copy.38 = f32[2,2,12,12,128]{4,1,3,2,0:T(2,128)} copy(f32[2,2,12,12,128]{4,3,2,1,0:T(8,128)S(1)} %reshape.69) | data formatting | bytes 589824 | tf_op jit(solution)/shard_map/reshape | solution.py:80
  (23 shorter events, 0.3 us)
Async XLA Ops:
  0.0 21.0 %copy-start = (bf16[2,34,2,12,12]{1,2,4,3,0:T(2,128)(2,1)S(1)}, bf16[2,34,2,12,12]{1,2,4,3,0:T(2,128)(2,1)}, u32[]{:S(2)}) copy-start(bf16[2,34,2,12,12]{1,2,4,3,0:T(2,128)(2,1)} %param.7) | copy-start | bytes 117508
  1.1 24.1 %collective-permute-start = (bf16[12,2,24,128]{3,2,1,0:T(8,128)(2,1)S(1)}, bf16[12,2,24,128]{3,2,1,0:T(8,128)(2,1)S(1)}, u32[]{:S(2)}, u32[]{:S(2)}) collective-permute-start(bf16[12,2,24,128]{3,2,1,0:T(8,128)(2,1)S(1)} %bitcast.63), channel_id=1, source_target_pairs={{8,16},{24,32},{40,48},{56,64},{72,80},{88,96},{104,112},{120,128}... | collective-permute-start | bytes 442376 | tf_op jit(solution)/shard_map/ppermute | solution.py:14
  19.1 6.3 %collective-permute-start.1 = (bf16[12,2,24,128]{3,2,1,0:T(8,128)(2,1)S(1)}, bf16[12,2,24,128]{3,2,1,0:T(8,128)(2,1)S(1)}, u32[]{:S(2)}, u32[]{:S(2)}) collective-permute-start(bf16[12,2,24,128]{3,2,1,0:T(8,128)(2,1)S(1)} %bitcast.64), channel_id=1, source_target_pairs={{0,8},{16,24},{32,40},{48,56},{64,72},{80,88},{96,104},{112,120},{... | collective-permute-start | bytes 442376 | tf_op jit(solution)/shard_map/ppermute | solution.py:13
  21.0 0.7 %copy-start.1 = (s32[2,34]{1,0:T(2,128)S(1)}, s32[2,34]{1,0:T(2,128)}, u32[]{:S(2)}) copy-start(s32[2,34]{1,0:T(2,128)} %param.8) | copy-start | bytes 820
  21.2 0.7 %copy-start.3 = (s32[70]{0:T(128)S(1)}, s32[70]{0:T(128)}, u32[]{:S(2)}) copy-start(s32[70]{0:T(128)} %param.9) | copy-start | bytes 844
  21.4 0.9 %copy-start.2 = (f32[70]{0:T(128)S(1)}, f32[70]{0:T(128)}, u32[]{:S(2)}) copy-start(f32[70]{0:T(128)} %param.11) | copy-start | bytes 844
  21.4 0.9 %copy-start.4 = (f32[70]{0:T(128)S(1)}, f32[70]{0:T(128)}, u32[]{:S(2)}) copy-start(f32[70]{0:T(128)} %param.10) | copy-start | bytes 844
  29.1 7.0 %collective-permute-start.2 = (bf16[216,128]{1,0:T(8,128)(2,1)S(1)}, bf16[216,128]{1,0:T(8,128)(2,1)S(1)}, u32[]{:S(2)}, u32[]{:S(2)}) collective-permute-start(bf16[216,128]{1,0:T(8,128)(2,1)S(1)} %select_n.101), channel_id=1, source_target_pairs={{1,2},{3,4},{5,6},{7,0},{2,1},{4,3},{6,5},{0,7},{9,10},{11,12},{13... | collective-permute-start | bytes 165896 | tf_op jit(solution)/shard_map/ppermute | solution.py:14
  34.1 3.1 %collective-permute-start.3 = (bf16[216,128]{1,0:T(8,128)(2,1)S(1)}, bf16[216,128]{1,0:T(8,128)(2,1)S(1)}, u32[]{:S(2)}, u32[]{:S(2)}) collective-permute-start(bf16[216,128]{1,0:T(8,128)(2,1)S(1)} %select_n.103), channel_id=1, source_target_pairs={{0,1},{2,3},{4,5},{6,7},{1,0},{3,2},{5,4},{7,6},{8,9},{10,11},{12,... | collective-permute-start | bytes 165896 | tf_op jit(solution)/shard_map/ppermute | solution.py:13

commit v10 on v7

--- a/solution.py
+++ b/solution.py
@@ -90,9 +90,12 @@
         return part.reshape(rows, reach).astype(jnp.float32)
 
     lower, upper = swapped(pack(flat[:, :reach]), pack(flat[:, points - reach:]), "energy")
-    widened = jnp.concatenate([unpack(lower), flat, unpack(upper)], axis=1)
-    result = jnp.dot(
-        widened.reshape(-1, extent), kernel, precision=hi, preferred_element_type=jnp.float32
+    result = jnp.dot(flat, kernel[reach:reach + points], precision=hi, preferred_element_type=jnp.float32)
+    result = result + jnp.dot(
+        unpack(lower), kernel[:reach], precision=hi, preferred_element_type=jnp.float32
+    )
+    result = result + jnp.dot(
+        unpack(upper), kernel[reach + points:], precision=hi, preferred_element_type=jnp.float32
     )
     return result.reshape(coupled.shape)
 

time: 36.6 us -> 36.4 us (level)
  waiting for transfers between devices: 1.49 us -> 1.09 us
    ppermute x1, waiting for transfers between devices: 1.19 us -> 0.8 us  [swapped(): from_even = lax.ppermute(jnp.where(even, tail, head), axis, edges[0])]
    dot_general x1 -> x3, matrix products: 0.73 us -> 0.9 us  [the longest x1 0.39 us: shards(): jnp.dot(flat, kernel[reach:reach + points], precision=hi, preferred_eleme...]
  transfers between devices with their start and end apart: 4 -> 4, of which waited for: 2 -> 2; matrix products, arithmetic and copies ran while one was open for 11% -> 12% of each run, Pallas kernels for 0% -> 0%
where the time goes in v10:
time: 36.4 us; the launch traced here: 36.2 us
  starting transfers between devices  23.7 us (65%)
  matrix products  4.15 us (11%)
  other arithmetic  3.48 us (10%)
  local copies, waits for them, and re-layouts  3.38 us (9%)
  waiting for transfers between devices  1.09 us (3%)
    ppermute x1, starting transfers between devices, extended(): from_odd = lax.ppermute(jnp.where(even, head, tail), axis, edges[1])  15.1 us
    ppermute x1, starting transfers between devices, swapped(): from_odd = lax.ppermute(jnp.where(even, head, tail), axis, edges[1])  4.82 us
    dot_general x1, matrix products, coupled_blocks(): jnp.einsum('akplie,akqpml->aqime', x, right, preferred_element_type=f32)  3.25 us
    ppermute x1, starting transfers between devices, extended(): from_even = lax.ppermute(jnp.where(even, tail, head), axis, edges[0])  1.92 us
    ppermute x1, starting transfers between devices, swapped(): from_even = lax.ppermute(jnp.where(even, tail, head), axis, edges[0])  1.92 us
    reduce_sum x1, other arithmetic, make_kernel(): jnp.sum(jnp.where(spread_diff[:, :, None] == -offsets, w_absorb, jnp.floa...  1.81 us
    transpose x1, local copies, waits for them, and re-layouts, shards(): green.transpose(3, 0, 2, 1, 4)  1.05 us
    reshape x2, local copies, waits for them, and re-layouts, shards(): return result.reshape(coupled.shape)  0.97 us
  transfers between devices with their start and end apart: 4, of which 2 were waited for; matrix products, arithmetic and copies ran while one was open for 12% of the time, Pallas kernels for 0%

profile of v10, /device:TPU:57, one launch (start us, length us, event | category | flops | bytes accessed | tf_op | source)
XLA Modules:
  0.0 36.2 jit_solution(1631608100192710822)
XLA Ops:
  0.0 1.0 %copy.36 = bf16[12,2,12,2,128]{4,3,2,1,0:T(2,128)(2,1)S(1)} copy(bf16[12,2,12,2,128]{4,3,0,2,1:T(2,128)(2,1)} %bitcast.64) | data formatting | bytes 294912 | tf_op jit(solution)/shard_map/transpose | solution.py:70
  1.1 15.1 %collective-permute-start = (bf16[12,2,24,128]{3,2,1,0:T(8,128)(2,1)S(1)}, bf16[12,2,24,128]{3,2,1,0:T(8,128)(2,1)S(1)}, u32[]{:S(2)}, u32[]{:S(2)}) collective-permute-start(bf16[12,2,24,128]{3,2,1,0:T(8,128)(2,1)S(1)} %bitcast.65), channel_id=1, source_target_pairs={{8,16},{24,32},{40,48},{56,64},{72,80},{88,96},{104,112},{120,128}... | collective-permute-start | bytes 442376 | tf_op jit(solution)/shard_map/ppermute | solution.py:19
  16.2 1.9 %collective-permute-start.1 = (bf16[12,2,24,128]{3,2,1,0:T(8,128)(2,1)S(1)}, bf16[12,2,24,128]{3,2,1,0:T(8,128)(2,1)S(1)}, u32[]{:S(2)}, u32[]{:S(2)}) collective-permute-start(bf16[12,2,24,128]{3,2,1,0:T(8,128)(2,1)S(1)} %bitcast.66), channel_id=1, source_target_pairs={{0,8},{16,24},{32,40},{48,56},{64,72},{80,88},{96,104},{112,120},{... | collective-permute-start | bytes 442376 | tf_op jit(solution)/shard_map/ppermute | solution.py:18
  18.1 0.1 copy.55
  18.2 0.2 slice_negate_fusion
  18.5 0.2 copy-done.1
  18.9 0.4 %pad_maximum_fusion = (bf16[2,34,12,12,2]{1,0,3,2,4:T(2,128)(2,1)S(1)}, bf16[2,34,12,12,2]{1,0,3,2,4:T(2,128)(2,1)S(1)}) fusion(bf16[2,34,12,12,1]{1,0,3,2,4:T(2,128)(2,1)S(1)} %fusion.34, bf16[2,34,12,12,1]{1,0,3,2,4:T(2,128)(2,1)S(1)} %get-tuple-element.20, bf16[2,34,12,12,1]{1,0,3,2,4:T(2,128)(2,1)S(1)} %get-tuple-element.18), kind=kLoop, calls=%fused_computation.22 | loop fusion | flops 39168 | bytes 137088 | tf_op jit(solution)/shard_map/stack | solution.py:56
  19.3 1.8 %select_reduce_fusion = (f32[224,128]{1,0:T(8,128)S(1)}, f32[224,128]{1,0:T(8,128)S(1)}) fusion(f32[70]{0:T(128)S(1)} %copy-done.2, s32[224,128]{1,0:T(8,128)S(1)} %iota_subtract_fusion, s32[70]{0:T(128)S(1)} %neg.19, f32[70]{0:T(128)S(1)} %copy-done.4, s32[70]{0:T(128)S(1)} %copy-done.3), kind=kLoop, calls=%fused_computation.1 | loop fusion | flops 11984896 | bytes 345184 | tf_op jit(solution)/shard_map/reduce_sum | solution.py:44
  21.1 0.2 maximum_bitcast_fusion.5
  21.4 0.1 copy.33
  21.7 0.5 %maximum_bitcast_fusion.3 = bf16[2,34,2,2,12,12,1]{1,0,5,4,3,2,6:T(2,128)(2,1)S(1)} fusion(bf16[2,34,1,2,12,12]{1,0,5,4,3,2:T(2,128)(2,1)S(1)} %maximum_bitcast_fusion.5, bf16[2,34,1,2,12,12]{1,0,5,4,3,2:T(2,128)(2,1)S(1)} %bitcast.63), kind=kLoop, calls=%fused_computation.19 | loop fusion | flops 39168 | bytes 156672 | tf_op jit(solution)/shard_map/stack | solution.py:61
  22.2 0.3 collective-permute-done.1
  22.5 3.2 %fusion.9 = f32[2,2,12,12,128]{4,3,2,1,0:T(8,128)S(1)} fusion(bf16[2,34,6]{1,2,0:T(8,128)(2,1)S(1)} %fusion.31, bf16[12,2,24,128]{3,2,1,0:T(8,128)(2,1)S(1)} %get-tuple-element.12, bf16[12,2,24,128]{3,2,1,0:T(8,128)(2,1)S(1)} %bitcast.67, bf16[12,2,24,128]{3,2,1,0:T(8,128)(2,1)S(1)} %get-tuple-element.11, ...), kind=kOutput, calls=%fused_computation.8 | convolution fusion | flops 847081728 | bytes 894768 | tf_op jit(solution)/shard_map/akplie,akqpml->aqime/dot_general | solution.py:62
  26.0 0.2 select_n.72
  26.2 4.8 %collective-permute-start.2 = (bf16[216,128]{1,0:T(8,128)(2,1)S(1)}, bf16[216,128]{1,0:T(8,128)(2,1)S(1)}, u32[]{:S(2)}, u32[]{:S(2)}) collective-permute-start(bf16[216,128]{1,0:T(8,128)(2,1)S(1)} %select_n.72), channel_id=1, source_target_pairs={{1,2},{3,4},{5,6},{2,1},{4,3},{6,5},{9,10},{11,12},{13,14},{10,9},... | collective-permute-start | bytes 165896 | tf_op jit(solution)/shard_map/ppermute | solution.py:36
  31.0 0.2 select_n.74
  31.2 1.9 %collective-permute-start.3 = (bf16[216,128]{1,0:T(8,128)(2,1)S(1)}, bf16[216,128]{1,0:T(8,128)(2,1)S(1)}, u32[]{:S(2)}, u32[]{:S(2)}) collective-permute-start(bf16[216,128]{1,0:T(8,128)(2,1)S(1)} %select_n.74), channel_id=1, source_target_pairs={{0,1},{2,3},{4,5},{6,7},{1,0},{3,2},{5,4},{7,6},{8,9},{10,11},{12,... | collective-permute-start | bytes 165896 | tf_op jit(solution)/shard_map/ppermute | solution.py:35
  33.1 0.4 %fusion.27 = f32[576,128]{1,0:T(8,128)S(1)} fusion(f32[576,128]{1,0:T(8,128)S(1)} %reshape.68, f32[224,128]{1,0:T(8,128)S(1)} %add.24), kind=kOutput, calls=%fused_computation.29 | convolution fusion | flops 113246208 | bytes 655360 | tf_op jit(solution)/shard_map/dot_general | solution.py:93
  33.5 0.8 %collective-permute-done.3 = bf16[216,128]{1,0:T(8,128)(2,1)S(1)} collective-permute-done((bf16[216,128]{1,0:T(8,128)(2,1)S(1)}, bf16[216,128]{1,0:T(8,128)(2,1)S(1)}, u32[]{:S(2)}, u32[]{:S(2)}) %collective-permute-start.3) | collective-permute-done | bytes 55328 | tf_op jit(solution)/shard_map/ppermute | solution.py:35
  34.3 0.2 reshape.69
  34.5 0.2 reshape.70
  34.7 0.3 convolution_add_fusion.1
  35.0 0.3 convolution_add_fusion
  35.3 0.9 %copy.38 = f32[2,2,12,12,128]{4,1,3,2,0:T(2,128)} copy(f32[2,2,12,12,128]{4,3,2,1,0:T(8,128)S(1)} %reshape.71) | data formatting | bytes 589824 | tf_op jit(solution)/shard_map/reshape | solution.py:100
  (25 shorter events, 0.6 us)
Async XLA Ops:
  0.0 18.1 %copy-start = (bf16[2,34,2,12,12]{1,2,4,3,0:T(2,128)(2,1)S(1)}, bf16[2,34,2,12,12]{1,2,4,3,0:T(2,128)(2,1)}, u32[]{:S(2)}) copy-start(bf16[2,34,2,12,12]{1,2,4,3,0:T(2,128)(2,1)} %param.7) | copy-start | bytes 117508
  1.1 21.2 %collective-permute-start = (bf16[12,2,24,128]{3,2,1,0:T(8,128)(2,1)S(1)}, bf16[12,2,24,128]{3,2,1,0:T(8,128)(2,1)S(1)}, u32[]{:S(2)}, u32[]{:S(2)}) collective-permute-start(bf16[12,2,24,128]{3,2,1,0:T(8,128)(2,1)S(1)} %bitcast.65), channel_id=1, source_target_pairs={{8,16},{24,32},{40,48},{56,64},{72,80},{88,96},{104,112},{120,128}... | collective-permute-start | bytes 442376 | tf_op jit(solution)/shard_map/ppermute | solution.py:19
  16.2 6.3 %collective-permute-start.1 = (bf16[12,2,24,128]{3,2,1,0:T(8,128)(2,1)S(1)}, bf16[12,2,24,128]{3,2,1,0:T(8,128)(2,1)S(1)}, u32[]{:S(2)}, u32[]{:S(2)}) collective-permute-start(bf16[12,2,24,128]{3,2,1,0:T(8,128)(2,1)S(1)} %bitcast.66), channel_id=1, source_target_pairs={{0,8},{16,24},{32,40},{48,56},{64,72},{80,88},{96,104},{112,120},{... | collective-permute-start | bytes 442376 | tf_op jit(solution)/shard_map/ppermute | solution.py:18
  18.1 0.7 %copy-start.1 = (s32[2,34]{1,0:T(2,128)S(1)}, s32[2,34]{1,0:T(2,128)}, u32[]{:S(2)}) copy-start(s32[2,34]{1,0:T(2,128)} %param.8) | copy-start | bytes 820
  18.2 0.7 %copy-start.3 = (s32[70]{0:T(128)S(1)}, s32[70]{0:T(128)}, u32[]{:S(2)}) copy-start(s32[70]{0:T(128)} %param.9) | copy-start | bytes 844
  18.4 0.9 %copy-start.2 = (f32[70]{0:T(128)S(1)}, f32[70]{0:T(128)}, u32[]{:S(2)}) copy-start(f32[70]{0:T(128)} %param.11) | copy-start | bytes 844
  18.4 0.9 %copy-start.4 = (f32[70]{0:T(128)S(1)}, f32[70]{0:T(128)}, u32[]{:S(2)}) copy-start(f32[70]{0:T(128)} %param.10) | copy-start | bytes 844
  26.2 7.3 %collective-permute-start.2 = (bf16[216,128]{1,0:T(8,128)(2,1)S(1)}, bf16[216,128]{1,0:T(8,128)(2,1)S(1)}, u32[]{:S(2)}, u32[]{:S(2)}) collective-permute-start(bf16[216,128]{1,0:T(8,128)(2,1)S(1)} %select_n.72), channel_id=1, source_target_pairs={{1,2},{3,4},{5,6},{2,1},{4,3},{6,5},{9,10},{11,12},{13,14},{10,9},... | collective-permute-start | bytes 165896 | tf_op jit(solution)/shard_map/ppermute | solution.py:36
  31.2 3.1 %collective-permute-start.3 = (bf16[216,128]{1,0:T(8,128)(2,1)S(1)}, bf16[216,128]{1,0:T(8,128)(2,1)S(1)}, u32[]{:S(2)}, u32[]{:S(2)}) collective-permute-start(bf16[216,128]{1,0:T(8,128)(2,1)S(1)} %select_n.74), channel_id=1, source_target_pairs={{0,1},{2,3},{4,5},{6,7},{1,0},{3,2},{5,4},{7,6},{8,9},{10,11},{12,... | collective-permute-start | bytes 165896 | tf_op jit(solution)/shard_map/ppermute | solution.py:35

commit v11 on v10

--- a/solution.py
+++ b/solution.py
@@ -63,7 +63,7 @@
 
 
 def shards(green, coupling, neighbours, offsets, w_emit, w_absorb):
-    hi = lax.Precision.HIGHEST
+    hi = lax.Precision.HIGH
     atoms_here = green.shape[0]
     points = green.shape[-1]
     reach = points * 3 // 8

time: 36.4 us -> 36.3 us (level)
  transfers between devices with their start and end apart: 4 -> 4, of which waited for: 2 -> 2; matrix products, arithmetic and copies ran while one was open for 12% -> 11% of each run, Pallas kernels for 0% -> 0%
where the time goes in v11:
time: 36.3 us; the launch traced here: 36.1 us
  starting transfers between devices  23.7 us (65%)
  matrix products  3.96 us (11%)
  other arithmetic  3.48 us (10%)
  local copies, waits for them, and re-layouts  3.38 us (9%)
  waiting for transfers between devices  1.21 us (3%)
    ppermute x1, starting transfers between devices, extended(): from_odd = lax.ppermute(jnp.where(even, head, tail), axis, edges[1])  15.1 us
    ppermute x1, starting transfers between devices, swapped(): from_odd = lax.ppermute(jnp.where(even, head, tail), axis, edges[1])  4.82 us
    dot_general x1, matrix products, coupled_blocks(): jnp.einsum('akplie,akqpml->aqime', x, right, preferred_element_type=f32)  3.25 us
    ppermute x1, starting transfers between devices, extended(): from_even = lax.ppermute(jnp.where(even, tail, head), axis, edges[0])  1.92 us
    ppermute x1, starting transfers between devices, swapped(): from_even = lax.ppermute(jnp.where(even, tail, head), axis, edges[0])  1.92 us
    reduce_sum x1, other arithmetic, make_kernel(): jnp.sum(jnp.where(spread_diff[:, :, None] == -offsets, w_absorb, jnp.floa...  1.81 us
    transpose x1, local copies, waits for them, and re-layouts, shards(): green.transpose(3, 0, 2, 1, 4)  1.05 us
    reshape x2, local copies, waits for them, and re-layouts, shards(): return result.reshape(coupled.shape)  0.97 us
  transfers between devices with their start and end apart: 4, of which 2 were waited for; matrix products, arithmetic and copies ran while one was open for 11% of the time, Pallas kernels for 0%

profile of v11, /device:TPU:57, one launch (start us, length us, event | category | flops | bytes accessed | tf_op | source)
XLA Modules:
  0.0 36.1 jit_solution(12529065814213976333)
XLA Ops:
  0.0 1.0 %copy.36 = bf16[12,2,12,2,128]{4,3,2,1,0:T(2,128)(2,1)S(1)} copy(bf16[12,2,12,2,128]{4,3,0,2,1:T(2,128)(2,1)} %bitcast.64) | data formatting | bytes 294912 | tf_op jit(solution)/shard_map/transpose | solution.py:70
  1.1 15.1 %collective-permute-start = (bf16[12,2,24,128]{3,2,1,0:T(8,128)(2,1)S(1)}, bf16[12,2,24,128]{3,2,1,0:T(8,128)(2,1)S(1)}, u32[]{:S(2)}, u32[]{:S(2)}) collective-permute-start(bf16[12,2,24,128]{3,2,1,0:T(8,128)(2,1)S(1)} %bitcast.65), channel_id=1, source_target_pairs={{8,16},{24,32},{40,48},{56,64},{72,80},{88,96},{104,112},{120,128}... | collective-permute-start | bytes 442376 | tf_op jit(solution)/shard_map/ppermute | solution.py:19
  16.2 1.9 %collective-permute-start.1 = (bf16[12,2,24,128]{3,2,1,0:T(8,128)(2,1)S(1)}, bf16[12,2,24,128]{3,2,1,0:T(8,128)(2,1)S(1)}, u32[]{:S(2)}, u32[]{:S(2)}) collective-permute-start(bf16[12,2,24,128]{3,2,1,0:T(8,128)(2,1)S(1)} %bitcast.66), channel_id=1, source_target_pairs={{0,8},{16,24},{32,40},{48,56},{64,72},{80,88},{96,104},{112,120},{... | collective-permute-start | bytes 442376 | tf_op jit(solution)/shard_map/ppermute | solution.py:18
  18.1 0.1 copy.55
  18.2 0.2 slice_negate_fusion
  18.5 0.2 copy-done.1
  18.9 0.4 %pad_maximum_fusion = (bf16[2,34,12,12,2]{1,0,3,2,4:T(2,128)(2,1)S(1)}, bf16[2,34,12,12,2]{1,0,3,2,4:T(2,128)(2,1)S(1)}) fusion(bf16[2,34,12,12,1]{1,0,3,2,4:T(2,128)(2,1)S(1)} %fusion.34, bf16[2,34,12,12,1]{1,0,3,2,4:T(2,128)(2,1)S(1)} %get-tuple-element.20, bf16[2,34,12,12,1]{1,0,3,2,4:T(2,128)(2,1)S(1)} %get-tuple-element.18), kind=kLoop, calls=%fused_computation.22 | loop fusion | flops 39168 | bytes 137088 | tf_op jit(solution)/shard_map/stack | solution.py:56
  19.3 1.8 %select_reduce_fusion = (f32[224,128]{1,0:T(8,128)S(1)}, f32[224,128]{1,0:T(8,128)S(1)}) fusion(f32[70]{0:T(128)S(1)} %copy-done.2, s32[224,128]{1,0:T(8,128)S(1)} %iota_subtract_fusion, s32[70]{0:T(128)S(1)} %neg.19, f32[70]{0:T(128)S(1)} %copy-done.4, s32[70]{0:T(128)S(1)} %copy-done.3), kind=kLoop, calls=%fused_computation.1 | loop fusion | flops 11984896 | bytes 345184 | tf_op jit(solution)/shard_map/reduce_sum | solution.py:44
  21.1 0.2 maximum_bitcast_fusion.5
  21.4 0.1 copy.33
  21.7 0.5 %maximum_bitcast_fusion.3 = bf16[2,34,2,2,12,12,1]{1,0,5,4,3,2,6:T(2,128)(2,1)S(1)} fusion(bf16[2,34,1,2,12,12]{1,0,5,4,3,2:T(2,128)(2,1)S(1)} %maximum_bitcast_fusion.5, bf16[2,34,1,2,12,12]{1,0,5,4,3,2:T(2,128)(2,1)S(1)} %bitcast.63), kind=kLoop, calls=%fused_computation.19 | loop fusion | flops 39168 | bytes 156672 | tf_op jit(solution)/shard_map/stack | solution.py:61
  22.2 0.3 collective-permute-done.1
  22.5 3.2 %fusion.9 = f32[2,2,12,12,128]{4,3,2,1,0:T(8,128)S(1)} fusion(bf16[2,34,6]{1,2,0:T(8,128)(2,1)S(1)} %fusion.31, bf16[12,2,24,128]{3,2,1,0:T(8,128)(2,1)S(1)} %get-tuple-element.12, bf16[12,2,24,128]{3,2,1,0:T(8,128)(2,1)S(1)} %bitcast.67, bf16[12,2,24,128]{3,2,1,0:T(8,128)(2,1)S(1)} %get-tuple-element.11, ...), kind=kOutput, calls=%fused_computation.8 | convolution fusion | flops 847081728 | bytes 894768 | tf_op jit(solution)/shard_map/akplie,akqpml->aqime/dot_general | solution.py:62
  26.0 0.2 select_n.72
  26.2 4.8 %collective-permute-start.2 = (bf16[216,128]{1,0:T(8,128)(2,1)S(1)}, bf16[216,128]{1,0:T(8,128)(2,1)S(1)}, u32[]{:S(2)}, u32[]{:S(2)}) collective-permute-start(bf16[216,128]{1,0:T(8,128)(2,1)S(1)} %select_n.72), channel_id=1, source_target_pairs={{1,2},{3,4},{5,6},{2,1},{4,3},{6,5},{9,10},{11,12},{13,14},{10,9},... | collective-permute-start | bytes 165896 | tf_op jit(solution)/shard_map/ppermute | solution.py:36
  31.0 0.2 select_n.74
  31.2 1.9 %collective-permute-start.3 = (bf16[216,128]{1,0:T(8,128)(2,1)S(1)}, bf16[216,128]{1,0:T(8,128)(2,1)S(1)}, u32[]{:S(2)}, u32[]{:S(2)}) collective-permute-start(bf16[216,128]{1,0:T(8,128)(2,1)S(1)} %select_n.74), channel_id=1, source_target_pairs={{0,1},{2,3},{4,5},{6,7},{1,0},{3,2},{5,4},{7,6},{8,9},{10,11},{12,... | collective-permute-start | bytes 165896 | tf_op jit(solution)/shard_map/ppermute | solution.py:35
  33.1 0.3 fusion.27
  33.4 0.9 %collective-permute-done.3 = bf16[216,128]{1,0:T(8,128)(2,1)S(1)} collective-permute-done((bf16[216,128]{1,0:T(8,128)(2,1)S(1)}, bf16[216,128]{1,0:T(8,128)(2,1)S(1)}, u32[]{:S(2)}, u32[]{:S(2)}) %collective-permute-start.3) | collective-permute-done | bytes 55328 | tf_op jit(solution)/shard_map/ppermute | solution.py:35
  34.3 0.2 reshape.69
  34.5 0.2 reshape.70
  34.7 0.2 convolution_add_fusion.1
  34.9 0.2 convolution_add_fusion
  35.2 0.9 %copy.38 = f32[2,2,12,12,128]{4,1,3,2,0:T(2,128)} copy(f32[2,2,12,12,128]{4,3,2,1,0:T(8,128)S(1)} %reshape.71) | data formatting | bytes 589824 | tf_op jit(solution)/shard_map/reshape | solution.py:100
  (25 shorter events, 0.6 us)
Async XLA Ops:
  0.0 18.1 %copy-start = (bf16[2,34,2,12,12]{1,2,4,3,0:T(2,128)(2,1)S(1)}, bf16[2,34,2,12,12]{1,2,4,3,0:T(2,128)(2,1)}, u32[]{:S(2)}) copy-start(bf16[2,34,2,12,12]{1,2,4,3,0:T(2,128)(2,1)} %param.7) | copy-start | bytes 117508
  1.1 21.2 %collective-permute-start = (bf16[12,2,24,128]{3,2,1,0:T(8,128)(2,1)S(1)}, bf16[12,2,24,128]{3,2,1,0:T(8,128)(2,1)S(1)}, u32[]{:S(2)}, u32[]{:S(2)}) collective-permute-start(bf16[12,2,24,128]{3,2,1,0:T(8,128)(2,1)S(1)} %bitcast.65), channel_id=1, source_target_pairs={{8,16},{24,32},{40,48},{56,64},{72,80},{88,96},{104,112},{120,128}... | collective-permute-start | bytes 442376 | tf_op jit(solution)/shard_map/ppermute | solution.py:19
  16.2 6.3 %collective-permute-start.1 = (bf16[12,2,24,128]{3,2,1,0:T(8,128)(2,1)S(1)}, bf16[12,2,24,128]{3,2,1,0:T(8,128)(2,1)S(1)}, u32[]{:S(2)}, u32[]{:S(2)}) collective-permute-start(bf16[12,2,24,128]{3,2,1,0:T(8,128)(2,1)S(1)} %bitcast.66), channel_id=1, source_target_pairs={{0,8},{16,24},{32,40},{48,56},{64,72},{80,88},{96,104},{112,120},{... | collective-permute-start | bytes 442376 | tf_op jit(solution)/shard_map/ppermute | solution.py:18
  18.1 0.7 %copy-start.1 = (s32[2,34]{1,0:T(2,128)S(1)}, s32[2,34]{1,0:T(2,128)}, u32[]{:S(2)}) copy-start(s32[2,34]{1,0:T(2,128)} %param.8) | copy-start | bytes 820
  18.2 0.7 %copy-start.3 = (s32[70]{0:T(128)S(1)}, s32[70]{0:T(128)}, u32[]{:S(2)}) copy-start(s32[70]{0:T(128)} %param.9) | copy-start | bytes 844
  18.4 0.9 %copy-start.2 = (f32[70]{0:T(128)S(1)}, f32[70]{0:T(128)}, u32[]{:S(2)}) copy-start(f32[70]{0:T(128)} %param.11) | copy-start | bytes 844
  18.4 0.9 %copy-start.4 = (f32[70]{0:T(128)S(1)}, f32[70]{0:T(128)}, u32[]{:S(2)}) copy-start(f32[70]{0:T(128)} %param.10) | copy-start | bytes 844
  26.2 7.2 %collective-permute-start.2 = (bf16[216,128]{1,0:T(8,128)(2,1)S(1)}, bf16[216,128]{1,0:T(8,128)(2,1)S(1)}, u32[]{:S(2)}, u32[]{:S(2)}) collective-permute-start(bf16[216,128]{1,0:T(8,128)(2,1)S(1)} %select_n.72), channel_id=1, source_target_pairs={{1,2},{3,4},{5,6},{2,1},{4,3},{6,5},{9,10},{11,12},{13,14},{10,9},... | collective-permute-start | bytes 165896 | tf_op jit(solution)/shard_map/ppermute | solution.py:36
  31.2 3.1 %collective-permute-start.3 = (bf16[216,128]{1,0:T(8,128)(2,1)S(1)}, bf16[216,128]{1,0:T(8,128)(2,1)S(1)}, u32[]{:S(2)}, u32[]{:S(2)}) collective-permute-start(bf16[216,128]{1,0:T(8,128)(2,1)S(1)} %select_n.74), channel_id=1, source_target_pairs={{0,1},{2,3},{4,5},{6,7},{1,0},{3,2},{5,4},{7,6},{8,9},{10,11},{12,... | collective-permute-start | bytes 165896 | tf_op jit(solution)/shard_map/ppermute | solution.py:35

commit v12 on v11

--- a/solution.py
+++ b/solution.py
@@ -59,7 +59,7 @@
     x = jnp.einsum("akqwis,lwse->akqile", left, window, preferred_element_type=f32).astype(bf16)
     x = x.transpose(0, 1, 2, 4, 3, 5)
     right = jnp.stack([jnp.stack([mr, mi], axis=2), jnp.stack([-mi, mr], axis=2)], axis=2)
-    return jnp.einsum("akplie,akqpml->aqime", x, right, preferred_element_type=f32)
+    return jnp.einsum("akplie,akqpml->aimqe", x, right, preferred_element_type=f32)
 
 
 def shards(green, coupling, neighbours, offsets, w_emit, w_absorb):
@@ -97,7 +97,7 @@
     result = result + jnp.dot(
         unpack(upper), kernel[reach + points:], precision=hi, preferred_element_type=jnp.float32
     )
-    return result.reshape(coupled.shape)
+    return result.reshape(coupled.shape).transpose(0, 3, 1, 2, 4)
 
 
 def solution(mesh):

time: 36.3 us -> 36.3 us (level)
  local copies, waits for them, and re-layouts: 3.38 us -> 2.62 us
  matrix products: 3.96 us -> 4.67 us
    reshape x3 -> x0, local copies, waits for them, and re-layouts: 1 us -> none  [the longest x2 0.97 us: shards(): return result.reshape(coupled.shape)]
    dot_general x1, matrix products: 0.23 us -> 0.94 us  [shards(): jnp.dot(unpack(upper), kernel[reach + points:], precision=hi, preferred_e...]
where the time goes in v12:
time: 36.3 us; the launch traced here: 36.1 us
  starting transfers between devices  23.7 us (65%)
  matrix products  4.67 us (13%)
  other arithmetic  3.48 us (10%)
  local copies, waits for them, and re-layouts  2.62 us (7%)
  waiting for transfers between devices  1.21 us (3%)
    ppermute x1, starting transfers between devices, extended(): from_odd = lax.ppermute(jnp.where(even, head, tail), axis, edges[1])  15.1 us
    ppermute x1, starting transfers between devices, swapped(): from_odd = lax.ppermute(jnp.where(even, head, tail), axis, edges[1])  4.82 us
    dot_general x1, matrix products, coupled_blocks(): jnp.einsum('akplie,akqpml->aimqe', x, right, preferred_element_type=f32)  3.25 us
    ppermute x1, starting transfers between devices, extended(): from_even = lax.ppermute(jnp.where(even, tail, head), axis, edges[0])  1.92 us
    ppermute x1, starting transfers between devices, swapped(): from_even = lax.ppermute(jnp.where(even, tail, head), axis, edges[0])  1.92 us
    reduce_sum x1, other arithmetic, make_kernel(): jnp.sum(jnp.where(spread_diff[:, :, None] == -offsets, w_absorb, jnp.floa...  1.81 us
    transpose x1, local copies, waits for them, and re-layouts, shards(): green.transpose(3, 0, 2, 1, 4)  1.05 us
    dot_general x1, matrix products, shards(): jnp.dot(unpack(upper), kernel[reach + points:], precision=hi, preferred_e...  0.94 us
  transfers between devices with their start and end apart: 4, of which 2 were waited for; matrix products, arithmetic and copies ran while one was open for 11% of the time, Pallas kernels for 0%

profile of v12, /device:TPU:57, one launch (start us, length us, event | category | flops | bytes accessed | tf_op | source)
XLA Modules:
  0.0 36.1 jit_solution(8705623959556667134)
XLA Ops:
  0.0 1.0 %copy.35 = bf16[12,2,12,2,128]{4,3,2,1,0:T(2,128)(2,1)S(1)} copy(bf16[12,2,12,2,128]{4,3,0,2,1:T(2,128)(2,1)} %bitcast.70) | data formatting | bytes 294912 | tf_op jit(solution)/shard_map/transpose | solution.py:70
  1.1 15.1 %collective-permute-start = (bf16[12,2,24,128]{3,2,1,0:T(8,128)(2,1)S(1)}, bf16[12,2,24,128]{3,2,1,0:T(8,128)(2,1)S(1)}, u32[]{:S(2)}, u32[]{:S(2)}) collective-permute-start(bf16[12,2,24,128]{3,2,1,0:T(8,128)(2,1)S(1)} %bitcast.71), channel_id=1, source_target_pairs={{8,16},{24,32},{40,48},{56,64},{72,80},{88,96},{104,112},{120,128}... | collective-permute-start | bytes 442376 | tf_op jit(solution)/shard_map/ppermute | solution.py:19
  16.2 1.9 %collective-permute-start.1 = (bf16[12,2,24,128]{3,2,1,0:T(8,128)(2,1)S(1)}, bf16[12,2,24,128]{3,2,1,0:T(8,128)(2,1)S(1)}, u32[]{:S(2)}, u32[]{:S(2)}) collective-permute-start(bf16[12,2,24,128]{3,2,1,0:T(8,128)(2,1)S(1)} %bitcast.72), channel_id=1, source_target_pairs={{0,8},{16,24},{32,40},{48,56},{64,72},{80,88},{96,104},{112,120},{... | collective-permute-start | bytes 442376 | tf_op jit(solution)/shard_map/ppermute | solution.py:18
  18.1 0.1 copy.54
  18.2 0.2 slice_negate_fusion
  18.5 0.2 copy-done.1
  18.9 0.4 %pad_maximum_fusion = (bf16[2,34,12,12,2]{1,0,3,2,4:T(2,128)(2,1)S(1)}, bf16[2,34,12,12,2]{1,0,3,2,4:T(2,128)(2,1)S(1)}) fusion(bf16[2,34,12,12,1]{1,0,3,2,4:T(2,128)(2,1)S(1)} %fusion.34, bf16[2,34,12,12,1]{1,0,3,2,4:T(2,128)(2,1)S(1)} %get-tuple-element.20, bf16[2,34,12,12,1]{1,0,3,2,4:T(2,128)(2,1)S(1)} %get-tuple-element.18), kind=kLoop, calls=%fused_computation.22 | loop fusion | flops 39168 | bytes 137088 | tf_op jit(solution)/shard_map/stack | solution.py:56
  19.3 1.8 %select_reduce_fusion = (f32[224,128]{1,0:T(8,128)S(1)}, f32[224,128]{1,0:T(8,128)S(1)}) fusion(f32[70]{0:T(128)S(1)} %copy-done.2, s32[224,128]{1,0:T(8,128)S(1)} %iota_subtract_fusion, s32[70]{0:T(128)S(1)} %neg.19, f32[70]{0:T(128)S(1)} %copy-done.4, s32[70]{0:T(128)S(1)} %copy-done.3), kind=kLoop, calls=%fused_computation.1 | loop fusion | flops 11984896 | bytes 345184 | tf_op jit(solution)/shard_map/reduce_sum | solution.py:44
  21.1 0.2 maximum_bitcast_fusion.5
  21.5 0.1 copy.33
  21.7 0.5 %maximum_bitcast_fusion.3 = bf16[2,34,2,2,12,12,1]{1,0,5,4,3,2,6:T(2,128)(2,1)S(1)} fusion(bf16[2,34,1,2,12,12]{1,0,5,4,3,2:T(2,128)(2,1)S(1)} %maximum_bitcast_fusion.5, bf16[2,34,1,2,12,12]{1,0,5,4,3,2:T(2,128)(2,1)S(1)} %bitcast.69), kind=kLoop, calls=%fused_computation.19 | loop fusion | flops 39168 | bytes 156672 | tf_op jit(solution)/shard_map/stack | solution.py:61
  22.2 0.3 collective-permute-done.1
  22.5 3.2 %fusion.9 = f32[2,12,12,2,128]{4,2,1,3,0:T(8,128)S(1)} fusion(bf16[2,34,6]{1,2,0:T(8,128)(2,1)S(1)} %fusion.31, bf16[12,2,24,128]{3,2,1,0:T(8,128)(2,1)S(1)} %get-tuple-element.12, bf16[12,2,24,128]{3,2,1,0:T(8,128)(2,1)S(1)} %bitcast.73, bf16[12,2,24,128]{3,2,1,0:T(8,128)(2,1)S(1)} %get-tuple-element.11, ...), kind=kOutput, calls=%fused_computation.8 | convolution fusion | flops 847081728 | bytes 894768 | tf_op jit(solution)/shard_map/akplie,akqpml->aimqe/dot_general | solution.py:62
  25.8 0.2 copy.37
  26.2 0.2 select_n.72
  26.4 4.8 %collective-permute-start.2 = (bf16[216,128]{1,0:T(8,128)(2,1)S(1)}, bf16[216,128]{1,0:T(8,128)(2,1)S(1)}, u32[]{:S(2)}, u32[]{:S(2)}) collective-permute-start(bf16[216,128]{1,0:T(8,128)(2,1)S(1)} %select_n.72), channel_id=1, source_target_pairs={{1,2},{3,4},{5,6},{2,1},{4,3},{6,5},{9,10},{11,12},{13,14},{10,9},... | collective-permute-start | bytes 165896 | tf_op jit(solution)/shard_map/ppermute | solution.py:36
  31.2 0.2 select_n.74
  31.4 1.9 %collective-permute-start.3 = (bf16[216,128]{1,0:T(8,128)(2,1)S(1)}, bf16[216,128]{1,0:T(8,128)(2,1)S(1)}, u32[]{:S(2)}, u32[]{:S(2)}) collective-permute-start(bf16[216,128]{1,0:T(8,128)(2,1)S(1)} %select_n.74), channel_id=1, source_target_pairs={{0,1},{2,3},{4,5},{6,7},{1,0},{3,2},{5,4},{7,6},{8,9},{10,11},{12,... | collective-permute-start | bytes 165896 | tf_op jit(solution)/shard_map/ppermute | solution.py:35
  33.3 0.3 fusion.27
  33.6 0.9 %collective-permute-done.3 = bf16[216,128]{1,0:T(8,128)(2,1)S(1)} collective-permute-done((bf16[216,128]{1,0:T(8,128)(2,1)S(1)}, bf16[216,128]{1,0:T(8,128)(2,1)S(1)}, u32[]{:S(2)}, u32[]{:S(2)}) %collective-permute-start.3) | collective-permute-done | bytes 55328 | tf_op jit(solution)/shard_map/ppermute | solution.py:35
  34.5 0.2 reshape.69
  34.7 0.2 reshape.70
  34.9 0.2 convolution_add_fusion.1
  35.1 0.9 %convolution_add_fusion = f32[576,128]{1,0:T(8,128)} fusion(f32[576,128]{1,0:T(8,128)S(1)} %convolution_add_fusion.1, bf16[576,48]{1,0:T(8,128)(2,1)S(1)} %reshape.70, f32[224,128]{1,0:T(8,128)S(1)} %add.24), kind=kOutput, calls=%fused_computation.9 | convolution fusion | flops 21307392 | bytes 761856 | tf_op jit(solution)/shard_map/dot_general | solution.py:97
  (23 shorter events, 0.5 us)
Async XLA Ops:
  0.0 18.1 %copy-start = (bf16[2,34,2,12,12]{1,2,4,3,0:T(2,128)(2,1)S(1)}, bf16[2,34,2,12,12]{1,2,4,3,0:T(2,128)(2,1)}, u32[]{:S(2)}) copy-start(bf16[2,34,2,12,12]{1,2,4,3,0:T(2,128)(2,1)} %param.7) | copy-start | bytes 117508
  1.1 21.2 %collective-permute-start = (bf16[12,2,24,128]{3,2,1,0:T(8,128)(2,1)S(1)}, bf16[12,2,24,128]{3,2,1,0:T(8,128)(2,1)S(1)}, u32[]{:S(2)}, u32[]{:S(2)}) collective-permute-start(bf16[12,2,24,128]{3,2,1,0:T(8,128)(2,1)S(1)} %bitcast.71), channel_id=1, source_target_pairs={{8,16},{24,32},{40,48},{56,64},{72,80},{88,96},{104,112},{120,128}... | collective-permute-start | bytes 442376 | tf_op jit(solution)/shard_map/ppermute | solution.py:19
  16.2 6.3 %collective-permute-start.1 = (bf16[12,2,24,128]{3,2,1,0:T(8,128)(2,1)S(1)}, bf16[12,2,24,128]{3,2,1,0:T(8,128)(2,1)S(1)}, u32[]{:S(2)}, u32[]{:S(2)}) collective-permute-start(bf16[12,2,24,128]{3,2,1,0:T(8,128)(2,1)S(1)} %bitcast.72), channel_id=1, source_target_pairs={{0,8},{16,24},{32,40},{48,56},{64,72},{80,88},{96,104},{112,120},{... | collective-permute-start | bytes 442376 | tf_op jit(solution)/shard_map/ppermute | solution.py:18
  18.1 0.7 %copy-start.1 = (s32[2,34]{1,0:T(2,128)S(1)}, s32[2,34]{1,0:T(2,128)}, u32[]{:S(2)}) copy-start(s32[2,34]{1,0:T(2,128)} %param.8) | copy-start | bytes 820
  18.2 0.7 %copy-start.3 = (s32[70]{0:T(128)S(1)}, s32[70]{0:T(128)}, u32[]{:S(2)}) copy-start(s32[70]{0:T(128)} %param.9) | copy-start | bytes 844
  18.4 0.9 %copy-start.2 = (f32[70]{0:T(128)S(1)}, f32[70]{0:T(128)}, u32[]{:S(2)}) copy-start(f32[70]{0:T(128)} %param.11) | copy-start | bytes 844
  18.4 0.9 %copy-start.4 = (f32[70]{0:T(128)S(1)}, f32[70]{0:T(128)}, u32[]{:S(2)}) copy-start(f32[70]{0:T(128)} %param.10) | copy-start | bytes 844
  26.4 7.2 %collective-permute-start.2 = (bf16[216,128]{1,0:T(8,128)(2,1)S(1)}, bf16[216,128]{1,0:T(8,128)(2,1)S(1)}, u32[]{:S(2)}, u32[]{:S(2)}) collective-permute-start(bf16[216,128]{1,0:T(8,128)(2,1)S(1)} %select_n.72), channel_id=1, source_target_pairs={{1,2},{3,4},{5,6},{2,1},{4,3},{6,5},{9,10},{11,12},{13,14},{10,9},... | collective-permute-start | bytes 165896 | tf_op jit(solution)/shard_map/ppermute | solution.py:36
  31.4 3.1 %collective-permute-start.3 = (bf16[216,128]{1,0:T(8,128)(2,1)S(1)}, bf16[216,128]{1,0:T(8,128)(2,1)S(1)}, u32[]{:S(2)}, u32[]{:S(2)}) collective-permute-start(bf16[216,128]{1,0:T(8,128)(2,1)S(1)} %select_n.74), channel_id=1, source_target_pairs={{0,1},{2,3},{4,5},{6,7},{1,0},{3,2},{5,4},{7,6},{8,9},{10,11},{12,... | collective-permute-start | bytes 165896 | tf_op jit(solution)/shard_map/ppermute | solution.py:35

commit v13 on v12

--- a/solution.py
+++ b/solution.py
@@ -91,12 +91,12 @@
 
     lower, upper = swapped(pack(flat[:, :reach]), pack(flat[:, points - reach:]), "energy")
     result = jnp.dot(flat, kernel[reach:reach + points], precision=hi, preferred_element_type=jnp.float32)
-    result = result + jnp.dot(
-        unpack(lower), kernel[:reach], precision=hi, preferred_element_type=jnp.float32
-    )
-    result = result + jnp.dot(
-        unpack(upper), kernel[reach + points:], precision=hi, preferred_element_type=jnp.float32
-    )
+    for halo, block in ((lower, kernel[:reach]), (upper, kernel[reach + points:])):
+        block_hi = block.astype(jnp.bfloat16)
+        block_lo = (block - block_hi.astype(jnp.float32)).astype(jnp.bfloat16)
+        values = halo.reshape(rows, reach)
+        result = result + jnp.dot(values, block_hi, preferred_element_type=jnp.float32)
+        result = result + jnp.dot(values, block_lo, preferred_element_type=jnp.float32)
     return result.reshape(coupled.shape).transpose(0, 3, 1, 2, 4)
 
 

time: 36.3 us -> 36.5 us (level)
    dot_general x2 -> x4, matrix products: 1.16 us -> 1.38 us  [the longest x2 1.06 us: shards(): jnp.dot(values, block_lo, preferred_element_type=jnp.float32)]
where the time goes in v13:
time: 36.5 us; the launch traced here: 36.3 us
  starting transfers between devices  23.7 us (65%)
  matrix products  4.9 us (13%)
  other arithmetic  3.48 us (10%)
  local copies, waits for them, and re-layouts  2.62 us (7%)
  waiting for transfers between devices  1.21 us (3%)
    ppermute x1, starting transfers between devices, extended(): from_odd = lax.ppermute(jnp.where(even, head, tail), axis, edges[1])  15.1 us
    ppermute x1, starting transfers between devices, swapped(): from_odd = lax.ppermute(jnp.where(even, head, tail), axis, edges[1])  4.82 us
    dot_general x1, matrix products, coupled_blocks(): jnp.einsum('akplie,akqpml->aimqe', x, right, preferred_element_type=f32)  3.25 us
    ppermute x1, starting transfers between devices, extended(): from_even = lax.ppermute(jnp.where(even, tail, head), axis, edges[0])  1.92 us
    ppermute x1, starting transfers between devices, swapped(): from_even = lax.ppermute(jnp.where(even, tail, head), axis, edges[0])  1.92 us
    reduce_sum x1, other arithmetic, make_kernel(): jnp.sum(jnp.where(spread_diff[:, :, None] == -offsets, w_absorb, jnp.floa...  1.81 us
    dot_general x2, matrix products, shards(): jnp.dot(values, block_lo, preferred_element_type=jnp.float32)  1.06 us
    transpose x1, local copies, waits for them, and re-layouts, shards(): green.transpose(3, 0, 2, 1, 4)  1.05 us
  transfers between devices with their start and end apart: 4, of which 2 were waited for; matrix products, arithmetic and copies ran while one was open for 11% of the time, Pallas kernels for 0%

profile of v13, /device:TPU:57, one launch (start us, length us, event | category | flops | bytes accessed | tf_op | source)
XLA Modules:
  0.0 36.3 jit_solution(1762464278294607387)
XLA Ops:
  0.0 1.0 %copy.35 = bf16[12,2,12,2,128]{4,3,2,1,0:T(2,128)(2,1)S(1)} copy(bf16[12,2,12,2,128]{4,3,0,2,1:T(2,128)(2,1)} %bitcast.72) | data formatting | bytes 294912 | tf_op jit(solution)/shard_map/transpose | solution.py:70
  1.1 15.1 %collective-permute-start = (bf16[12,2,24,128]{3,2,1,0:T(8,128)(2,1)S(1)}, bf16[12,2,24,128]{3,2,1,0:T(8,128)(2,1)S(1)}, u32[]{:S(2)}, u32[]{:S(2)}) collective-permute-start(bf16[12,2,24,128]{3,2,1,0:T(8,128)(2,1)S(1)} %bitcast.73), channel_id=1, source_target_pairs={{8,16},{24,32},{40,48},{56,64},{72,80},{88,96},{104,112},{120,128}... | collective-permute-start | bytes 442376 | tf_op jit(solution)/shard_map/ppermute | solution.py:19
  16.2 1.9 %collective-permute-start.1 = (bf16[12,2,24,128]{3,2,1,0:T(8,128)(2,1)S(1)}, bf16[12,2,24,128]{3,2,1,0:T(8,128)(2,1)S(1)}, u32[]{:S(2)}, u32[]{:S(2)}) collective-permute-start(bf16[12,2,24,128]{3,2,1,0:T(8,128)(2,1)S(1)} %bitcast.74), channel_id=1, source_target_pairs={{0,8},{16,24},{32,40},{48,56},{64,72},{80,88},{96,104},{112,120},{... | collective-permute-start | bytes 442376 | tf_op jit(solution)/shard_map/ppermute | solution.py:18
  18.2 0.2 slice_negate_fusion
  18.5 0.2 copy-done.1
  18.9 0.4 %pad_maximum_fusion = (bf16[2,34,12,12,2]{1,0,3,2,4:T(2,128)(2,1)S(1)}, bf16[2,34,12,12,2]{1,0,3,2,4:T(2,128)(2,1)S(1)}) fusion(bf16[2,34,12,12,1]{1,0,3,2,4:T(2,128)(2,1)S(1)} %fusion.36, bf16[2,34,12,12,1]{1,0,3,2,4:T(2,128)(2,1)S(1)} %get-tuple-element.20, bf16[2,34,12,12,1]{1,0,3,2,4:T(2,128)(2,1)S(1)} %get-tuple-element.18), kind=kLoop, calls=%fused_computation.24 | loop fusion | flops 39168 | bytes 137088 | tf_op jit(solution)/shard_map/stack | solution.py:56
  19.3 1.8 %select_reduce_fusion = (f32[224,128]{1,0:T(8,128)S(1)}, f32[224,128]{1,0:T(8,128)S(1)}) fusion(f32[70]{0:T(128)S(1)} %copy-done.2, s32[224,128]{1,0:T(8,128)S(1)} %iota_subtract_fusion, s32[70]{0:T(128)S(1)} %neg.19, f32[70]{0:T(128)S(1)} %copy-done.4, s32[70]{0:T(128)S(1)} %copy-done.3), kind=kLoop, calls=%fused_computation.1 | loop fusion | flops 11984896 | bytes 345184 | tf_op jit(solution)/shard_map/reduce_sum | solution.py:44
  21.1 0.2 maximum_bitcast_fusion.5
  21.7 0.5 %maximum_bitcast_fusion.3 = bf16[2,34,2,2,12,12,1]{1,0,5,4,3,2,6:T(2,128)(2,1)S(1)} fusion(bf16[2,34,1,2,12,12]{1,0,5,4,3,2:T(2,128)(2,1)S(1)} %maximum_bitcast_fusion.5, bf16[2,34,1,2,12,12]{1,0,5,4,3,2:T(2,128)(2,1)S(1)} %bitcast.71), kind=kLoop, calls=%fused_computation.21 | loop fusion | flops 39168 | bytes 156672 | tf_op jit(solution)/shard_map/stack | solution.py:61
  22.2 0.3 collective-permute-done.1
  22.5 3.2 %fusion.9 = f32[2,12,12,2,128]{4,2,1,3,0:T(8,128)S(1)} fusion(bf16[2,34,6]{1,2,0:T(8,128)(2,1)S(1)} %fusion.32, bf16[12,2,24,128]{3,2,1,0:T(8,128)(2,1)S(1)} %get-tuple-element.12, bf16[12,2,24,128]{3,2,1,0:T(8,128)(2,1)S(1)} %bitcast.75, bf16[12,2,24,128]{3,2,1,0:T(8,128)(2,1)S(1)} %get-tuple-element.11, ...), kind=kOutput, calls=%fused_computation.8 | convolution fusion | flops 847081728 | bytes 894768 | tf_op jit(solution)/shard_map/akplie,akqpml->aimqe/dot_general | solution.py:62
  25.8 0.2 copy.37
  26.2 0.2 select_n.72
  26.4 4.8 %collective-permute-start.2 = (bf16[216,128]{1,0:T(8,128)(2,1)S(1)}, bf16[216,128]{1,0:T(8,128)(2,1)S(1)}, u32[]{:S(2)}, u32[]{:S(2)}) collective-permute-start(bf16[216,128]{1,0:T(8,128)(2,1)S(1)} %select_n.72), channel_id=1, source_target_pairs={{1,2},{3,4},{5,6},{2,1},{4,3},{6,5},{9,10},{11,12},{13,14},{10,9},... | collective-permute-start | bytes 165896 | tf_op jit(solution)/shard_map/ppermute | solution.py:36
  31.2 0.2 select_n.74
  31.4 1.9 %collective-permute-start.3 = (bf16[216,128]{1,0:T(8,128)(2,1)S(1)}, bf16[216,128]{1,0:T(8,128)(2,1)S(1)}, u32[]{:S(2)}, u32[]{:S(2)}) collective-permute-start(bf16[216,128]{1,0:T(8,128)(2,1)S(1)} %select_n.74), channel_id=1, source_target_pairs={{0,1},{2,3},{4,5},{6,7},{1,0},{3,2},{5,4},{7,6},{8,9},{10,11},{12,... | collective-permute-start | bytes 165896 | tf_op jit(solution)/shard_map/ppermute | solution.py:35
  33.3 0.3 fusion.29
  33.6 0.9 %collective-permute-done.3 = bf16[216,128]{1,0:T(8,128)(2,1)S(1)} collective-permute-done((bf16[216,128]{1,0:T(8,128)(2,1)S(1)}, bf16[216,128]{1,0:T(8,128)(2,1)S(1)}, u32[]{:S(2)}, u32[]{:S(2)}) %collective-permute-start.3) | collective-permute-done | bytes 55328 | tf_op jit(solution)/shard_map/ppermute | solution.py:35
  34.5 0.2 reshape.70
  34.7 0.2 fusion.33
  34.9 0.2 fusion.31
  35.0 0.2 reshape.69
  35.2 0.2 convolution_add_fusion.1
  35.4 0.9 %fusion.15 = f32[576,128]{1,0:T(8,128)} fusion(f32[576,128]{1,0:T(8,128)S(1)} %fusion.31, f32[576,128]{1,0:T(8,128)S(1)} %fusion.33, f32[576,128]{1,0:T(8,128)S(1)} %convolution_add_fusion.1, bf16[576,48]{1,0:T(8,128)(2,1)S(1)} %reshape.69, f32[224,128]{1,0:T(8,128)S(1)} %add.30), kind=kOutput, calls=%fused_computation.11 | convolution fusion | flops 7323648 | bytes 1351680 | tf_op jit(solution)/shard_map/dot_general | solution.py:99
  (25 shorter events, 0.7 us)
Async XLA Ops:
  0.0 18.1 %copy-start = (bf16[2,34,2,12,12]{1,2,4,3,0:T(2,128)(2,1)S(1)}, bf16[2,34,2,12,12]{1,2,4,3,0:T(2,128)(2,1)}, u32[]{:S(2)}) copy-start(bf16[2,34,2,12,12]{1,2,4,3,0:T(2,128)(2,1)} %param.7) | copy-start | bytes 117508
  1.1 21.2 %collective-permute-start = (bf16[12,2,24,128]{3,2,1,0:T(8,128)(2,1)S(1)}, bf16[12,2,24,128]{3,2,1,0:T(8,128)(2,1)S(1)}, u32[]{:S(2)}, u32[]{:S(2)}) collective-permute-start(bf16[12,2,24,128]{3,2,1,0:T(8,128)(2,1)S(1)} %bitcast.73), channel_id=1, source_target_pairs={{8,16},{24,32},{40,48},{56,64},{72,80},{88,96},{104,112},{120,128}... | collective-permute-start | bytes 442376 | tf_op jit(solution)/shard_map/ppermute | solution.py:19
  16.2 6.3 %collective-permute-start.1 = (bf16[12,2,24,128]{3,2,1,0:T(8,128)(2,1)S(1)}, bf16[12,2,24,128]{3,2,1,0:T(8,128)(2,1)S(1)}, u32[]{:S(2)}, u32[]{:S(2)}) collective-permute-start(bf16[12,2,24,128]{3,2,1,0:T(8,128)(2,1)S(1)} %bitcast.74), channel_id=1, source_target_pairs={{0,8},{16,24},{32,40},{48,56},{64,72},{80,88},{96,104},{112,120},{... | collective-permute-start | bytes 442376 | tf_op jit(solution)/shard_map/ppermute | solution.py:18
  18.1 0.7 %copy-start.1 = (s32[2,34]{1,0:T(2,128)S(1)}, s32[2,34]{1,0:T(2,128)}, u32[]{:S(2)}) copy-start(s32[2,34]{1,0:T(2,128)} %param.8) | copy-start | bytes 820
  18.2 0.7 %copy-start.3 = (s32[70]{0:T(128)S(1)}, s32[70]{0:T(128)}, u32[]{:S(2)}) copy-start(s32[70]{0:T(128)} %param.9) | copy-start | bytes 844
  18.4 0.9 %copy-start.2 = (f32[70]{0:T(128)S(1)}, f32[70]{0:T(128)}, u32[]{:S(2)}) copy-start(f32[70]{0:T(128)} %param.11) | copy-start | bytes 844
  18.4 0.9 %copy-start.4 = (f32[70]{0:T(128)S(1)}, f32[70]{0:T(128)}, u32[]{:S(2)}) copy-start(f32[70]{0:T(128)} %param.10) | copy-start | bytes 844
  26.4 7.2 %collective-permute-start.2 = (bf16[216,128]{1,0:T(8,128)(2,1)S(1)}, bf16[216,128]{1,0:T(8,128)(2,1)S(1)}, u32[]{:S(2)}, u32[]{:S(2)}) collective-permute-start(bf16[216,128]{1,0:T(8,128)(2,1)S(1)} %select_n.72), channel_id=1, source_target_pairs={{1,2},{3,4},{5,6},{2,1},{4,3},{6,5},{9,10},{11,12},{13,14},{10,9},... | collective-permute-start | bytes 165896 | tf_op jit(solution)/shard_map/ppermute | solution.py:36
  31.4 3.1 %collective-permute-start.3 = (bf16[216,128]{1,0:T(8,128)(2,1)S(1)}, bf16[216,128]{1,0:T(8,128)(2,1)S(1)}, u32[]{:S(2)}, u32[]{:S(2)}) collective-permute-start(bf16[216,128]{1,0:T(8,128)(2,1)S(1)} %select_n.74), channel_id=1, source_target_pairs={{0,1},{2,3},{4,5},{6,7},{1,0},{3,2},{5,4},{7,6},{8,9},{10,11},{12,... | collective-permute-start | bytes 165896 | tf_op jit(solution)/shard_map/ppermute | solution.py:35
